TPU v7x, 256 devices: a whole 4x4x8 slice. The times are simulated.
256 devices in a mesh: seq: 64 (over y, x_lo, z), dp: 4 (over x_hi, core).
Axes of the slice: x: 4 (x_hi: 2, x_lo: 2; x = x_hi * 2 + x_lo), y: 4, z: 8, core: 2. Of those that a mesh axis runs over, the one named last changes fastest.
Arguments:
- inputs: float32 [4, 32768, 256], P('dp', 'seq'), may hold values from -6 to 6
- out_cotangent: float32 [4, 32768, 256], P('dp', 'seq'), may hold values from -6 to 6
- skip_cotangent: float32 [4, 32768, 256], P('dp', 'seq'), may hold values from -6 to 6
- convolution_weight: float32 [2, 512, 1024], replicated, may hold values from -0.25 to 0.25
- convolution_bias: float32 [2, 1024], replicated, may hold values from -3 to 3
- output_weight: float32 [2, 512, 512], replicated, may hold values from -0.25 to 0.25
Outputs:
- input_grad: float32 [4, 32768, 256], P('dp', 'seq')
- conv_grad: float32 [1024, 1024], P(('seq', 'dp'))
- out_grad: float32 [1024, 512], P(('seq', 'dp'))
- bias_grad: float32 [2048], P(('seq', 'dp'))
All inputs are finite; a program needn't handle non-finite values.
Results may differ from a plain program's by a relative error of at most 0.00025.
Values sent between devices are 32-bit elements; how exact they have to be, the bound alone decides.
No kernel may reach another device: no remote copies, remote signals or barrier semaphores. Data moves between devices by JAX's collectives and lax.ppermute only.
A program may use at most 128 MiB of HBM per device.

v0:
```python
import math

import jax
import jax.numpy as jnp
from jax import lax
from jax.sharding import PartitionSpec as P


SEQ_AXES = ("y", "xl", "z")
DP_AXES = ("xh", "c")


def reduce_rows(block, axis):
    parts = lax.axis_size(axis)
    block = block.reshape(parts, block.shape[0] // parts, block.shape[1])
    return lax.all_to_all(block, axis, 0, 0, tiled=True).sum(axis=0)


def reduce_to_owner(packed):
    rows, width = packed.shape
    halves = lax.all_to_all(packed.reshape(rows, 2, width // 2), "c", 1, 1, tiled=True)
    block = halves.sum(axis=1)
    for axis in ("y", "xl", "z", "xh"):
        block = reduce_rows(block, axis)
    return lax.all_to_all(block, "c", 0, 1, tiled=True)


def from_behind(block, axis, distance):
    devices = range(lax.axis_size(axis))
    route = [(i - distance, i) for i in devices if i - distance in devices]
    return lax.ppermute(block, axis, route)


def matmul(left, right):
    return jnp.dot(left, right, precision=lax.Precision.HIGH, preferred_element_type=jnp.float32)


def contract(left, right, left_dim, right_dim):
    return lax.dot_general(
        left,
        right,
        (((left_dim,), (right_dim,)), ((), ())),
        precision=lax.Precision.HIGH,
        preferred_element_type=jnp.float32,
    )


def layer_forward_step(earlier, values, weight, bias):
    joined = jnp.concatenate([earlier, values], axis=1)
    mixed = matmul(joined, weight) + bias
    width = weight.shape[1] // 2
    tanh_part = jnp.tanh(mixed[:, :width])
    sigm_part = jax.nn.sigmoid(mixed[:, width:])
    return (joined, tanh_part, sigm_part, tanh_part * sigm_part)


def layer_backward_step(
    joined, tanh_part, sigm_part, hidden, weight, out_w, carried_state, skip_cotangent_rows
):
    channels = carried_state.shape[1]
    outer = jnp.concatenate([carried_state, skip_cotangent_rows], axis=1)
    dhidden = contract(outer, out_w, 1, 1)
    dfilter = dhidden * sigm_part * (1.0 - tanh_part * tanh_part)
    dgate = dhidden * tanh_part * sigm_part * (1.0 - sigm_part)
    dmixed = jnp.concatenate([dfilter, dgate], axis=1)
    out_t = contract(outer, hidden, 0, 0)
    conv_g = contract(joined, dmixed, 0, 0)
    bias_g = jnp.sum(dmixed, axis=0)
    back = contract(dmixed, weight, 1, 1)
    return (back[:, :channels], back[:, channels:], conv_g, out_t, bias_g)


def local(
    inputs, out_cotangent, skip_cotangent, convolution_weight, convolution_bias, output_weight
):
    start_row = inputs[0]
    output_cotangent_rows = out_cotangent[0]
    skip_cotangent_rows = skip_cotangent[0]
    rows, channels = start_row.shape
    half = rows // 2
    tail = from_behind(start_row[rows - half :], SEQ_AXES, 1)
    earlier1 = jnp.concatenate([tail, start_row[: rows - half]], axis=0)
    first_joined, first_tanh, first_sigmoid, first_hidden = layer_forward_step(
        earlier1, start_row, convolution_weight[0], convolution_bias[0]
    )
    second_layer = start_row + matmul(first_hidden, output_weight[0][:, :channels])
    earlier2 = from_behind(second_layer, SEQ_AXES, 1)
    second_joined, second_tanh, second_sigmoid, second_hidden = layer_forward_step(
        earlier2, second_layer, convolution_weight[1], convolution_bias[1]
    )
    past2, local2, second_conv_output, second_output, second_bias = layer_backward_step(
        second_joined,
        second_tanh,
        second_sigmoid,
        second_hidden,
        convolution_weight[1],
        output_weight[1],
        output_cotangent_rows,
        skip_cotangent_rows,
    )
    carried_state = output_cotangent_rows + local2 + from_behind(past2, SEQ_AXES, -1)
    past1, local1, first_conv_output, first_output, first_bias = layer_backward_step(
        first_joined,
        first_tanh,
        first_sigmoid,
        first_hidden,
        convolution_weight[0],
        output_weight[0],
        carried_state,
        skip_cotangent_rows,
    )
    rim_rows = from_behind(past1[:half], SEQ_AXES, -1)
    input_grad = carried_state + local1 + jnp.concatenate([past1[half:], rim_rows], axis=0)
    devices = lax.axis_size(SEQ_AXES + DP_AXES)
    factor = 1.0 / math.sqrt(rows * devices)
    conv_terms = jnp.concatenate([first_conv_output, second_conv_output], axis=0)
    out_terms = jnp.concatenate([first_output, second_output], axis=0)
    bias_terms = jnp.concatenate([first_bias, second_bias], axis=0)
    bias_cols = bias_terms.reshape(conv_terms.shape[0], -1)
    bias_cols = jnp.pad(bias_cols, ((0, 0), (0, 128 - bias_cols.shape[1])))
    packed = jnp.concatenate([conv_terms, out_terms, bias_cols], axis=1)
    summed = reduce_to_owner(packed) * factor
    conv_width, out_width = conv_terms.shape[1], out_terms.shape[1]
    conv_grad = summed[:, :conv_width]
    out_grad = summed[:, conv_width : conv_width + out_width]
    bias_grad = summed[:, conv_width + out_width : conv_width + out_width + bias_terms.shape[0] // conv_terms.shape[0]]
    bias_grad = bias_grad.reshape(-1)
    return (input_grad[None], conv_grad, out_grad, bias_grad)


def solution(mesh):
    fine = jax.sharding.Mesh(mesh.devices.reshape(4, 2, 8, 2, 2), ("y", "xl", "z", "xh", "c"))
    rows_spec = P(("xh", "c"), ("y", "xl", "z"), None)
    owner = ("y", "xl", "z", "xh", "c")
    return jax.shard_map(
        local,
        mesh=fine,
        in_specs=(rows_spec, rows_spec, rows_spec, P(), P(), P()),
        out_specs=(rows_spec, P(owner, None), P(owner, None), P(owner)),
        check_vma=False,
    )
```

profile of v0, /device:TPU:1, one launch (start us, length us, event | category | flops | bytes accessed | tf_op | source)
XLA Modules:
  0.0 206.4 jit_solution(10918489497842623245)
XLA Ops:
  0.6 0.0 copy-start.20
  0.7 1.4 copy.133
  2.1 4.4 %collective-permute-start = (f32[256,256]{0,1:T(8,128)S(1)}, f32[256,256]{0,1:T(8,128)S(1)}, u32[]{:S(2)}, u32[]{:S(2)}) collective-permute-start(f32[256,256]{0,1:T(8,128)S(1)} %get-tuple-element.46), channel_id=1, source_target_pairs={{0,4},{4,8},{8,12},{12,16},{16,20},{20,24},{24,28},{28,32},{32,36}... | collective-permute-start | bytes 786440 | tf_op jit(solution)/shard_map/ppermute | solution.py:31
  6.5 0.0 copy-done.20
  6.5 0.1 slice_bitcast_fusion
  6.6 4.8 %collective-permute-done = f32[256,256]{0,1:T(8,128)S(1)} collective-permute-done((f32[256,256]{0,1:T(8,128)S(1)}, f32[256,256]{0,1:T(8,128)S(1)}, u32[]{:S(2)}, u32[]{:S(2)}) %collective-permute-start) | collective-permute-done | bytes 262176 | tf_op jit(solution)/shard_map/ppermute | solution.py:31
  11.4 3.7 %fusion.12 = f32[512,1024]{0,1:T(8,128)S(1)} fusion(f32[2,512,1024]{2,1,0:T(8,128)} %param.9, f32[1024]{0:T(1024)S(1)} %bitcast.63, f32[512,256]{0,1:T(8,128)S(1)} %bitcast.54, f32[256,256]{0,1:T(8,128)S(1)} %get-tuple-element.47, f32[256,256]{0,1:T(8,128)S(1)} %collective-permute-done), kind=kOutput, calls=%fused_computation.16 | convolution fusion | flops 1611661312 | bytes 5246976 | tf_op jit(solution)/shard_map/dot_general | solution.py:35
  15.1 0.0 copy-start.23
  15.1 0.0 copy-start.24
  15.2 0.9 convolution_add_fusion
  16.1 0.4 copy-done.9
  16.5 4.1 %collective-permute-start.1 = (f32[512,256]{0,1:T(8,128)S(1)}, f32[512,256]{0,1:T(8,128)S(1)}, u32[]{:S(2)}, u32[]{:S(2)}) collective-permute-start(f32[512,256]{0,1:T(8,128)S(1)} %convolution_add_fusion), channel_id=1, source_target_pairs={{0,4},{4,8},{8,12},{12,16},{16,20},{20,24},{24,28},{28,32},{32,36}... | collective-permute-start | bytes 1572872 | tf_op jit(solution)/shard_map/ppermute | solution.py:31
  20.6 0.0 copy-done.23
  20.6 1.0 copy.132
  21.6 1.0 copy.131
  22.6 7.6 %collective-permute-done.1 = f32[512,256]{0,1:T(8,128)S(1)} collective-permute-done((f32[512,256]{0,1:T(8,128)S(1)}, f32[512,256]{0,1:T(8,128)S(1)}, u32[]{:S(2)}, u32[]{:S(2)}) %collective-permute-start.1) | collective-permute-done | bytes 524320 | tf_op jit(solution)/shard_map/ppermute | solution.py:31
  30.2 3.8 %fusion.15 = f32[512,1024]{0,1:T(8,128)S(1)} fusion(f32[2,512,1024]{2,1,0:T(8,128)} %param.9, f32[1024]{0:T(1024)S(1)} %bitcast.62, f32[512,256]{0,1:T(8,128)S(1)} %convolution_add_fusion, f32[512,256]{0,1:T(8,128)S(1)} %collective-permute-done.1), kind=kOutput, calls=%fused_computation.17 | convolution fusion | flops 1611399168 | bytes 5246976 | tf_op jit(solution)/shard_map/dot_general | solution.py:35
  34.1 0.0 copy-start
  34.1 1.4 subtract_multiply_fusion.3
  35.5 1.5 copy-done
  37.0 1.9 fusion
  38.9 1.0 copy-done.6
  39.9 0.9 slice.106
  40.8 1.5 collective-permute-start.2
  42.2 0.2 fusion.20
  42.5 0.9 concatenate.52
  43.4 4.4 %fusion.21 = f32[512,1024]{1,0:T(8,128)} fusion(f32[512,512]{0,1:T(8,128)S(1)} %get-tuple-element.43, f32[512,512]{0,1:T(8,128)S(1)} %get-tuple-element.42, f32[512,256]{0,1:T(8,128)S(1)} %convolution_add_fusion, f32[512,256]{0,1:T(8,128)} %copy-done.8), kind=kOutput, calls=%fused_computation.21 | convolution fusion | flops 1611399168 | bytes 5242880 | tf_op jit(solution)/shard_map/dot_general | solution.py:39
  47.8 0.0 copy-start.22
  47.8 2.2 %fusion.30 = f32[512,512]{1,0:T(8,128)} fusion(f32[512,256]{0,1:T(8,128)S(1)} %bitcast.59, f32[512,256]{0,1:T(8,128)S(1)} %bitcast.57, f32[512,1024]{0,1:T(8,128)S(1)} %copy-done.12), kind=kOutput, calls=%fused_computation.39 | convolution fusion | flops 806617088 | bytes 4194304 | tf_op jit(solution)/shard_map/dot_general | solution.py:39
  50.0 4.9 %collective-permute-done.2 = f32[512,256]{0,1:T(8,128)} collective-permute-done((f32[512,256]{0,1:T(8,128)}, f32[512,256]{0,1:T(8,128)}, u32[]{:S(2)}, u32[]{:S(2)}) %collective-permute-start.2) | collective-permute-done | bytes 524320 | tf_op jit(solution)/shard_map/ppermute | solution.py:31
  54.9 1.2 fusion.38
  56.2 0.0 copy-start.15
  56.2 1.4 subtract_multiply_fusion.1
  57.6 2.2 %fusion.33 = f32[512,512]{1,0:T(8,128)} fusion(f32[512,256]{0,1:T(8,128)S(1)} %bitcast.61, f32[512,256]{0,1:T(8,128)S(1)} %fusion.38, f32[512,1024]{0,1:T(8,128)S(1)} %copy-done.10), kind=kOutput, calls=%fused_computation.47 | convolution fusion | flops 806617088 | bytes 4194304 | tf_op jit(solution)/shard_map/dot_general | solution.py:39
  59.9 0.2 fusion.18
  60.1 0.9 concatenate.51
  61.0 1.0 select_maximum_fusion
  62.1 1.9 fusion.19
  64.0 5.4 %pad_maximum_fusion = f32[1024,1664]{1,0:T(8,128)} fusion(f32[1024,128]{1,0:T(8,128)S(1)} %select_maximum_fusion, f32[512,512]{1,0:T(8,128)S(1)} %copy-done.19, f32[512,512]{1,0:T(8,128)} %fusion.33, f32[512,1024]{1,0:T(8,128)S(1)} %copy-done.5, f32[512,1024]{1,0:T(8,128)S(1)} %fusion.19), kind=kLoop, calls=%fused_computation | loop fusion | flops 6815744 | bytes 13631488 | tf_op jit(solution)/shard_map/concatenate | solution.py:121
  69.3 7.7 %copy.141 = f32[1024,1664]{0,1:T(8,128)} copy(f32[1024,1664]{1,0:T(8,128)} %pad_maximum_fusion) | data formatting | bytes 13631488 | tf_op jit(solution)/shard_map/concatenate | solution.py:121
  77.0 18.8 %all_to_all.38 = f32[1024,2,832]{0,2,1:T(8,128)} all-to-all(f32[1024,2,832]{0,2,1:T(8,128)} %bitcast.51), channel_id=1, replica_groups=mesh['y'=4,'xl'=2,'z'=8,'xh'=2,'c'=2] {'c'}, dimensions={1} | all-to-all | bytes 13631488 | tf_op jit(solution)/shard_map/all_to_all | solution.py:21
  95.8 4.0 %reduce_sum.65 = f32[1024,832]{0,1:T(8,128)S(1)} reduce(f32[1024,2,832]{0,2,1:T(8,128)} %all_to_all.38, f32[]{:T(128)} %constant.1.clone.1), dimensions={1}, to_apply=%region_2.3 | reduce | flops 851968 | bytes 10223620 | tf_op jit(solution)/shard_map/reduce_sum | solution.py:22
  99.8 0.3 copy.154
  100.1 52.4 %all_to_all.39 = f32[4,256,832]{1,2,0:T(8,128)S(1)} all-to-all(f32[4,256,832]{1,2,0:T(8,128)S(1)} %bitcast.53), channel_id=1, replica_groups=mesh['y'=4,'xl'=2,'z'=8,'xh'=2,'c'=2] {'y'}, dimensions={0} | all-to-all | bytes 6815744 | tf_op jit(solution)/shard_map/all_to_all | solution.py:16
  152.5 1.2 reduce_sum.66
  153.7 1.2 copy_bitcast_fusion.1
  154.9 12.7 %all_to_all.40 = f32[2,128,832]{1,2,0:T(8,128)S(1)} all-to-all(f32[2,128,832]{1,2,0:T(8,128)S(1)} %copy_bitcast_fusion.1), channel_id=1, replica_groups=mesh['y'=4,'xl'=2,'z'=8,'xh'=2,'c'=2] {'xl'}, dimensions={0} | all-to-all | bytes 1703936 | tf_op jit(solution)/shard_map/all_to_all | solution.py:16
  167.6 0.1 reduce_sum.67
  167.7 1.0 copy.144
  168.7 4.1 %all-to-all-start.3 = ((f32[8,16,832]{2,1,0:T(8,128)}), f32[8,16,832]{2,1,0:T(8,128)}, u32[]{:S(2)}, u32[]{:S(2)}) async-start(f32[8,16,832]{2,1,0:T(8,128)} %bitcast.13), calls=%async_computation.3 | async-start | bytes 917504 | tf_op jit(solution)/shard_map/all_to_all | solution.py:16
  172.8 3.4 %fusion.4 = f32[512,512]{0,1:T(8,128)S(1)} fusion(f32[2,512,1024]{2,1,0:T(8,128)} %param.9, f32[512,512]{0,1:T(8,128)S(1)} %copy-done.4, f32[512,512]{0,1:T(8,128)S(1)} %copy-done.2), kind=kOutput, calls=%fused_computation.8 | convolution fusion | flops 1611137024 | bytes 5242880 | tf_op jit(solution)/shard_map/dot_general | solution.py:39
  176.3 1.3 collective-permute-start.3
  177.6 8.6 %all-to-all-done.3 = f32[8,16,832]{2,1,0:T(8,128)} async-done(((f32[8,16,832]{2,1,0:T(8,128)}), f32[8,16,832]{2,1,0:T(8,128)}, u32[]{:S(2)}, u32[]{:S(2)}) %all-to-all-start.3) | async-done | bytes 426016 | tf_op jit(solution)/shard_map/all_to_all | solution.py:16
  186.2 1.7 reduce_sum.68
  187.9 3.7 %all-to-all-start.4 = ((f32[2,8,832]{2,1,0:T(8,128)}), f32[2,8,832]{2,1,0:T(8,128)S(1)}, u32[]{:S(2)}, u32[]{:S(2)}) async-start(f32[2,8,832]{2,1,0:T(8,128)} %bitcast.14), calls=%async_computation.4 | async-start | bytes 114688 | tf_op jit(solution)/shard_map/all_to_all | solution.py:16
  191.6 0.0 collective-permute-done.3
  191.6 1.2 fusion.37
  192.7 1.0 copy.146
  193.7 2.3 %all-to-all-done.4 = f32[2,8,832]{2,1,0:T(8,128)S(1)} async-done(((f32[2,8,832]{2,1,0:T(8,128)}), f32[2,8,832]{2,1,0:T(8,128)S(1)}, u32[]{:S(2)}, u32[]{:S(2)}) %all-to-all-start.4) | async-done | bytes 53280 | tf_op jit(solution)/shard_map/all_to_all | solution.py:16
  196.0 8.5 %all_to_all.41 = f32[2,4,832]{2,1,0:T(4,128)S(1)} all-to-all(f32[2,4,832]{2,1,0:T(4,128)S(1)} %all_to_all.30), channel_id=1, replica_groups=mesh['y'=4,'xl'=2,'z'=8,'xh'=2,'c'=2] {'c'}, dimensions={0} | all-to-all | bytes 53248 | tf_op jit(solution)/shard_map/all_to_all | solution.py:25
  204.5 0.1 mul.71
  204.6 0.6 slice.110
  205.2 0.6 slice.111
  205.8 0.6 reshape.41
  (53 shorter events, 0.2 us)
Async XLA Ops:
  0.6 5.9 %copy-start.27 = (f32[2,1024]{1,0:T(2,128)S(1)}, f32[2,1024]{1,0:T(2,128)}, u32[]{:S(2)}) copy-start(f32[2,1024]{1,0:T(2,128)} %param.10) | copy-start | bytes 24580
  0.6 5.9 %copy-start.20 = (f32[2,512,512]{2,1,0:T(8,128)S(1)}, f32[2,512,512]{2,1,0:T(8,128)}, u32[]{:S(2)}) copy-start(f32[2,512,512]{2,1,0:T(8,128)} %param.11) | copy-start | bytes 6291460
  2.1 9.3 %collective-permute-start = (f32[256,256]{0,1:T(8,128)S(1)}, f32[256,256]{0,1:T(8,128)S(1)}, u32[]{:S(2)}, u32[]{:S(2)}) collective-permute-start(f32[256,256]{0,1:T(8,128)S(1)} %get-tuple-element.46), channel_id=1, source_target_pairs={{0,4},{4,8},{8,12},{12,16},{16,20},{20,24},{24,28},{28,32},{32,36}... | collective-permute-start | bytes 786440 | tf_op jit(solution)/shard_map/ppermute | solution.py:31
  11.4 3.7 %copy-start.16 = (f32[256,256]{0,1:T(8,128)}, f32[256,256]{0,1:T(8,128)S(1)}, u32[]{:S(2)}) copy-start(f32[256,256]{0,1:T(8,128)S(1)} %collective-permute-done) | copy-start | bytes 786436
  15.1 1.3 copy-start.9
  15.1 5.5 %copy-start.23 = (f32[1,512,256]{2,1,0:T(8,128)S(1)}, f32[1,512,256]{2,1,0:T(8,128)}, u32[]{:S(2)}) copy-start(f32[1,512,256]{2,1,0:T(8,128)} %param.8) | copy-start | bytes 1572868
  15.1 6.5 %copy-start.24 = (f32[1,512,256]{2,1,0:T(8,128)S(1)}, f32[1,512,256]{2,1,0:T(8,128)}, u32[]{:S(2)}) copy-start(f32[1,512,256]{2,1,0:T(8,128)} %param.7) | copy-start | bytes 1572868
  16.5 13.7 %collective-permute-start.1 = (f32[512,256]{0,1:T(8,128)S(1)}, f32[512,256]{0,1:T(8,128)S(1)}, u32[]{:S(2)}, u32[]{:S(2)}) collective-permute-start(f32[512,256]{0,1:T(8,128)S(1)} %convolution_add_fusion), channel_id=1, source_target_pairs={{0,4},{4,8},{8,12},{12,16},{16,20},{20,24},{24,28},{28,32},{32,36}... | collective-permute-start | bytes 1572872 | tf_op jit(solution)/shard_map/ppermute | solution.py:31
  30.2 3.8 %copy-start.8 = (f32[512,256]{0,1:T(8,128)}, f32[512,256]{0,1:T(8,128)S(1)}, u32[]{:S(2)}) copy-start(f32[512,256]{0,1:T(8,128)S(1)} %collective-permute-done.1) | copy-start | bytes 1572868
  30.2 3.8 %copy-start.13 = (f32[1,512,256]{1,2,0:T(8,128)S(1)}, f32[1,512,256]{1,2,0:T(8,128)}, u32[]{:S(2)}) copy-start(f32[1,512,256]{1,2,0:T(8,128)} %copy.131) | copy-start | bytes 1572868
  30.2 3.9 %copy-start.21 = (f32[2,512,512]{2,1,0:T(8,128)S(1)}, f32[2,512,512]{2,1,0:T(8,128)}, u32[]{:S(2)}) copy-start(f32[2,512,512]{2,1,0:T(8,128)} %param.11) | copy-start | bytes 6291460
  30.2 3.9 %copy-start.25 = (f32[1,512,256]{1,2,0:T(8,128)S(1)}, f32[1,512,256]{1,2,0:T(8,128)}, u32[]{:S(2)}) copy-start(f32[1,512,256]{1,2,0:T(8,128)} %copy.132) | copy-start | bytes 1572868
  34.0 1.5 copy-start.11
  34.1 2.9 %copy-start = (f32[2,512,1024]{2,1,0:T(8,128)S(1)}, f32[2,512,1024]{2,1,0:T(8,128)}, u32[]{:S(2)}) copy-start(f32[2,512,1024]{2,1,0:T(8,128)} %param.9) | copy-start | bytes 12582916
  38.9 1.0 copy-start.6
  40.8 14.2 %collective-permute-start.2 = (f32[512,256]{0,1:T(8,128)}, f32[512,256]{0,1:T(8,128)}, u32[]{:S(2)}, u32[]{:S(2)}) collective-permute-start(f32[512,256]{0,1:T(8,128)} %slice.106), channel_id=1, source_target_pairs={{4,0},{8,4},{12,8},{16,12},{20,16},{24,20},{28,24},{32,28},{36,32}... | collective-permute-start | bytes 1572872 | tf_op jit(solution)/shard_map/ppermute | solution.py:31
  43.4 4.4 %copy-start.12 = (f32[512,1024]{0,1:T(8,128)S(1)}, f32[512,1024]{0,1:T(8,128)}, u32[]{:S(2)}) copy-start(f32[512,1024]{0,1:T(8,128)} %copy-done.11) | copy-start | bytes 6291460
  43.4 4.4 %copy-start.14 = (f32[1,512,256]{1,2,0:T(8,128)S(1)}, f32[1,512,256]{1,2,0:T(8,128)}, u32[]{:S(2)}) copy-start(f32[1,512,256]{1,2,0:T(8,128)} %copy.131) | copy-start | bytes 1572868
  43.4 4.4 %copy-start.26 = (f32[1,512,256]{1,2,0:T(8,128)S(1)}, f32[1,512,256]{1,2,0:T(8,128)}, u32[]{:S(2)}) copy-start(f32[1,512,256]{1,2,0:T(8,128)} %copy.132) | copy-start | bytes 1572868
  47.7 7.2 %copy-start.7 = (f32[512,512]{0,1:T(8,128)S(1)}, f32[512,512]{0,1:T(8,128)}, u32[]{:S(2)}) copy-start(f32[512,512]{0,1:T(8,128)} %copy-done.6) | copy-start | bytes 3145732
  47.8 8.4 %copy-start.22 = (f32[2,512,512]{2,1,0:T(8,128)S(1)}, f32[2,512,512]{2,1,0:T(8,128)}, u32[]{:S(2)}) copy-start(f32[2,512,512]{2,1,0:T(8,128)} %param.11) | copy-start | bytes 6291460
  50.0 6.1 %copy-start.10 = (f32[512,1024]{0,1:T(8,128)S(1)}, f32[512,1024]{0,1:T(8,128)}, u32[]{:S(2)}) copy-start(f32[512,1024]{0,1:T(8,128)} %copy-done.9) | copy-start | bytes 6291460
  56.2 1.4 copy-start.15
  57.6 4.4 %copy-start.1 = (f32[512,512]{0,1:T(8,128)}, f32[512,512]{0,1:T(8,128)S(1)}, u32[]{:S(2)}) copy-start(f32[512,512]{0,1:T(8,128)S(1)} %get-tuple-element.40) | copy-start | bytes 3145732
  57.6 4.4 %copy-start.3 = (f32[512,512]{0,1:T(8,128)}, f32[512,512]{0,1:T(8,128)S(1)}, u32[]{:S(2)}) copy-start(f32[512,512]{0,1:T(8,128)S(1)} %get-tuple-element.41) | copy-start | bytes 3145732
  59.9 1.1 copy-start.18
  59.9 2.2 %copy-start.17 = (f32[256,256]{0,1:T(8,128)S(1)}, f32[256,256]{0,1:T(8,128)}, u32[]{:S(2)}) copy-start(f32[256,256]{0,1:T(8,128)} %copy-done.16) | copy-start | bytes 786436
  62.0 1.9 copy-start.5
  62.0 1.9 copy-start.19
  154.9 17.9 %copy-start.2 = (f32[512,512]{0,1:T(8,128)S(1)}, f32[512,512]{0,1:T(8,128)}, u32[]{:S(2)}) copy-start(f32[512,512]{0,1:T(8,128)} %copy-done.1) | copy-start | bytes 3145732
  154.9 17.9 %copy-start.4 = (f32[512,512]{0,1:T(8,128)S(1)}, f32[512,512]{0,1:T(8,128)}, u32[]{:S(2)}) copy-start(f32[512,512]{0,1:T(8,128)} %copy-done.3) | copy-start | bytes 3145732
  168.7 17.5 %all-to-all-start.3 = ((f32[8,16,832]{2,1,0:T(8,128)}), f32[8,16,832]{2,1,0:T(8,128)}, u32[]{:S(2)}, u32[]{:S(2)}) async-start(f32[8,16,832]{2,1,0:T(8,128)} %bitcast.13), calls=%async_computation.3 | async-start | bytes 917504 | tf_op jit(solution)/shard_map/all_to_all | solution.py:16
  176.3 15.3 %collective-permute-start.3 = (f32[256,256]{0,1:T(8,128)S(1)}, f32[256,256]{0,1:T(8,128)S(1)}, u32[]{:S(2)}, u32[]{:S(2)}) collective-permute-start(f32[256,256]{0,1:T(8,128)S(1)} %get-tuple-element.45), channel_id=1, source_target_pairs={{4,0},{8,4},{12,8},{16,12},{20,16},{24,20},{28,24},{32,28},{36,32}... | collective-permute-start | bytes 786440 | tf_op jit(solution)/shard_map/ppermute | solution.py:31
  187.9 8.1 %all-to-all-start.4 = ((f32[2,8,832]{2,1,0:T(8,128)}), f32[2,8,832]{2,1,0:T(8,128)S(1)}, u32[]{:S(2)}, u32[]{:S(2)}) async-start(f32[2,8,832]{2,1,0:T(8,128)} %bitcast.14), calls=%async_computation.4 | async-start | bytes 114688 | tf_op jit(solution)/shard_map/all_to_all | solution.py:16
where the time goes:
time: 208 us; the launch traced here: 206 us
  blocking collectives  92.4 us (44%)
  waiting for transfers between devices  28.2 us (14%)
  matrix products  27.3 us (13%)
  local copies, waits for them, and re-layouts  22.2 us (11%)
  starting transfers between devices  19.1 us (9%)
  other arithmetic  16.1 us (8%)
    all_to_all x2, blocking collectives, reduce_rows(): return lax.all_to_all(block, axis, 0, 0, tiled=True).sum(axis=0)  65.1 us
    dot_general x8, matrix products, contract(): lax.dot_general(left, right, (((left_dim,), (right_dim,)), ((), ())), pre...  18.9 us
    all_to_all x1, blocking collectives, reduce_to_owner(): lax.all_to_all(packed.reshape(rows, 2, width // 2), 'c', 1, 1, tiled=True)  18.8 us
    ppermute x4, waiting for transfers between devices, from_behind(): return lax.ppermute(block, axis, route)  17.3 us
    ppermute x4, starting transfers between devices, from_behind(): return lax.ppermute(block, axis, route)  11.3 us
    all_to_all x2, waiting for transfers between devices, reduce_rows(): return lax.all_to_all(block, axis, 0, 0, tiled=True).sum(axis=0)  10.9 us
    all_to_all x1, blocking collectives, reduce_to_owner(): return lax.all_to_all(block, 'c', 0, 1, tiled=True)  8.46 us
    dot_general x3, matrix products, matmul(): jnp.dot(left, right, precision=lax.Precision.HIGH, preferred_element_type...  8.41 us
  transfers between devices with their start and end apart: 6, of which 5 were waited for; matrix products, arithmetic and copies ran while one was open for 8% of the time, Pallas kernels for 0%

commit v1 on v0

--- a/solution.py
+++ b/solution.py
@@ -18,11 +18,11 @@
 
 def reduce_to_owner(packed):
     rows, width = packed.shape
-    halves = lax.all_to_all(packed.reshape(rows, 2, width // 2), "c", 1, 1, tiled=True)
-    block = halves.sum(axis=1)
-    for axis in ("y", "xl", "z", "xh"):
+    sizes = [lax.axis_size(a) for a in ("y", "xl", "z", "xh", "c")]
+    block = packed.reshape(*sizes, -1, width).transpose(4, 3, 1, 0, 2, 5, 6).reshape(rows, width)
+    for axis in ("c", ("xh", "xl"), "y", "z"):
         block = reduce_rows(block, axis)
-    return lax.all_to_all(block, "c", 0, 1, tiled=True)
+    return block
 
 
 def from_behind(block, axis, distance):

time: 208 us -> 201 us (0.966)
  the two profiles are of different devices: /device:TPU:1 before, /device:TPU:10 now
where the time goes in v1:
time: 201 us; the launch traced here: 200 us
  blocking collectives  55.8 us (28%)
  waiting for transfers between devices  38.5 us (19%)
  local copies, waits for them, and re-layouts  33.9 us (17%)
  starting transfers between devices  27.3 us (14%)
  matrix products  27.3 us (14%)
  other arithmetic  16.6 us (8%)
    all_to_all x2, blocking collectives, reduce_rows(): return lax.all_to_all(block, axis, 0, 0, tiled=True).sum(axis=0)  55.8 us
    ppermute x4, waiting for transfers between devices, from_behind(): return lax.ppermute(block, axis, route)  27.8 us
    dot_general x8, matrix products, contract(): lax.dot_general(left, right, (((left_dim,), (right_dim,)), ((), ())), pre...  18.9 us
    reshape x2, local copies, waits for them, and re-layouts, reduce_to_owner(): packed.reshape(*sizes, -1, width).transpose(4, 3, 1, 0, 2, 5, 6)  17.8 us
    all_to_all x2, starting transfers between devices, reduce_rows(): return lax.all_to_all(block, axis, 0, 0, tiled=True).sum(axis=0)  14.1 us
    ppermute x4, starting transfers between devices, from_behind(): return lax.ppermute(block, axis, route)  13.2 us
    all_to_all x2, waiting for transfers between devices, reduce_rows(): return lax.all_to_all(block, axis, 0, 0, tiled=True).sum(axis=0)  10.7 us
    dot_general x3, matrix products, matmul(): jnp.dot(left, right, precision=lax.Precision.HIGH, preferred_element_type...  8.42 us
  transfers between devices with their start and end apart: 6, of which 5 were waited for; matrix products, arithmetic and copies ran while one was open for 8% of the time, Pallas kernels for 0%

profile of v1, /device:TPU:10, one launch (start us, length us, event | category | flops | bytes accessed | tf_op | source)
XLA Modules:
  0.0 200.4 jit_solution(10964333660329480509)
XLA Ops:
  0.6 0.0 copy-start.21
  0.7 1.4 copy.79
  2.1 3.8 %collective-permute-start = (f32[256,256]{0,1:T(8,128)S(1)}, f32[256,256]{0,1:T(8,128)S(1)}, u32[]{:S(2)}, u32[]{:S(2)}) collective-permute-start(f32[256,256]{0,1:T(8,128)S(1)} %get-tuple-element.34), channel_id=1, source_target_pairs={{0,4},{4,8},{8,12},{12,16},{16,20},{20,24},{24,28},{28,32},{32,36}... | collective-permute-start | bytes 786440 | tf_op jit(solution)/shard_map/ppermute | solution.py:31
  6.0 0.1 slice_bitcast_fusion
  6.0 10.1 %collective-permute-done = f32[256,256]{0,1:T(8,128)S(1)} collective-permute-done((f32[256,256]{0,1:T(8,128)S(1)}, f32[256,256]{0,1:T(8,128)S(1)}, u32[]{:S(2)}, u32[]{:S(2)}) %collective-permute-start) | collective-permute-done | bytes 262176 | tf_op jit(solution)/shard_map/ppermute | solution.py:31
  16.1 3.7 %fusion.12 = f32[512,1024]{0,1:T(8,128)S(1)} fusion(f32[2,512,1024]{2,1,0:T(8,128)} %param.9, f32[1024]{0:T(1024)S(1)} %bitcast.53, f32[512,256]{0,1:T(8,128)S(1)} %bitcast.44, f32[256,256]{0,1:T(8,128)S(1)} %get-tuple-element.35, f32[256,256]{0,1:T(8,128)S(1)} %collective-permute-done), kind=kOutput, calls=%fused_computation.15 | convolution fusion | flops 1611661312 | bytes 5246976 | tf_op jit(solution)/shard_map/dot_general | solution.py:35
  19.8 0.0 copy-done.17
  19.8 0.0 copy-start.9
  19.8 0.0 copy-start.24
  19.8 0.0 copy-start.25
  19.9 0.9 convolution_add_fusion
  20.8 0.4 copy-done.9
  21.2 1.9 collective-permute-start.1
  23.1 1.0 copy.78
  24.1 1.0 copy.77
  25.1 13.2 %collective-permute-done.1 = f32[512,256]{0,1:T(8,128)S(1)} collective-permute-done((f32[512,256]{0,1:T(8,128)S(1)}, f32[512,256]{0,1:T(8,128)S(1)}, u32[]{:S(2)}, u32[]{:S(2)}) %collective-permute-start.1) | collective-permute-done | bytes 524320 | tf_op jit(solution)/shard_map/ppermute | solution.py:31
  38.3 3.8 %fusion.15 = f32[512,1024]{0,1:T(8,128)S(1)} fusion(f32[2,512,1024]{2,1,0:T(8,128)} %param.9, f32[1024]{0:T(1024)S(1)} %bitcast.52, f32[512,256]{0,1:T(8,128)S(1)} %convolution_add_fusion, f32[512,256]{0,1:T(8,128)S(1)} %collective-permute-done.1), kind=kOutput, calls=%fused_computation.16 | convolution fusion | flops 1611399168 | bytes 5246976 | tf_op jit(solution)/shard_map/dot_general | solution.py:35
  42.1 0.0 copy-done.8
  42.1 0.0 copy-start.11
  42.1 0.0 copy-done.13
  42.1 0.0 copy-start
  42.1 1.4 subtract_multiply_fusion.3
  43.6 1.5 copy-done
  45.1 1.9 fusion
  47.0 1.0 copy-done.6
  47.9 0.9 slice.106
  48.8 2.1 %collective-permute-start.2 = (f32[512,256]{0,1:T(8,128)}, f32[512,256]{0,1:T(8,128)}, u32[]{:S(2)}, u32[]{:S(2)}) collective-permute-start(f32[512,256]{0,1:T(8,128)} %slice.106), channel_id=1, source_target_pairs={{4,0},{8,4},{12,8},{16,12},{20,16},{24,20},{28,24},{32,28},{36,32}... | collective-permute-start | bytes 1572872 | tf_op jit(solution)/shard_map/ppermute | solution.py:31
  50.9 0.2 fusion.20
  51.1 0.9 concatenate.52
  52.1 4.4 %fusion.21 = f32[512,1024]{1,0:T(8,128)} fusion(f32[512,512]{0,1:T(8,128)S(1)} %get-tuple-element.31, f32[512,512]{0,1:T(8,128)S(1)} %get-tuple-element.30, f32[512,256]{0,1:T(8,128)S(1)} %convolution_add_fusion, f32[512,256]{0,1:T(8,128)} %copy-done.8), kind=kOutput, calls=%fused_computation.20 | convolution fusion | flops 1611399168 | bytes 5242880 | tf_op jit(solution)/shard_map/dot_general | solution.py:39
  56.4 0.0 copy-start.23
  56.4 2.3 %fusion.30 = f32[512,512]{1,0:T(8,128)} fusion(f32[512,256]{0,1:T(8,128)S(1)} %bitcast.49, f32[512,256]{0,1:T(8,128)S(1)} %bitcast.47, f32[512,1024]{0,1:T(8,128)S(1)} %copy-done.12), kind=kOutput, calls=%fused_computation.38 | convolution fusion | flops 806617088 | bytes 4194304 | tf_op jit(solution)/shard_map/dot_general | solution.py:39
  58.7 4.5 %collective-permute-done.2 = f32[512,256]{0,1:T(8,128)} collective-permute-done((f32[512,256]{0,1:T(8,128)}, f32[512,256]{0,1:T(8,128)}, u32[]{:S(2)}, u32[]{:S(2)}) %collective-permute-start.2) | collective-permute-done | bytes 524320 | tf_op jit(solution)/shard_map/ppermute | solution.py:31
  63.2 1.2 fusion.38
  64.4 0.0 copy-start.15
  64.4 1.4 subtract_multiply_fusion.1
  65.9 2.2 %fusion.33 = f32[512,512]{1,0:T(8,128)} fusion(f32[512,256]{0,1:T(8,128)S(1)} %bitcast.51, f32[512,256]{0,1:T(8,128)S(1)} %fusion.38, f32[512,1024]{0,1:T(8,128)S(1)} %copy-done.10), kind=kOutput, calls=%fused_computation.46 | convolution fusion | flops 806617088 | bytes 4194304 | tf_op jit(solution)/shard_map/dot_general | solution.py:39
  68.1 0.2 fusion.18
  68.4 0.9 concatenate.51
  69.3 1.0 select_maximum_fusion
  70.3 1.9 fusion.19
  72.2 5.6 %pad_maximum_fusion = f32[1024,1664]{1,0:T(8,128)} fusion(f32[1024,128]{1,0:T(8,128)S(1)} %select_maximum_fusion, f32[512,512]{1,0:T(8,128)S(1)} %copy-done.20, f32[512,512]{1,0:T(8,128)} %fusion.33, f32[512,1024]{1,0:T(8,128)S(1)} %copy-done.5, f32[512,1024]{1,0:T(8,128)S(1)} %fusion.19), kind=kLoop, calls=%fused_computation | loop fusion | flops 6815744 | bytes 13631488 | tf_op jit(solution)/shard_map/concatenate | solution.py:121
  77.8 8.5 %reshape.28 = f32[4,2,8,2,2,4,1664]{6,5,4,3,2,1,0:T(4,128)} reshape(f32[1024,1664]{1,0:T(8,128)} %pad_maximum_fusion) | data formatting | bytes 13631488 | tf_op jit(solution)/shard_map/reshape | solution.py:22
  86.3 9.3 %copy.87 = f32[4,2,8,2,2,4,1664]{6,4,5,2,0,1,3:T(2,128)} copy(f32[4,2,8,2,2,4,1664]{6,5,4,3,2,1,0:T(4,128)} %reshape.28) | data formatting | bytes 13631488 | tf_op jit(solution)/shard_map/reshape | solution.py:22
  95.6 3.4 %copy.88 = f32[2,512,1664]{2,1,0:T(8,128)S(1)} copy(f32[2,512,1664]{2,0,1:T(2,128)} %bitcast.42) | data formatting | bytes 13631488 | tf_op jit(solution)/shard_map/reshape;reshape | solution.py:15
  99.0 10.4 %all_to_all.20 = f32[2,512,1664]{2,1,0:T(8,128)} all-to-all(f32[2,512,1664]{2,1,0:T(8,128)S(1)} %copy.88), channel_id=1, replica_groups=mesh['y'=4,'xl'=2,'z'=8,'xh'=2,'c'=2] {'c'}, dimensions={0} | all-to-all | bytes 13631488 | tf_op jit(solution)/shard_map/all_to_all | solution.py:16
  109.4 3.7 %reduce_sum.56 = f32[512,1664]{1,0:T(8,128)S(1)} reduce(f32[2,512,1664]{2,1,0:T(8,128)} %all_to_all.20, f32[]{:T(128)} %constant.1.clone.1), dimensions={0}, to_apply=%region_2.3 | reduce | flops 851968 | bytes 10223620 | tf_op jit(solution)/shard_map/reduce_sum | solution.py:16
  113.1 45.4 %all_to_all.21 = f32[4,128,1664]{2,1,0:T(8,128)} all-to-all(f32[4,128,1664]{2,1,0:T(8,128)S(1)} %bitcast.43), channel_id=1, replica_groups=mesh['y'=4,'xl'=2,'z'=8,'xh'=2,'c'=2] {'xh','xl'}, dimensions={0} | all-to-all | bytes 6815744 | tf_op jit(solution)/shard_map/all_to_all | solution.py:16
  158.5 3.3 %reduce_sum.57 = f32[128,1664]{1,0:T(8,128)} reduce(f32[4,128,1664]{2,1,0:T(8,128)} %all_to_all.21, f32[]{:T(128)} %constant.1.clone.1), dimensions={0}, to_apply=%region_3.4 | reduce | flops 638976 | bytes 4259844 | tf_op jit(solution)/shard_map/reduce_sum | solution.py:16
  161.8 5.0 %all-to-all-start.2 = ((f32[4,32,1664]{2,1,0:T(8,128)}), f32[4,32,1664]{2,1,0:T(8,128)}, u32[]{:S(2)}, u32[]{:S(2)}) async-start(f32[4,32,1664]{2,1,0:T(8,128)} %bitcast.15), calls=%async_computation.2 | async-start | bytes 1703936 | tf_op jit(solution)/shard_map/all_to_all | solution.py:16
  166.8 3.4 %fusion.4 = f32[512,512]{0,1:T(8,128)S(1)} fusion(f32[2,512,1024]{2,1,0:T(8,128)} %param.9, f32[512,512]{0,1:T(8,128)S(1)} %copy-done.4, f32[512,512]{0,1:T(8,128)S(1)} %copy-done.2), kind=kOutput, calls=%fused_computation.7 | convolution fusion | flops 1611137024 | bytes 5242880 | tf_op jit(solution)/shard_map/dot_general | solution.py:39
  170.2 0.0 copy-start.16
  170.3 5.3 %collective-permute-start.3 = (f32[256,256]{0,1:T(8,128)S(1)}, f32[256,256]{0,1:T(8,128)S(1)}, u32[]{:S(2)}, u32[]{:S(2)}) collective-permute-start(f32[256,256]{0,1:T(8,128)S(1)} %get-tuple-element.33), channel_id=1, source_target_pairs={{4,0},{8,4},{12,8},{16,12},{20,16},{24,20},{28,24},{32,28},{36,32}... | collective-permute-start | bytes 786440 | tf_op jit(solution)/shard_map/ppermute | solution.py:31
  175.6 1.9 all-to-all-done.2
  177.5 1.2 reduce_sum.58
  178.8 0.7 reshape.31
  179.5 9.1 %all-to-all-start.3 = ((f32[8,4,1664]{2,1,0:T(4,128)}), f32[8,4,1664]{2,1,0:T(4,128)S(1)}, u32[]{:S(2)}, u32[]{:S(2)}) async-start(f32[8,4,1664]{2,1,0:T(4,128)} %reshape.31), calls=%async_computation.3 | async-start | bytes 425984 | tf_op jit(solution)/shard_map/all_to_all | solution.py:16
  188.6 0.0 collective-permute-done.3
  188.6 0.1 fusion.37
  188.8 1.0 copy.90
  189.7 8.8 %all-to-all-done.3 = f32[8,4,1664]{2,1,0:T(4,128)S(1)} async-done(((f32[8,4,1664]{2,1,0:T(4,128)}), f32[8,4,1664]{2,1,0:T(4,128)S(1)}, u32[]{:S(2)}, u32[]{:S(2)}) %all-to-all-start.3) | async-done | bytes 213024 | tf_op jit(solution)/shard_map/all_to_all | solution.py:16
  198.6 0.6 slice.110
  199.2 0.6 slice.111
  199.8 0.6 reshape.32
  (49 shorter events, 0.2 us)
Async XLA Ops:
  0.6 5.3 %copy-start.28 = (f32[2,1024]{1,0:T(2,128)S(1)}, f32[2,1024]{1,0:T(2,128)}, u32[]{:S(2)}) copy-start(f32[2,1024]{1,0:T(2,128)} %param.10) | copy-start | bytes 24580
  0.6 5.3 %copy-start.21 = (f32[2,512,512]{2,1,0:T(8,128)S(1)}, f32[2,512,512]{2,1,0:T(8,128)}, u32[]{:S(2)}) copy-start(f32[2,512,512]{2,1,0:T(8,128)} %param.11) | copy-start | bytes 6291460
  2.1 14.0 %collective-permute-start = (f32[256,256]{0,1:T(8,128)S(1)}, f32[256,256]{0,1:T(8,128)S(1)}, u32[]{:S(2)}, u32[]{:S(2)}) collective-permute-start(f32[256,256]{0,1:T(8,128)S(1)} %get-tuple-element.34), channel_id=1, source_target_pairs={{0,4},{4,8},{8,12},{12,16},{16,20},{20,24},{24,28},{28,32},{32,36}... | collective-permute-start | bytes 786440 | tf_op jit(solution)/shard_map/ppermute | solution.py:31
  16.1 3.7 %copy-start.17 = (f32[256,256]{0,1:T(8,128)}, f32[256,256]{0,1:T(8,128)S(1)}, u32[]{:S(2)}) copy-start(f32[256,256]{0,1:T(8,128)S(1)} %collective-permute-done) | copy-start | bytes 786436
  19.8 1.3 copy-start.9
  19.8 3.2 %copy-start.24 = (f32[1,512,256]{2,1,0:T(8,128)S(1)}, f32[1,512,256]{2,1,0:T(8,128)}, u32[]{:S(2)}) copy-start(f32[1,512,256]{2,1,0:T(8,128)} %param.8) | copy-start | bytes 1572868
  19.8 4.2 %copy-start.25 = (f32[1,512,256]{2,1,0:T(8,128)S(1)}, f32[1,512,256]{2,1,0:T(8,128)}, u32[]{:S(2)}) copy-start(f32[1,512,256]{2,1,0:T(8,128)} %param.7) | copy-start | bytes 1572868
  21.2 17.1 %collective-permute-start.1 = (f32[512,256]{0,1:T(8,128)S(1)}, f32[512,256]{0,1:T(8,128)S(1)}, u32[]{:S(2)}, u32[]{:S(2)}) collective-permute-start(f32[512,256]{0,1:T(8,128)S(1)} %convolution_add_fusion), channel_id=1, source_target_pairs={{0,4},{4,8},{8,12},{12,16},{16,20},{20,24},{24,28},{28,32},{32,36}... | collective-permute-start | bytes 1572872 | tf_op jit(solution)/shard_map/ppermute | solution.py:31
  38.3 3.8 %copy-start.8 = (f32[512,256]{0,1:T(8,128)}, f32[512,256]{0,1:T(8,128)S(1)}, u32[]{:S(2)}) copy-start(f32[512,256]{0,1:T(8,128)S(1)} %collective-permute-done.1) | copy-start | bytes 1572868
  38.3 3.8 %copy-start.13 = (f32[1,512,256]{1,2,0:T(8,128)S(1)}, f32[1,512,256]{1,2,0:T(8,128)}, u32[]{:S(2)}) copy-start(f32[1,512,256]{1,2,0:T(8,128)} %copy.77) | copy-start | bytes 1572868
  38.3 3.9 %copy-start.22 = (f32[2,512,512]{2,1,0:T(8,128)S(1)}, f32[2,512,512]{2,1,0:T(8,128)}, u32[]{:S(2)}) copy-start(f32[2,512,512]{2,1,0:T(8,128)} %param.11) | copy-start | bytes 6291460
  38.3 3.9 %copy-start.26 = (f32[1,512,256]{1,2,0:T(8,128)S(1)}, f32[1,512,256]{1,2,0:T(8,128)}, u32[]{:S(2)}) copy-start(f32[1,512,256]{1,2,0:T(8,128)} %copy.78) | copy-start | bytes 1572868
  42.1 1.5 copy-start.11
  42.1 2.9 %copy-start = (f32[2,512,1024]{2,1,0:T(8,128)S(1)}, f32[2,512,1024]{2,1,0:T(8,128)}, u32[]{:S(2)}) copy-start(f32[2,512,1024]{2,1,0:T(8,128)} %param.9) | copy-start | bytes 12582916
  47.0 1.0 copy-start.6
  48.8 14.4 %collective-permute-start.2 = (f32[512,256]{0,1:T(8,128)}, f32[512,256]{0,1:T(8,128)}, u32[]{:S(2)}, u32[]{:S(2)}) collective-permute-start(f32[512,256]{0,1:T(8,128)} %slice.106), channel_id=1, source_target_pairs={{4,0},{8,4},{12,8},{16,12},{20,16},{24,20},{28,24},{32,28},{36,32}... | collective-permute-start | bytes 1572872 | tf_op jit(solution)/shard_map/ppermute | solution.py:31
  52.1 4.4 %copy-start.12 = (f32[512,1024]{0,1:T(8,128)S(1)}, f32[512,1024]{0,1:T(8,128)}, u32[]{:S(2)}) copy-start(f32[512,1024]{0,1:T(8,128)} %copy-done.11) | copy-start | bytes 6291460
  52.1 4.4 %copy-start.14 = (f32[1,512,256]{1,2,0:T(8,128)S(1)}, f32[1,512,256]{1,2,0:T(8,128)}, u32[]{:S(2)}) copy-start(f32[1,512,256]{1,2,0:T(8,128)} %copy.77) | copy-start | bytes 1572868
  52.1 4.4 %copy-start.27 = (f32[1,512,256]{1,2,0:T(8,128)S(1)}, f32[1,512,256]{1,2,0:T(8,128)}, u32[]{:S(2)}) copy-start(f32[1,512,256]{1,2,0:T(8,128)} %copy.78) | copy-start | bytes 1572868
  56.4 6.8 %copy-start.7 = (f32[512,512]{0,1:T(8,128)S(1)}, f32[512,512]{0,1:T(8,128)}, u32[]{:S(2)}) copy-start(f32[512,512]{0,1:T(8,128)} %copy-done.6) | copy-start | bytes 3145732
  56.4 8.0 %copy-start.23 = (f32[2,512,512]{2,1,0:T(8,128)S(1)}, f32[2,512,512]{2,1,0:T(8,128)}, u32[]{:S(2)}) copy-start(f32[2,512,512]{2,1,0:T(8,128)} %param.11) | copy-start | bytes 6291460
  58.7 5.7 %copy-start.10 = (f32[512,1024]{0,1:T(8,128)S(1)}, f32[512,1024]{0,1:T(8,128)}, u32[]{:S(2)}) copy-start(f32[512,1024]{0,1:T(8,128)} %copy-done.9) | copy-start | bytes 6291460
  64.4 1.4 copy-start.15
  65.9 4.4 %copy-start.1 = (f32[512,512]{0,1:T(8,128)}, f32[512,512]{0,1:T(8,128)S(1)}, u32[]{:S(2)}) copy-start(f32[512,512]{0,1:T(8,128)S(1)} %get-tuple-element.28) | copy-start | bytes 3145732
  65.9 4.4 %copy-start.3 = (f32[512,512]{0,1:T(8,128)}, f32[512,512]{0,1:T(8,128)S(1)}, u32[]{:S(2)}) copy-start(f32[512,512]{0,1:T(8,128)S(1)} %get-tuple-element.29) | copy-start | bytes 3145732
  68.1 1.1 copy-start.19
  68.1 2.2 %copy-start.18 = (f32[256,256]{0,1:T(8,128)S(1)}, f32[256,256]{0,1:T(8,128)}, u32[]{:S(2)}) copy-start(f32[256,256]{0,1:T(8,128)} %copy-done.17) | copy-start | bytes 786436
  70.3 1.9 copy-start.5
  70.3 1.9 copy-start.20
  158.5 8.3 %copy-start.2 = (f32[512,512]{0,1:T(8,128)S(1)}, f32[512,512]{0,1:T(8,128)}, u32[]{:S(2)}) copy-start(f32[512,512]{0,1:T(8,128)} %copy-done.1) | copy-start | bytes 3145732
  158.5 8.3 %copy-start.4 = (f32[512,512]{0,1:T(8,128)S(1)}, f32[512,512]{0,1:T(8,128)}, u32[]{:S(2)}) copy-start(f32[512,512]{0,1:T(8,128)} %copy-done.3) | copy-start | bytes 3145732
  161.8 15.8 %all-to-all-start.2 = ((f32[4,32,1664]{2,1,0:T(8,128)}), f32[4,32,1664]{2,1,0:T(8,128)}, u32[]{:S(2)}, u32[]{:S(2)}) async-start(f32[4,32,1664]{2,1,0:T(8,128)} %bitcast.15), calls=%async_computation.2 | async-start | bytes 1703936 | tf_op jit(solution)/shard_map/all_to_all | solution.py:16
  170.2 18.4 %copy-start.16 = (f32[512,256]{0,1:T(8,128)S(1)}, f32[512,256]{0,1:T(8,128)}, u32[]{:S(2)}) copy-start(f32[512,256]{0,1:T(8,128)} %copy-done.15) | copy-start | bytes 1572868
  170.3 18.3 %collective-permute-start.3 = (f32[256,256]{0,1:T(8,128)S(1)}, f32[256,256]{0,1:T(8,128)S(1)}, u32[]{:S(2)}, u32[]{:S(2)}) collective-permute-start(f32[256,256]{0,1:T(8,128)S(1)} %get-tuple-element.33), channel_id=1, source_target_pairs={{4,0},{8,4},{12,8},{16,12},{20,16},{24,20},{28,24},{32,28},{36,32}... | collective-permute-start | bytes 786440 | tf_op jit(solution)/shard_map/ppermute | solution.py:31
  179.5 19.1 %all-to-all-start.3 = ((f32[8,4,1664]{2,1,0:T(4,128)}), f32[8,4,1664]{2,1,0:T(4,128)S(1)}, u32[]{:S(2)}, u32[]{:S(2)}) async-start(f32[8,4,1664]{2,1,0:T(4,128)} %reshape.31), calls=%async_computation.3 | async-start | bytes 425984 | tf_op jit(solution)/shard_map/all_to_all | solution.py:16

commit v2 on v0

--- a/solution.py
+++ b/solution.py
@@ -18,9 +18,11 @@
 
 def reduce_to_owner(packed):
     rows, width = packed.shape
-    halves = lax.all_to_all(packed.reshape(rows, 2, width // 2), "c", 1, 1, tiled=True)
+    y, xl, z, xh, c = [lax.axis_size(a) for a in ("y", "xl", "z", "xh", "c")]
+    block = packed.reshape(y, xl, z, xh, -1, width).transpose(3, 1, 0, 2, 4, 5).reshape(rows, width)
+    halves = lax.all_to_all(block.reshape(rows, c, width // c), "c", 1, 1, tiled=True)
     block = halves.sum(axis=1)
-    for axis in ("y", "xl", "z", "xh"):
+    for axis in (("xh", "xl"), "y", "z"):
         block = reduce_rows(block, axis)
     return lax.all_to_all(block, "c", 0, 1, tiled=True)
 

time: 208 us -> 218 us (1.048)
  the two profiles are of different devices: /device:TPU:1 before, /device:TPU:10 now
where the time goes in v2:
time: 218 us; the launch traced here: 216 us
  blocking collectives  65.1 us (30%)
  local copies, waits for them, and re-layouts  40.3 us (18%)
  waiting for transfers between devices  39.8 us (18%)
  matrix products  29.6 us (14%)
  starting transfers between devices  27.2 us (12%)
  other arithmetic  13.4 us (6%)
    all_to_all x1, blocking collectives, reduce_rows(): return lax.all_to_all(block, axis, 0, 0, tiled=True).sum(axis=0)  45.4 us
    ppermute x4, waiting for transfers between devices, from_behind(): return lax.ppermute(block, axis, route)  27.7 us
    another operation x2, local copies, waits for them, and re-layouts, reduce_to_owner(): block.reshape(rows, c, width // c)  21.8 us
    dot_general x8, matrix products, contract(): lax.dot_general(left, right, (((left_dim,), (right_dim,)), ((), ())), pre...  21.1 us
    all_to_all x1, blocking collectives, reduce_to_owner(): lax.all_to_all(block.reshape(rows, c, width // c), 'c', 1, 1, tiled=True)  16 us
    all_to_all x2, starting transfers between devices, reduce_rows(): return lax.all_to_all(block, axis, 0, 0, tiled=True).sum(axis=0)  14.1 us
    ppermute x4, starting transfers between devices, from_behind(): return lax.ppermute(block, axis, route)  13.2 us
    all_to_all x2, waiting for transfers between devices, reduce_rows(): return lax.all_to_all(block, axis, 0, 0, tiled=True).sum(axis=0)  12 us
  transfers between devices with their start and end apart: 6, of which 5 were waited for; matrix products, arithmetic and copies ran while one was open for 8% of the time, Pallas kernels for 0%

profile of v2, /device:TPU:10, one launch (start us, length us, event | category | flops | bytes accessed | tf_op | source)
XLA Modules:
  0.0 216.4 jit_solution(2987108821333103382)
XLA Ops:
  0.6 0.0 copy-start.17
  0.7 1.4 copy.133
  2.1 3.8 %collective-permute-start = (f32[256,256]{0,1:T(8,128)S(1)}, f32[256,256]{0,1:T(8,128)S(1)}, u32[]{:S(2)}, u32[]{:S(2)}) collective-permute-start(f32[256,256]{0,1:T(8,128)S(1)} %get-tuple-element.46), channel_id=1, source_target_pairs={{0,4},{4,8},{8,12},{12,16},{16,20},{20,24},{24,28},{28,32},{32,36}... | collective-permute-start | bytes 786440 | tf_op jit(solution)/shard_map/ppermute | solution.py:33
  5.9 0.0 copy-done.24
  6.0 0.1 slice_bitcast_fusion
  6.0 10.1 %collective-permute-done = f32[256,256]{0,1:T(8,128)S(1)} collective-permute-done((f32[256,256]{0,1:T(8,128)S(1)}, f32[256,256]{0,1:T(8,128)S(1)}, u32[]{:S(2)}, u32[]{:S(2)}) %collective-permute-start) | collective-permute-done | bytes 262176 | tf_op jit(solution)/shard_map/ppermute | solution.py:33
  16.1 3.7 %fusion.12 = f32[512,1024]{0,1:T(8,128)S(1)} fusion(f32[2,512,1024]{2,1,0:T(8,128)} %param.9, f32[1024]{0:T(1024)S(1)} %bitcast.64, f32[512,256]{0,1:T(8,128)S(1)} %bitcast.55, f32[256,256]{0,1:T(8,128)S(1)} %get-tuple-element.47, f32[256,256]{0,1:T(8,128)S(1)} %collective-permute-done), kind=kOutput, calls=%fused_computation.17 | convolution fusion | flops 1611661312 | bytes 5246976 | tf_op jit(solution)/shard_map/dot_general | solution.py:37
  19.8 0.0 copy-done.16
  19.8 0.0 copy-start.20
  19.8 0.0 copy-start.21
  19.9 0.9 convolution_add_fusion
  20.8 0.3 copy-done.8
  21.1 1.9 collective-permute-start.1
  23.1 1.0 copy.132
  24.1 1.0 copy.131
  25.1 13.2 %collective-permute-done.1 = f32[512,256]{0,1:T(8,128)S(1)} collective-permute-done((f32[512,256]{0,1:T(8,128)S(1)}, f32[512,256]{0,1:T(8,128)S(1)}, u32[]{:S(2)}, u32[]{:S(2)}) %collective-permute-start.1) | collective-permute-done | bytes 524320 | tf_op jit(solution)/shard_map/ppermute | solution.py:33
  38.2 3.8 %fusion.15 = f32[512,1024]{0,1:T(8,128)S(1)} fusion(f32[2,512,1024]{2,1,0:T(8,128)} %param.9, f32[1024]{0:T(1024)S(1)} %bitcast.63, f32[512,256]{0,1:T(8,128)S(1)} %convolution_add_fusion, f32[512,256]{0,1:T(8,128)S(1)} %collective-permute-done.1), kind=kOutput, calls=%fused_computation.18 | convolution fusion | flops 1611399168 | bytes 5246976 | tf_op jit(solution)/shard_map/dot_general | solution.py:37
  42.1 0.0 copy-start
  42.1 1.4 subtract_multiply_fusion.3
  43.5 1.5 copy-done
  45.0 1.9 fusion
  46.9 1.0 copy-done.5
  47.9 0.9 slice.106
  48.8 2.1 collective-permute-start.2
  50.9 0.2 fusion.20
  51.1 0.9 concatenate.52
  52.0 4.4 %fusion.21 = f32[512,1024]{1,0:T(8,128)} fusion(f32[512,512]{0,1:T(8,128)S(1)} %get-tuple-element.43, f32[512,512]{0,1:T(8,128)S(1)} %get-tuple-element.42, f32[512,256]{0,1:T(8,128)S(1)} %convolution_add_fusion, f32[512,256]{0,1:T(8,128)} %copy-done.7), kind=kOutput, calls=%fused_computation.22 | convolution fusion | flops 1611399168 | bytes 5242880 | tf_op jit(solution)/shard_map/dot_general | solution.py:41
  56.4 0.0 copy-start.19
  56.4 2.2 %fusion.30 = f32[512,512]{1,0:T(8,128)} fusion(f32[512,256]{0,1:T(8,128)S(1)} %bitcast.60, f32[512,256]{0,1:T(8,128)S(1)} %bitcast.58, f32[512,1024]{0,1:T(8,128)S(1)} %copy-done.11), kind=kOutput, calls=%fused_computation.40 | convolution fusion | flops 806617088 | bytes 4194304 | tf_op jit(solution)/shard_map/dot_general | solution.py:41
  58.7 4.5 %collective-permute-done.2 = f32[512,256]{0,1:T(8,128)} collective-permute-done((f32[512,256]{0,1:T(8,128)}, f32[512,256]{0,1:T(8,128)}, u32[]{:S(2)}, u32[]{:S(2)}) %collective-permute-start.2) | collective-permute-done | bytes 524320 | tf_op jit(solution)/shard_map/ppermute | solution.py:33
  63.2 1.2 fusion.38
  64.4 0.0 copy-start.14
  64.4 1.4 subtract_multiply_fusion.1
  65.9 2.3 %fusion.33 = f32[512,512]{1,0:T(8,128)} fusion(f32[512,256]{0,1:T(8,128)S(1)} %bitcast.62, f32[512,256]{0,1:T(8,128)S(1)} %fusion.38, f32[512,1024]{0,1:T(8,128)S(1)} %copy-done.9), kind=kOutput, calls=%fused_computation.48 | convolution fusion | flops 806617088 | bytes 4194304 | tf_op jit(solution)/shard_map/dot_general | solution.py:41
  68.1 0.2 fusion.18
  68.3 0.9 concatenate.51
  69.2 1.1 select_maximum_fusion
  70.4 4.1 %fusion.19 = f32[512,1024]{1,0:T(8,128)} fusion(f32[512,512]{0,1:T(8,128)S(1)} %get-tuple-element.41, f32[512,512]{0,1:T(8,128)S(1)} %get-tuple-element.40, f32[512,256]{0,1:T(8,128)S(1)} %bitcast.56, f32[256,256]{0,1:T(8,128)S(1)} %get-tuple-element.47, f32[256,256]{0,1:T(8,128)} %copy-done.16), kind=kOutput, calls=%fused_computation.20 | convolution fusion | flops 1611661312 | bytes 5242880 | tf_op jit(solution)/shard_map/dot_general | solution.py:41
  74.5 3.4 %pad_maximum_fusion = f32[1024,1664]{1,0:T(8,128)S(1)} fusion(f32[1024,128]{1,0:T(8,128)S(1)} %select_maximum_fusion, f32[512,512]{1,0:T(8,128)} %fusion.30, f32[512,512]{1,0:T(8,128)} %fusion.33, f32[512,1024]{1,0:T(8,128)} %fusion.21, f32[512,1024]{1,0:T(8,128)} %fusion.19), kind=kLoop, calls=%fused_computation | loop fusion | flops 6815744 | bytes 13631488 | tf_op jit(solution)/shard_map/concatenate | solution.py:123
  77.9 3.6 %copy.153 = f32[4,2,8,2,8,1664]{5,4,2,0,1,3:T(8,128)} copy(f32[4,2,8,2,8,1664]{5,4,3,2,1,0:T(8,128)S(1)} %bitcast.52) | data formatting | bytes 13631488 | tf_op jit(solution)/shard_map/reshape | solution.py:22
  81.5 10.1 %reshape_reshape.3 = f32[1024,2,832]{2,1,0:T(2,128)} reshape(f32[2,2,4,8,8,1664]{5,4,3,2,1,0:T(8,128)} %bitcast.51) | data formatting | bytes 13631488 | tf_op jit(solution)/shard_map/reshape;reshape | solution.py:23
  91.6 11.6 %copy.142 = f32[1024,2,832]{0,2,1:T(8,128)} copy(f32[1024,2,832]{2,1,0:T(2,128)} %reshape_reshape.3) | data formatting | bytes 13631488 | tf_op jit(solution)/shard_map/reshape;reshape | solution.py:23
  103.3 16.0 %all_to_all.33 = f32[1024,2,832]{0,2,1:T(8,128)} all-to-all(f32[1024,2,832]{0,2,1:T(8,128)} %copy.142), channel_id=1, replica_groups=mesh['y'=4,'xl'=2,'z'=8,'xh'=2,'c'=2] {'c'}, dimensions={1} | all-to-all | bytes 13631488 | tf_op jit(solution)/shard_map/all_to_all | solution.py:23
  119.2 4.0 %reduce_sum.56 = f32[1024,832]{0,1:T(8,128)S(1)} reduce(f32[1024,2,832]{0,2,1:T(8,128)} %all_to_all.33, f32[]{:T(128)} %constant.1.clone.1), dimensions={1}, to_apply=%region_2.3 | reduce | flops 851968 | bytes 10223620 | tf_op jit(solution)/shard_map/reduce_sum | solution.py:24
  123.2 0.3 copy.154
  123.5 45.4 %all_to_all.34 = f32[4,256,832]{1,2,0:T(8,128)S(1)} all-to-all(f32[4,256,832]{1,2,0:T(8,128)S(1)} %bitcast.54), channel_id=1, replica_groups=mesh['y'=4,'xl'=2,'z'=8,'xh'=2,'c'=2] {'xh','xl'}, dimensions={0} | all-to-all | bytes 6815744 | tf_op jit(solution)/shard_map/all_to_all | solution.py:16
  168.9 1.2 reduce_sum.57
  170.1 2.6 %copy.144 = f32[256,832]{1,0:T(8,128)} copy(f32[256,832]{0,1:T(8,128)} %reduce_sum.57) | data formatting | bytes 1703936 | tf_op jit(solution)/shard_map/reduce_sum | solution.py:16
  172.7 5.0 %all-to-all-start.2 = ((f32[4,64,832]{2,1,0:T(8,128)}), f32[4,64,832]{2,1,0:T(8,128)}, u32[]{:S(2)}, u32[]{:S(2)}) async-start(f32[4,64,832]{2,1,0:T(8,128)} %bitcast.14), calls=%async_computation.2 | async-start | bytes 1835008 | tf_op jit(solution)/shard_map/all_to_all | solution.py:16
  177.7 3.4 %fusion.4 = f32[512,512]{0,1:T(8,128)S(1)} fusion(f32[2,512,1024]{2,1,0:T(8,128)} %param.9, f32[512,512]{0,1:T(8,128)S(1)} %copy-done.4, f32[512,512]{0,1:T(8,128)S(1)} %copy-done.2), kind=kOutput, calls=%fused_computation.9 | convolution fusion | flops 1611137024 | bytes 5242880 | tf_op jit(solution)/shard_map/dot_general | solution.py:41
  181.1 0.0 copy-start.15
  181.2 5.3 %collective-permute-start.3 = (f32[256,256]{0,1:T(8,128)S(1)}, f32[256,256]{0,1:T(8,128)S(1)}, u32[]{:S(2)}, u32[]{:S(2)}) collective-permute-start(f32[256,256]{0,1:T(8,128)S(1)} %get-tuple-element.45), channel_id=1, source_target_pairs={{4,0},{8,4},{12,8},{16,12},{20,16},{24,20},{28,24},{32,28},{36,32}... | collective-permute-start | bytes 786440 | tf_op jit(solution)/shard_map/ppermute | solution.py:33
  186.5 3.0 %all-to-all-done.2 = f32[4,64,832]{2,1,0:T(8,128)} async-done(((f32[4,64,832]{2,1,0:T(8,128)}), f32[4,64,832]{2,1,0:T(8,128)}, u32[]{:S(2)}, u32[]{:S(2)}) %all-to-all-start.2) | async-done | bytes 852000 | tf_op jit(solution)/shard_map/all_to_all | solution.py:16
  189.5 1.9 reduce_sum.58
  191.5 9.0 %all-to-all-start.3 = ((f32[8,8,832]{2,1,0:T(8,128)}), f32[8,8,832]{2,1,0:T(8,128)S(1)}, u32[]{:S(2)}, u32[]{:S(2)}) async-start(f32[8,8,832]{2,1,0:T(8,128)} %bitcast.15), calls=%async_computation.3 | async-start | bytes 458752 | tf_op jit(solution)/shard_map/all_to_all | solution.py:16
  200.5 0.0 collective-permute-done.3
  200.5 0.1 fusion.37
  200.7 1.0 copy.146
  201.7 9.0 %all-to-all-done.3 = f32[8,8,832]{2,1,0:T(8,128)S(1)} async-done(((f32[8,8,832]{2,1,0:T(8,128)}), f32[8,8,832]{2,1,0:T(8,128)S(1)}, u32[]{:S(2)}, u32[]{:S(2)}) %all-to-all-start.3) | async-done | bytes 213024 | tf_op jit(solution)/shard_map/all_to_all | solution.py:16
  210.7 3.7 %all_to_all.35 = f32[2,4,832]{2,1,0:T(4,128)S(1)} all-to-all(f32[2,4,832]{2,1,0:T(4,128)S(1)} %all_to_all.26), channel_id=1, replica_groups=mesh['y'=4,'xl'=2,'z'=8,'xh'=2,'c'=2] {'c'}, dimensions={0} | all-to-all | bytes 53248 | tf_op jit(solution)/shard_map/all_to_all | solution.py:27
  214.5 0.1 mul.71
  214.6 0.6 slice.110
  215.2 0.6 slice.111
  215.8 0.6 reshape.37
  (46 shorter events, 0.2 us)
Async XLA Ops:
  0.6 5.3 %copy-start.24 = (f32[2,1024]{1,0:T(2,128)S(1)}, f32[2,1024]{1,0:T(2,128)}, u32[]{:S(2)}) copy-start(f32[2,1024]{1,0:T(2,128)} %param.10) | copy-start | bytes 24580
  0.6 5.3 %copy-start.17 = (f32[2,512,512]{2,1,0:T(8,128)S(1)}, f32[2,512,512]{2,1,0:T(8,128)}, u32[]{:S(2)}) copy-start(f32[2,512,512]{2,1,0:T(8,128)} %param.11) | copy-start | bytes 6291460
  2.1 14.0 %collective-permute-start = (f32[256,256]{0,1:T(8,128)S(1)}, f32[256,256]{0,1:T(8,128)S(1)}, u32[]{:S(2)}, u32[]{:S(2)}) collective-permute-start(f32[256,256]{0,1:T(8,128)S(1)} %get-tuple-element.46), channel_id=1, source_target_pairs={{0,4},{4,8},{8,12},{12,16},{16,20},{20,24},{24,28},{28,32},{32,36}... | collective-permute-start | bytes 786440 | tf_op jit(solution)/shard_map/ppermute | solution.py:33
  16.1 3.7 %copy-start.16 = (f32[256,256]{0,1:T(8,128)}, f32[256,256]{0,1:T(8,128)S(1)}, u32[]{:S(2)}) copy-start(f32[256,256]{0,1:T(8,128)S(1)} %collective-permute-done) | copy-start | bytes 786436
  19.8 1.3 copy-start.8
  19.8 3.2 %copy-start.20 = (f32[1,512,256]{2,1,0:T(8,128)S(1)}, f32[1,512,256]{2,1,0:T(8,128)}, u32[]{:S(2)}) copy-start(f32[1,512,256]{2,1,0:T(8,128)} %param.8) | copy-start | bytes 1572868
  19.8 4.2 %copy-start.21 = (f32[1,512,256]{2,1,0:T(8,128)S(1)}, f32[1,512,256]{2,1,0:T(8,128)}, u32[]{:S(2)}) copy-start(f32[1,512,256]{2,1,0:T(8,128)} %param.7) | copy-start | bytes 1572868
  21.1 17.1 %collective-permute-start.1 = (f32[512,256]{0,1:T(8,128)S(1)}, f32[512,256]{0,1:T(8,128)S(1)}, u32[]{:S(2)}, u32[]{:S(2)}) collective-permute-start(f32[512,256]{0,1:T(8,128)S(1)} %convolution_add_fusion), channel_id=1, source_target_pairs={{0,4},{4,8},{8,12},{12,16},{16,20},{20,24},{24,28},{28,32},{32,36}... | collective-permute-start | bytes 1572872 | tf_op jit(solution)/shard_map/ppermute | solution.py:33
  38.2 3.8 %copy-start.7 = (f32[512,256]{0,1:T(8,128)}, f32[512,256]{0,1:T(8,128)S(1)}, u32[]{:S(2)}) copy-start(f32[512,256]{0,1:T(8,128)S(1)} %collective-permute-done.1) | copy-start | bytes 1572868
  38.2 3.8 %copy-start.12 = (f32[1,512,256]{1,2,0:T(8,128)S(1)}, f32[1,512,256]{1,2,0:T(8,128)}, u32[]{:S(2)}) copy-start(f32[1,512,256]{1,2,0:T(8,128)} %copy.131) | copy-start | bytes 1572868
  38.2 3.9 %copy-start.18 = (f32[2,512,512]{2,1,0:T(8,128)S(1)}, f32[2,512,512]{2,1,0:T(8,128)}, u32[]{:S(2)}) copy-start(f32[2,512,512]{2,1,0:T(8,128)} %param.11) | copy-start | bytes 6291460
  38.2 3.9 %copy-start.22 = (f32[1,512,256]{1,2,0:T(8,128)S(1)}, f32[1,512,256]{1,2,0:T(8,128)}, u32[]{:S(2)}) copy-start(f32[1,512,256]{1,2,0:T(8,128)} %copy.132) | copy-start | bytes 1572868
  42.1 1.5 copy-start.10
  42.1 2.9 %copy-start = (f32[2,512,1024]{2,1,0:T(8,128)S(1)}, f32[2,512,1024]{2,1,0:T(8,128)}, u32[]{:S(2)}) copy-start(f32[2,512,1024]{2,1,0:T(8,128)} %param.9) | copy-start | bytes 12582916
  46.9 1.0 copy-start.5
  48.8 14.4 %collective-permute-start.2 = (f32[512,256]{0,1:T(8,128)}, f32[512,256]{0,1:T(8,128)}, u32[]{:S(2)}, u32[]{:S(2)}) collective-permute-start(f32[512,256]{0,1:T(8,128)} %slice.106), channel_id=1, source_target_pairs={{4,0},{8,4},{12,8},{16,12},{20,16},{24,20},{28,24},{32,28},{36,32}... | collective-permute-start | bytes 1572872 | tf_op jit(solution)/shard_map/ppermute | solution.py:33
  52.0 4.4 %copy-start.11 = (f32[512,1024]{0,1:T(8,128)S(1)}, f32[512,1024]{0,1:T(8,128)}, u32[]{:S(2)}) copy-start(f32[512,1024]{0,1:T(8,128)} %copy-done.10) | copy-start | bytes 6291460
  52.0 4.4 %copy-start.13 = (f32[1,512,256]{1,2,0:T(8,128)S(1)}, f32[1,512,256]{1,2,0:T(8,128)}, u32[]{:S(2)}) copy-start(f32[1,512,256]{1,2,0:T(8,128)} %copy.131) | copy-start | bytes 1572868
  52.0 4.4 %copy-start.23 = (f32[1,512,256]{1,2,0:T(8,128)S(1)}, f32[1,512,256]{1,2,0:T(8,128)}, u32[]{:S(2)}) copy-start(f32[1,512,256]{1,2,0:T(8,128)} %copy.132) | copy-start | bytes 1572868
  56.4 6.8 %copy-start.6 = (f32[512,512]{0,1:T(8,128)S(1)}, f32[512,512]{0,1:T(8,128)}, u32[]{:S(2)}) copy-start(f32[512,512]{0,1:T(8,128)} %copy-done.5) | copy-start | bytes 3145732
  56.4 7.9 %copy-start.19 = (f32[2,512,512]{2,1,0:T(8,128)S(1)}, f32[2,512,512]{2,1,0:T(8,128)}, u32[]{:S(2)}) copy-start(f32[2,512,512]{2,1,0:T(8,128)} %param.11) | copy-start | bytes 6291460
  58.7 5.7 %copy-start.9 = (f32[512,1024]{0,1:T(8,128)S(1)}, f32[512,1024]{0,1:T(8,128)}, u32[]{:S(2)}) copy-start(f32[512,1024]{0,1:T(8,128)} %copy-done.8) | copy-start | bytes 6291460
  64.4 1.4 copy-start.14
  65.8 4.5 %copy-start.1 = (f32[512,512]{0,1:T(8,128)}, f32[512,512]{0,1:T(8,128)S(1)}, u32[]{:S(2)}) copy-start(f32[512,512]{0,1:T(8,128)S(1)} %get-tuple-element.40) | copy-start | bytes 3145732
  65.8 4.5 %copy-start.3 = (f32[512,512]{0,1:T(8,128)}, f32[512,512]{0,1:T(8,128)S(1)}, u32[]{:S(2)}) copy-start(f32[512,512]{0,1:T(8,128)S(1)} %get-tuple-element.41) | copy-start | bytes 3145732
  170.1 7.6 %copy-start.2 = (f32[512,512]{0,1:T(8,128)S(1)}, f32[512,512]{0,1:T(8,128)}, u32[]{:S(2)}) copy-start(f32[512,512]{0,1:T(8,128)} %copy-done.1) | copy-start | bytes 3145732
  170.1 7.6 %copy-start.4 = (f32[512,512]{0,1:T(8,128)S(1)}, f32[512,512]{0,1:T(8,128)}, u32[]{:S(2)}) copy-start(f32[512,512]{0,1:T(8,128)} %copy-done.3) | copy-start | bytes 3145732
  172.7 16.9 %all-to-all-start.2 = ((f32[4,64,832]{2,1,0:T(8,128)}), f32[4,64,832]{2,1,0:T(8,128)}, u32[]{:S(2)}, u32[]{:S(2)}) async-start(f32[4,64,832]{2,1,0:T(8,128)} %bitcast.14), calls=%async_computation.2 | async-start | bytes 1835008 | tf_op jit(solution)/shard_map/all_to_all | solution.py:16
  181.1 19.4 %copy-start.15 = (f32[512,256]{0,1:T(8,128)S(1)}, f32[512,256]{0,1:T(8,128)}, u32[]{:S(2)}) copy-start(f32[512,256]{0,1:T(8,128)} %copy-done.14) | copy-start | bytes 1572868
  181.2 19.4 %collective-permute-start.3 = (f32[256,256]{0,1:T(8,128)S(1)}, f32[256,256]{0,1:T(8,128)S(1)}, u32[]{:S(2)}, u32[]{:S(2)}) collective-permute-start(f32[256,256]{0,1:T(8,128)S(1)} %get-tuple-element.45), channel_id=1, source_target_pairs={{4,0},{8,4},{12,8},{16,12},{20,16},{24,20},{28,24},{32,28},{36,32}... | collective-permute-start | bytes 786440 | tf_op jit(solution)/shard_map/ppermute | solution.py:33
  191.5 19.2 %all-to-all-start.3 = ((f32[8,8,832]{2,1,0:T(8,128)}), f32[8,8,832]{2,1,0:T(8,128)S(1)}, u32[]{:S(2)}, u32[]{:S(2)}) async-start(f32[8,8,832]{2,1,0:T(8,128)} %bitcast.15), calls=%async_computation.3 | async-start | bytes 458752 | tf_op jit(solution)/shard_map/all_to_all | solution.py:16

commit v3 on v1

--- a/solution.py
+++ b/solution.py
@@ -47,7 +47,8 @@
 
 def layer_forward_step(earlier, values, weight, bias):
     joined = jnp.concatenate([earlier, values], axis=1)
-    mixed = matmul(joined, weight) + bias
+    taps = earlier.shape[1]
+    mixed = matmul(values, weight[taps:]) + matmul(earlier, weight[:taps]) + bias
     width = weight.shape[1] // 2
     tanh_part = jnp.tanh(mixed[:, :width])
     sigm_part = jax.nn.sigmoid(mixed[:, width:])
@@ -59,7 +60,8 @@
 ):
     channels = carried_state.shape[1]
     outer = jnp.concatenate([carried_state, skip_cotangent_rows], axis=1)
-    dhidden = contract(outer, out_w, 1, 1)
+    dhidden = contract(skip_cotangent_rows, out_w[:, channels:], 1, 1)
+    dhidden = dhidden + contract(carried_state, out_w[:, :channels], 1, 1)
     dfilter = dhidden * sigm_part * (1.0 - tanh_part * tanh_part)
     dgate = dhidden * tanh_part * sigm_part * (1.0 - sigm_part)
     dmixed = jnp.concatenate([dfilter, dgate], axis=1)

time: 201 us -> 198 us (0.985)
  waiting for transfers between devices: 38.5 us -> 32.7 us
  other arithmetic: 16.6 us -> 18.9 us
    ppermute x4, waiting for transfers between devices: 27.8 us -> 21.2 us  [from_behind(): return lax.ppermute(block, axis, route)]
    dot_general x8 -> x10, matrix products: 18.9 us -> 21.6 us  [contract(): lax.dot_general(left, right, (((left_dim,), (right_dim,)), ((), ())), pre...]
    concatenate x1, other arithmetic: 5.58 us -> 7.65 us  [local(): packed = jnp.concatenate([conv_terms, out_terms, bias_cols], axis=1)]
    dot_general x3 -> x5, matrix products: 8.42 us -> 6.98 us  [matmul(): jnp.dot(left, right, precision=lax.Precision.HIGH, preferred_element_type...]
    unnamed x62 -> x64, local copies, waits for them, and re-layouts: 7.31 us -> 7.59 us
  transfers between devices with their start and end apart: 6 -> 6, of which waited for: 5 -> 4; matrix products, arithmetic and copies ran while one was open for 8% -> 12% of each run, Pallas kernels for 0% -> 0%
where the time goes in v3:
time: 198 us; the launch traced here: 197 us
  blocking collectives  55.8 us (28%)
  local copies, waits for them, and re-layouts  34.5 us (17%)
  waiting for transfers between devices  32.7 us (17%)
  matrix products  28.6 us (14%)
  starting transfers between devices  25.8 us (13%)
  other arithmetic  18.9 us (10%)
    all_to_all x2, blocking collectives, reduce_rows(): return lax.all_to_all(block, axis, 0, 0, tiled=True).sum(axis=0)  55.8 us
    dot_general x10, matrix products, contract(): lax.dot_general(left, right, (((left_dim,), (right_dim,)), ((), ())), pre...  21.6 us
    ppermute x4, waiting for transfers between devices, from_behind(): return lax.ppermute(block, axis, route)  21.2 us
    reshape x2, local copies, waits for them, and re-layouts, reduce_to_owner(): packed.reshape(*sizes, -1, width).transpose(4, 3, 1, 0, 2, 5, 6)  17.8 us
    all_to_all x2, starting transfers between devices, reduce_rows(): return lax.all_to_all(block, axis, 0, 0, tiled=True).sum(axis=0)  13.3 us
    ppermute x4, starting transfers between devices, from_behind(): return lax.ppermute(block, axis, route)  12.5 us
    all_to_all x2, waiting for transfers between devices, reduce_rows(): return lax.all_to_all(block, axis, 0, 0, tiled=True).sum(axis=0)  11.5 us
    reduce_sum x4, other arithmetic, reduce_rows(): return lax.all_to_all(block, axis, 0, 0, tiled=True).sum(axis=0)  8.28 us
  transfers between devices with their start and end apart: 6, of which 4 were waited for; matrix products, arithmetic and copies ran while one was open for 12% of the time, Pallas kernels for 0%

profile of v3, /device:TPU:10, one launch (start us, length us, event | category | flops | bytes accessed | tf_op | source)
XLA Modules:
  0.0 197.3 jit_solution(9696399669007925038)
XLA Ops:
  0.6 0.0 copy-start.14
  0.6 1.3 copy.89
  2.0 0.0 copy-start.15
  2.0 4.0 %collective-permute-start = (f32[256,256]{0,1:T(8,128)S(1)}, f32[256,256]{0,1:T(8,128)S(1)}, u32[]{:S(2)}, u32[]{:S(2)}) collective-permute-start(f32[256,256]{0,1:T(8,128)S(1)} %get-tuple-element.36), channel_id=1, source_target_pairs={{0,4},{4,8},{8,12},{12,16},{16,20},{20,24},{24,28},{28,32},{32,36}... | collective-permute-start | bytes 786440 | tf_op jit(solution)/shard_map/ppermute | solution.py:31
  6.0 0.0 copy-start.29
  6.0 2.3 %fusion.32 = f32[512,1024]{0,1:T(8,128)S(1)} fusion(f32[2,512,1024]{2,1,0:T(8,128)} %param.9, f32[1,512,256]{2,1,0:T(8,128)S(1)} %copy-done.14), kind=kOutput, calls=%fused_computation.46 | convolution fusion | flops 805306368 | bytes 3670016 | tf_op jit(solution)/shard_map/dot_general | solution.py:35
  8.3 0.0 copy-start
  8.3 0.2 slice_bitcast_fusion
  8.5 7.7 %collective-permute-done = f32[256,256]{0,1:T(8,128)S(1)} collective-permute-done((f32[256,256]{0,1:T(8,128)S(1)}, f32[256,256]{0,1:T(8,128)S(1)}, u32[]{:S(2)}, u32[]{:S(2)}) %collective-permute-start) | collective-permute-done | bytes 262176 | tf_op jit(solution)/shard_map/ppermute | solution.py:31
  16.2 0.0 copy-done
  16.2 1.4 add_add_fusion.1
  17.6 0.0 copy-start.6
  17.6 0.9 convolution_add_fusion.2
  18.5 0.4 copy-done.16
  18.9 1.9 collective-permute-start.1
  20.8 0.6 fusion.46
  21.4 1.0 fusion.29
  22.5 13.5 %collective-permute-done.1 = f32[512,256]{0,1:T(8,128)S(1)} collective-permute-done((f32[512,256]{0,1:T(8,128)S(1)}, f32[512,256]{0,1:T(8,128)S(1)}, u32[]{:S(2)}, u32[]{:S(2)}) %collective-permute-start.1) | collective-permute-done | bytes 524320 | tf_op jit(solution)/shard_map/ppermute | solution.py:31
  36.0 1.4 add_add_fusion
  37.4 1.1 subtract_multiply_fusion.3
  38.5 0.3 copy-done.18
  38.8 1.9 fusion.2
  40.7 1.1 copy-done.7
  41.7 0.8 slice.157
  42.6 2.1 %collective-permute-start.2 = (f32[512,256]{0,1:T(8,128)}, f32[512,256]{0,1:T(8,128)}, u32[]{:S(2)}, u32[]{:S(2)}) collective-permute-start(f32[512,256]{0,1:T(8,128)} %slice.157), channel_id=1, source_target_pairs={{4,0},{8,4},{12,8},{16,12},{20,16},{24,20},{28,24},{32,28},{36,32}... | collective-permute-start | bytes 1572872 | tf_op jit(solution)/shard_map/ppermute | solution.py:31
  44.7 1.7 fusion.42
  46.4 2.1 %copy.87 = f32[1,512,256]{1,2,0:T(8,128)} copy(f32[1,512,256]{2,1,0:T(8,128)} %param.7) | data formatting | bytes 1048576 | tf_op args[1]
  48.4 1.0 copy.88
  49.4 0.2 fusion.8
  49.6 0.9 concatenate.52
  50.6 4.3 %fusion.9 = f32[512,1024]{1,0:T(8,128)} fusion(f32[512,512]{0,1:T(8,128)S(1)} %get-tuple-element.31, f32[512,512]{0,1:T(8,128)S(1)} %get-tuple-element.30, f32[512,256]{0,1:T(8,128)S(1)} %copy-done.12, f32[512,256]{0,1:T(8,128)} %copy-done.13), kind=kOutput, calls=%fused_computation.16 | convolution fusion | flops 1611399168 | bytes 5242880 | tf_op jit(solution)/shard_map/dot_general | solution.py:39
  54.9 2.3 %fusion.11 = f32[512,512]{1,0:T(8,128)} fusion(f32[512,256]{0,1:T(8,128)S(1)} %bitcast.61, f32[512,256]{0,1:T(8,128)S(1)} %bitcast.60, f32[512,1024]{0,1:T(8,128)S(1)} %copy-done.19), kind=kOutput, calls=%fused_computation.21 | convolution fusion | flops 806617088 | bytes 4194304 | tf_op jit(solution)/shard_map/dot_general | solution.py:39
  57.2 0.0 collective-permute-done.2
  57.2 1.3 fusion.44
  58.5 0.4 copy-done.17
  58.9 2.2 %fusion.10 = f32[512,512]{1,0:T(8,128)} fusion(f32[512,256]{0,1:T(8,128)S(1)} %bitcast.62, f32[512,256]{0,1:T(8,128)S(1)} %fusion.44, f32[512,1024]{0,1:T(8,128)S(1)} %copy-done.17), kind=kOutput, calls=%fused_computation.20 | convolution fusion | flops 806617088 | bytes 4194304 | tf_op jit(solution)/shard_map/dot_general | solution.py:39
  61.2 1.0 subtract_multiply_fusion.1
  62.3 0.2 fusion.6
  62.5 1.2 concatenate.51
  63.6 1.1 select_maximum_fusion
  64.8 3.0 %fusion.7 = f32[512,1024]{1,0:T(8,128)S(1)} fusion(f32[512,512]{0,1:T(8,128)S(1)} %get-tuple-element.29, f32[512,512]{0,1:T(8,128)S(1)} %get-tuple-element.28, f32[512,256]{0,1:T(8,128)S(1)} %bitcast.59, f32[256,256]{0,1:T(8,128)S(1)} %get-tuple-element.37, f32[256,256]{0,1:T(8,128)} %copy-done.23), kind=kOutput, calls=%fused_computation.14 | convolution fusion | flops 1611661312 | bytes 5242880 | tf_op jit(solution)/shard_map/dot_general | solution.py:39
  67.8 7.6 %pad_maximum_fusion = f32[1024,1664]{1,0:T(8,128)} fusion(f32[1024,128]{1,0:T(8,128)S(1)} %select_maximum_fusion, f32[512,512]{1,0:T(8,128)S(1)} %copy-done.25, f32[512,512]{1,0:T(8,128)S(1)} %copy-done.26, f32[512,1024]{1,0:T(8,128)S(1)} %copy-done.5, f32[512,1024]{1,0:T(8,128)S(1)} %fusion.7), kind=kLoop, calls=%fused_computation | loop fusion | flops 6815744 | bytes 13631488 | tf_op jit(solution)/shard_map/concatenate | solution.py:123
  75.5 8.5 %reshape.32 = f32[4,2,8,2,2,4,1664]{6,5,4,3,2,1,0:T(4,128)} reshape(f32[1024,1664]{1,0:T(8,128)} %pad_maximum_fusion) | data formatting | bytes 13631488 | tf_op jit(solution)/shard_map/reshape | solution.py:22
  83.9 9.3 %copy.99 = f32[4,2,8,2,2,4,1664]{6,4,5,2,0,1,3:T(2,128)} copy(f32[4,2,8,2,2,4,1664]{6,5,4,3,2,1,0:T(4,128)} %reshape.32) | data formatting | bytes 13631488 | tf_op jit(solution)/shard_map/reshape | solution.py:22
  93.3 3.4 %copy.100 = f32[2,512,1664]{2,1,0:T(8,128)S(1)} copy(f32[2,512,1664]{2,0,1:T(2,128)} %bitcast.57) | data formatting | bytes 13631488 | tf_op jit(solution)/shard_map/reshape;reshape | solution.py:15
  96.6 10.4 %all_to_all.20 = f32[2,512,1664]{2,1,0:T(8,128)} all-to-all(f32[2,512,1664]{2,1,0:T(8,128)S(1)} %copy.100), channel_id=1, replica_groups=mesh['y'=4,'xl'=2,'z'=8,'xh'=2,'c'=2] {'c'}, dimensions={0} | all-to-all | bytes 13631488 | tf_op jit(solution)/shard_map/all_to_all | solution.py:16
  107.1 3.7 %reduce_sum.56 = f32[512,1664]{1,0:T(8,128)S(1)} reduce(f32[2,512,1664]{2,1,0:T(8,128)} %all_to_all.20, f32[]{:T(128)} %constant.1.clone.1), dimensions={0}, to_apply=%region_2.3 | reduce | flops 851968 | bytes 10223620 | tf_op jit(solution)/shard_map/reduce_sum | solution.py:16
  110.8 45.4 %all_to_all.21 = f32[4,128,1664]{2,1,0:T(8,128)} all-to-all(f32[4,128,1664]{2,1,0:T(8,128)S(1)} %bitcast.58), channel_id=1, replica_groups=mesh['y'=4,'xl'=2,'z'=8,'xh'=2,'c'=2] {'xh','xl'}, dimensions={0} | all-to-all | bytes 6815744 | tf_op jit(solution)/shard_map/all_to_all | solution.py:16
  156.2 3.3 %reduce_sum.57 = f32[128,1664]{1,0:T(8,128)} reduce(f32[4,128,1664]{2,1,0:T(8,128)} %all_to_all.21, f32[]{:T(128)} %constant.1.clone.1), dimensions={0}, to_apply=%region_3.4 | reduce | flops 638976 | bytes 4259844 | tf_op jit(solution)/shard_map/reduce_sum | solution.py:16
  159.5 5.0 %all-to-all-start.2 = ((f32[4,32,1664]{2,1,0:T(8,128)}), f32[4,32,1664]{2,1,0:T(8,128)}, u32[]{:S(2)}, u32[]{:S(2)}) async-start(f32[4,32,1664]{2,1,0:T(8,128)} %bitcast.19), calls=%async_computation.2 | async-start | bytes 1703936 | tf_op jit(solution)/shard_map/all_to_all | solution.py:16
  164.5 3.4 %fusion = f32[512,512]{0,1:T(8,128)S(1)} fusion(f32[2,512,1024]{2,1,0:T(8,128)} %param.9, f32[512,512]{0,1:T(8,128)S(1)} %copy-done.4, f32[512,512]{0,1:T(8,128)S(1)} %copy-done.2), kind=kOutput, calls=%fused_computation.3 | convolution fusion | flops 1611137024 | bytes 5242880 | tf_op jit(solution)/shard_map/dot_general | solution.py:39
  167.9 0.0 copy-start.22
  168.0 4.6 %collective-permute-start.3 = (f32[256,256]{0,1:T(8,128)S(1)}, f32[256,256]{0,1:T(8,128)S(1)}, u32[]{:S(2)}, u32[]{:S(2)}) collective-permute-start(f32[256,256]{0,1:T(8,128)S(1)} %get-tuple-element.35), channel_id=1, source_target_pairs={{4,0},{8,4},{12,8},{16,12},{20,16},{24,20},{28,24},{32,28},{36,32}... | collective-permute-start | bytes 786440 | tf_op jit(solution)/shard_map/ppermute | solution.py:31
  172.6 2.7 %all-to-all-done.2 = f32[4,32,1664]{2,1,0:T(8,128)} async-done(((f32[4,32,1664]{2,1,0:T(8,128)}), f32[4,32,1664]{2,1,0:T(8,128)}, u32[]{:S(2)}, u32[]{:S(2)}) %all-to-all-start.2) | async-done | bytes 852000 | tf_op jit(solution)/shard_map/all_to_all | solution.py:16
  175.3 1.2 reduce_sum.58
  176.5 0.7 reshape.35
  177.2 8.3 %all-to-all-start.3 = ((f32[8,4,1664]{2,1,0:T(4,128)}), f32[8,4,1664]{2,1,0:T(4,128)S(1)}, u32[]{:S(2)}, u32[]{:S(2)}) async-start(f32[8,4,1664]{2,1,0:T(4,128)} %reshape.35), calls=%async_computation.3 | async-start | bytes 425984 | tf_op jit(solution)/shard_map/all_to_all | solution.py:16
  185.5 0.0 collective-permute-done.3
  185.5 0.1 fusion.41
  185.6 1.0 copy.102
  186.6 8.8 %all-to-all-done.3 = f32[8,4,1664]{2,1,0:T(4,128)S(1)} async-done(((f32[8,4,1664]{2,1,0:T(4,128)}), f32[8,4,1664]{2,1,0:T(4,128)S(1)}, u32[]{:S(2)}, u32[]{:S(2)}) %all-to-all-start.3) | async-done | bytes 213024 | tf_op jit(solution)/shard_map/all_to_all | solution.py:16
  195.5 0.6 slice.162
  196.1 0.6 slice.163
  196.7 0.6 reshape.36
  (55 shorter events, 0.2 us)
Async XLA Ops:
  0.6 5.3 %copy-start.14 = (f32[1,512,256]{2,1,0:T(8,128)S(1)}, f32[1,512,256]{2,1,0:T(8,128)}, u32[]{:S(2)}) copy-start(f32[1,512,256]{2,1,0:T(8,128)} %param.6) | copy-start | bytes 1572868
  2.0 6.3 %copy-start.15 = (f32[2,512,512]{2,1,0:T(8,128)S(1)}, f32[2,512,512]{2,1,0:T(8,128)}, u32[]{:S(2)}) copy-start(f32[2,512,512]{2,1,0:T(8,128)} %param.11) | copy-start | bytes 6291460
  2.0 14.2 %collective-permute-start = (f32[256,256]{0,1:T(8,128)S(1)}, f32[256,256]{0,1:T(8,128)S(1)}, u32[]{:S(2)}, u32[]{:S(2)}) collective-permute-start(f32[256,256]{0,1:T(8,128)S(1)} %get-tuple-element.36), channel_id=1, source_target_pairs={{0,4},{4,8},{8,12},{12,16},{16,20},{20,24},{24,28},{28,32},{32,36}... | collective-permute-start | bytes 786440 | tf_op jit(solution)/shard_map/ppermute | solution.py:31
  6.0 2.5 %copy-start.29 = (f32[2,1024]{1,0:T(2,128)S(1)}, f32[2,1024]{1,0:T(2,128)}, u32[]{:S(2)}) copy-start(f32[2,1024]{1,0:T(2,128)} %param.10) | copy-start | bytes 24580
  8.3 7.9 %copy-start = (f32[2,512,1024]{2,1,0:T(8,128)S(1)}, f32[2,512,1024]{2,1,0:T(8,128)}, u32[]{:S(2)}) copy-start(f32[2,512,1024]{2,1,0:T(8,128)} %param.9) | copy-start | bytes 12582916
  8.5 36.2 %copy-start.9 = (f32[512,512]{1,0:T(8,128)}, f32[512,512]{1,0:T(8,128)S(1)}, u32[]{:S(2)}) copy-start(f32[512,512]{1,0:T(8,128)S(1)} %get-tuple-element.32) | copy-start | bytes 3145732
  16.2 1.4 copy-start.23
  17.6 1.3 copy-start.16
  17.6 3.2 %copy-start.6 = (f32[1,512,256]{2,1,0:T(8,128)S(1)}, f32[1,512,256]{2,1,0:T(8,128)}, u32[]{:S(2)}) copy-start(f32[1,512,256]{2,1,0:T(8,128)} %param.8) | copy-start | bytes 1572868
  18.9 3.6 %copy-start.11 = (f32[512,256]{0,1:T(8,128)}, f32[512,256]{0,1:T(8,128)S(1)}, u32[]{:S(2)}) copy-start(f32[512,256]{0,1:T(8,128)S(1)} %convolution_add_fusion.2) | copy-start | bytes 1572868
  18.9 17.1 %collective-permute-start.1 = (f32[512,256]{0,1:T(8,128)S(1)}, f32[512,256]{0,1:T(8,128)S(1)}, u32[]{:S(2)}, u32[]{:S(2)}) collective-permute-start(f32[512,256]{0,1:T(8,128)S(1)} %convolution_add_fusion.2), channel_id=1, source_target_pairs={{0,4},{4,8},{8,12},{12,16},{16,20},{20,24},{24,28},{28,32},{32,36}... | collective-permute-start | bytes 1572872 | tf_op jit(solution)/shard_map/ppermute | solution.py:31
  36.0 1.4 copy-start.13
  36.0 1.4 copy-start.27
  37.4 1.4 copy-start.18
  40.6 1.1 copy-start.7
  42.6 14.6 %collective-permute-start.2 = (f32[512,256]{0,1:T(8,128)}, f32[512,256]{0,1:T(8,128)}, u32[]{:S(2)}, u32[]{:S(2)}) collective-permute-start(f32[512,256]{0,1:T(8,128)} %slice.157), channel_id=1, source_target_pairs={{4,0},{8,4},{12,8},{16,12},{20,16},{24,20},{28,24},{32,28},{36,32}... | collective-permute-start | bytes 1572872 | tf_op jit(solution)/shard_map/ppermute | solution.py:31
  49.4 1.1 copy-start.12
  50.6 4.4 %copy-start.19 = (f32[512,1024]{0,1:T(8,128)S(1)}, f32[512,1024]{0,1:T(8,128)}, u32[]{:S(2)}) copy-start(f32[512,1024]{0,1:T(8,128)} %copy-done.18) | copy-start | bytes 6291460
  50.6 4.4 %copy-start.20 = (f32[1,512,256]{1,2,0:T(8,128)S(1)}, f32[1,512,256]{1,2,0:T(8,128)}, u32[]{:S(2)}) copy-start(f32[1,512,256]{1,2,0:T(8,128)} %copy.87) | copy-start | bytes 1572868
  50.6 4.4 %copy-start.28 = (f32[1,512,256]{1,2,0:T(8,128)S(1)}, f32[1,512,256]{1,2,0:T(8,128)}, u32[]{:S(2)}) copy-start(f32[1,512,256]{1,2,0:T(8,128)} %copy.88) | copy-start | bytes 1572868
  54.9 2.3 %copy-start.8 = (f32[512,512]{0,1:T(8,128)S(1)}, f32[512,512]{0,1:T(8,128)}, u32[]{:S(2)}) copy-start(f32[512,512]{0,1:T(8,128)} %copy-done.7) | copy-start | bytes 3145732
  57.2 1.7 copy-start.17
  58.9 2.3 %copy-start.21 = (f32[512,256]{0,1:T(8,128)}, f32[512,256]{0,1:T(8,128)S(1)}, u32[]{:S(2)}) copy-start(f32[512,256]{0,1:T(8,128)S(1)} %fusion.44) | copy-start | bytes 1572868
  58.9 2.3 %copy-start.10 = (f32[512,512]{1,0:T(8,128)S(1)}, f32[512,512]{1,0:T(8,128)}, u32[]{:S(2)}) copy-start(f32[512,512]{1,0:T(8,128)} %copy-done.9) | copy-start | bytes 3145732
  58.9 2.3 %copy-start.24 = (f32[512,512]{0,1:T(8,128)S(1)}, f32[512,512]{0,1:T(8,128)}, u32[]{:S(2)}) copy-start(f32[512,512]{0,1:T(8,128)} %fusion.42) | copy-start | bytes 3145732
  62.3 5.5 %copy-start.1 = (f32[512,512]{0,1:T(8,128)}, f32[512,512]{0,1:T(8,128)S(1)}, u32[]{:S(2)}) copy-start(f32[512,512]{0,1:T(8,128)S(1)} %get-tuple-element.28) | copy-start | bytes 3145732
  62.3 5.5 %copy-start.3 = (f32[512,512]{0,1:T(8,128)}, f32[512,512]{0,1:T(8,128)S(1)}, u32[]{:S(2)}) copy-start(f32[512,512]{0,1:T(8,128)S(1)} %get-tuple-element.29) | copy-start | bytes 3145732
  64.7 3.0 %copy-start.5 = (f32[512,1024]{1,0:T(8,128)S(1)}, f32[512,1024]{1,0:T(8,128)}, u32[]{:S(2)}) copy-start(f32[512,1024]{1,0:T(8,128)} %fusion.9) | copy-start | bytes 6291460
  64.7 3.0 %copy-start.25 = (f32[512,512]{1,0:T(8,128)S(1)}, f32[512,512]{1,0:T(8,128)}, u32[]{:S(2)}) copy-start(f32[512,512]{1,0:T(8,128)} %fusion.11) | copy-start | bytes 3145732
  64.8 3.0 %copy-start.26 = (f32[512,512]{1,0:T(8,128)S(1)}, f32[512,512]{1,0:T(8,128)}, u32[]{:S(2)}) copy-start(f32[512,512]{1,0:T(8,128)} %fusion.10) | copy-start | bytes 3145732
  156.2 8.3 %copy-start.2 = (f32[512,512]{0,1:T(8,128)S(1)}, f32[512,512]{0,1:T(8,128)}, u32[]{:S(2)}) copy-start(f32[512,512]{0,1:T(8,128)} %copy-done.1) | copy-start | bytes 3145732
  156.2 8.3 %copy-start.4 = (f32[512,512]{0,1:T(8,128)S(1)}, f32[512,512]{0,1:T(8,128)}, u32[]{:S(2)}) copy-start(f32[512,512]{0,1:T(8,128)} %copy-done.3) | copy-start | bytes 3145732
  159.5 15.8 %all-to-all-start.2 = ((f32[4,32,1664]{2,1,0:T(8,128)}), f32[4,32,1664]{2,1,0:T(8,128)}, u32[]{:S(2)}, u32[]{:S(2)}) async-start(f32[4,32,1664]{2,1,0:T(8,128)} %bitcast.19), calls=%async_computation.2 | async-start | bytes 1703936 | tf_op jit(solution)/shard_map/all_to_all | solution.py:16
  167.9 17.6 %copy-start.22 = (f32[512,256]{0,1:T(8,128)S(1)}, f32[512,256]{0,1:T(8,128)}, u32[]{:S(2)}) copy-start(f32[512,256]{0,1:T(8,128)} %copy-done.21) | copy-start | bytes 1572868
  168.0 17.5 %collective-permute-start.3 = (f32[256,256]{0,1:T(8,128)S(1)}, f32[256,256]{0,1:T(8,128)S(1)}, u32[]{:S(2)}, u32[]{:S(2)}) collective-permute-start(f32[256,256]{0,1:T(8,128)S(1)} %get-tuple-element.35), channel_id=1, source_target_pairs={{4,0},{8,4},{12,8},{16,12},{20,16},{24,20},{28,24},{32,28},{36,32}... | collective-permute-start | bytes 786440 | tf_op jit(solution)/shard_map/ppermute | solution.py:31
  177.2 18.2 %all-to-all-start.3 = ((f32[8,4,1664]{2,1,0:T(4,128)}), f32[8,4,1664]{2,1,0:T(4,128)S(1)}, u32[]{:S(2)}, u32[]{:S(2)}) async-start(f32[8,4,1664]{2,1,0:T(4,128)} %reshape.35), calls=%async_computation.3 | async-start | bytes 425984 | tf_op jit(solution)/shard_map/all_to_all | solution.py:16

commit v4 on v3

--- a/solution.py
+++ b/solution.py
@@ -17,12 +17,16 @@
 
 
 def reduce_to_owner(packed):
-    rows, width = packed.shape
-    sizes = [lax.axis_size(a) for a in ("y", "xl", "z", "xh", "c")]
-    block = packed.reshape(*sizes, -1, width).transpose(4, 3, 1, 0, 2, 5, 6).reshape(rows, width)
     for axis in ("c", ("xh", "xl"), "y", "z"):
-        block = reduce_rows(block, axis)
-    return block
+        packed = reduce_rows(packed, axis)
+    return packed
+
+
+def owner_order(block):
+    sizes = [lax.axis_size(a) for a in ("xl", "z", "xh", "c")]
+    rows, channels = block.shape
+    block = block.reshape(rows, 2, *sizes, -1).transpose(0, 5, 4, 2, 1, 3, 6)
+    return block.reshape(rows, channels)
 
 
 def from_behind(block, axis, distance):
@@ -65,8 +69,8 @@
     dfilter = dhidden * sigm_part * (1.0 - tanh_part * tanh_part)
     dgate = dhidden * tanh_part * sigm_part * (1.0 - sigm_part)
     dmixed = jnp.concatenate([dfilter, dgate], axis=1)
-    out_t = contract(outer, hidden, 0, 0)
-    conv_g = contract(joined, dmixed, 0, 0)
+    out_t = contract(owner_order(outer), hidden, 0, 0)
+    conv_g = contract(owner_order(joined), dmixed, 0, 0)
     bias_g = jnp.sum(dmixed, axis=0)
     back = contract(dmixed, weight, 1, 1)
     return (back[:, :channels], back[:, channels:], conv_g, out_t, bias_g)
@@ -115,9 +119,18 @@
     input_grad = carried_state + local1 + jnp.concatenate([past1[half:], rim_rows], axis=0)
     devices = lax.axis_size(SEQ_AXES + DP_AXES)
     factor = 1.0 / math.sqrt(rows * devices)
-    conv_terms = jnp.concatenate([first_conv_output, second_conv_output], axis=0)
-    out_terms = jnp.concatenate([first_output, second_output], axis=0)
+    groups = lax.axis_size(("c", "xh", "xl"))
+
+    def interleave(first, second):
+        both = jnp.stack([first.reshape(groups, -1, first.shape[1]), second.reshape(groups, -1, second.shape[1])], axis=1)
+        return both.reshape(-1, first.shape[1])
+
+    conv_terms = interleave(first_conv_output, second_conv_output)
+    out_terms = interleave(first_output, second_output)
     bias_terms = jnp.concatenate([first_bias, second_bias], axis=0)
+    bias_per_row = bias_terms.shape[0] // conv_terms.shape[0]
+    sizes = [lax.axis_size(a) for a in ("y", "xl", "z", "xh", "c")]
+    bias_terms = bias_terms.reshape(*sizes, -1).transpose(4, 3, 1, 0, 2, 5)
     bias_cols = bias_terms.reshape(conv_terms.shape[0], -1)
     bias_cols = jnp.pad(bias_cols, ((0, 0), (0, 128 - bias_cols.shape[1])))
     packed = jnp.concatenate([conv_terms, out_terms, bias_cols], axis=1)
@@ -125,7 +138,7 @@
     conv_width, out_width = conv_terms.shape[1], out_terms.shape[1]
     conv_grad = summed[:, :conv_width]
     out_grad = summed[:, conv_width : conv_width + out_width]
-    bias_grad = summed[:, conv_width + out_width : conv_width + out_width + bias_terms.shape[0] // conv_terms.shape[0]]
+    bias_grad = summed[:, conv_width + out_width : conv_width + out_width + bias_per_row]
     bias_grad = bias_grad.reshape(-1)
     return (input_grad[None], conv_grad, out_grad, bias_grad)
 

time: 198 us -> 202 us (1.020)
  waiting for transfers between devices: 32.7 us -> 18.8 us
  matrix products: 28.6 us -> 36.8 us
  starting transfers between devices: 25.8 us -> 32.3 us
  local copies, waits for them, and re-layouts: 34.5 us -> 40.8 us
  other arithmetic: 18.9 us -> 15.7 us
    ppermute x4, waiting for transfers between devices: 21.2 us -> 8.76 us  [from_behind(): return lax.ppermute(block, axis, route)]
    concatenate x1, other arithmetic: 7.65 us -> 0.54 us  [local(): packed = jnp.concatenate([conv_terms, out_terms, bias_cols], axis=1)]
    reshape x2 -> x7, local copies, waits for them, and re-layouts: 17.8 us -> 11.9 us  [the longest x4 7.18 us: owner_order(): return block.reshape(rows, channels)]
    unnamed x64 -> x68, local copies, waits for them, and re-layouts: 7.59 us -> 12.8 us
    ppermute x4, starting transfers between devices: 12.5 us -> 17.6 us  [from_behind(): return lax.ppermute(block, axis, route)]
    concatenate x0 -> x4, local copies, waits for them, and re-layouts: none -> 4.32 us  [the longest x1 2.04 us: layer_forward_step(): joined = jnp.concatenate([earlier, values], axis=1)]
    dot_general x10, matrix products: 21.6 us -> 25.9 us  [contract(): lax.dot_general(left, right, (((left_dim,), (right_dim,)), ((), ())), pre...]
    dot_general x5, matrix products: 6.98 us -> 10.9 us  [matmul(): jnp.dot(left, right, precision=lax.Precision.HIGH, preferred_element_type...]
  transfers between devices with their start and end apart: 6 -> 6, of which waited for: 4 -> 3; matrix products, arithmetic and copies ran while one was open for 12% -> 20% of each run, Pallas kernels for 0% -> 0%
where the time goes in v4:
time: 202 us; the launch traced here: 201 us
  blocking collectives  54.9 us (27%)
  local copies, waits for them, and re-layouts  40.8 us (20%)
  matrix products  36.8 us (18%)
  starting transfers between devices  32.3 us (16%)
  waiting for transfers between devices  18.8 us (9%)
  other arithmetic  15.7 us (8%)
    all_to_all x2, blocking collectives, reduce_rows(): return lax.all_to_all(block, axis, 0, 0, tiled=True).sum(axis=0)  54.9 us
    dot_general x10, matrix products, contract(): lax.dot_general(left, right, (((left_dim,), (right_dim,)), ((), ())), pre...  25.9 us
    ppermute x4, starting transfers between devices, from_behind(): return lax.ppermute(block, axis, route)  17.6 us
    all_to_all x2, starting transfers between devices, reduce_rows(): return lax.all_to_all(block, axis, 0, 0, tiled=True).sum(axis=0)  14.7 us
    unnamed x68, local copies, waits for them, and re-layouts  12.8 us
    dot_general x5, matrix products, matmul(): jnp.dot(left, right, precision=lax.Precision.HIGH, preferred_element_type...  10.9 us
    all_to_all x2, waiting for transfers between devices, reduce_rows(): return lax.all_to_all(block, axis, 0, 0, tiled=True).sum(axis=0)  10 us
    ppermute x4, waiting for transfers between devices, from_behind(): return lax.ppermute(block, axis, route)  8.76 us
  transfers between devices with their start and end apart: 6, of which 3 were waited for; matrix products, arithmetic and copies ran while one was open for 20% of the time, Pallas kernels for 0%

profile of v4, /device:TPU:10, one launch (start us, length us, event | category | flops | bytes accessed | tf_op | source)
XLA Modules:
  0.0 200.6 jit_solution(11131274933773623478)
XLA Ops:
  0.7 2.0 fusion.68
  2.6 3.9 %collective-permute-start = (f32[256,256]{1,0:T(8,128)}, f32[256,256]{1,0:T(8,128)}, u32[]{:S(2)}, u32[]{:S(2)}) collective-permute-start(f32[256,256]{1,0:T(8,128)} %get-tuple-element.38), channel_id=1, source_target_pairs={{0,4},{4,8},{8,12},{12,16},{16,20},{20,24},{24,28},{28,32},{32,36}... | collective-permute-start | bytes 786440 | tf_op jit(solution)/shard_map/ppermute | solution.py:35
  6.6 2.0 %copy.144 = f32[1,512,256]{1,2,0:T(8,128)} copy(f32[1,512,256]{2,1,0:T(8,128)} %param.6) | data formatting | bytes 1048576 | tf_op args[0]
  8.6 1.0 copy.143
  9.6 1.0 copy.166
  10.7 1.0 copy.155
  11.7 1.6 slice_bitcast_fusion
  13.3 2.3 %fusion.32 = f32[512,1024]{0,1:T(8,128)S(1)} fusion(f32[2,512,1024]{2,1,0:T(8,128)} %param.9, f32[1,512,256]{2,1,0:T(8,128)S(1)} %copy-done.5), kind=kOutput, calls=%fused_computation.48 | convolution fusion | flops 805306368 | bytes 3670016 | tf_op jit(solution)/shard_map/dot_general | solution.py:39
  15.6 1.0 copy.162
  16.7 2.0 %copy.156 = f32[512,1,2,8,2,2,4]{0,6,5,4,3,2,1:T(4,128)} copy(f32[512,1,2,8,2,2,4]{0,1,6,5,4,3,2:T(1,128)} %bitcast.134) | data formatting | bytes 1048576 | tf_op jit(solution)/shard_map/concatenate | solution.py:53
  18.9 0.8 copy.154
  19.7 2.7 %fusion.42 = f32[512,512]{0,1:T(8,128)} fusion(f32[512,512]{1,0:T(8,128)} %get-tuple-element.32, f32[1,512,256]{2,1,0:T(8,128)S(1)} %copy-done.7), kind=kOutput, calls=%fused_computation.66 | convolution fusion | flops 402653184 | bytes 2097152 | tf_op jit(solution)/shard_map/dot_general | solution.py:43
  22.4 2.7 %add_add_fusion.1 = f32[512,1024]{0,1:T(8,128)S(1)} fusion(f32[512,1024]{0,1:T(8,128)S(1)} %fusion.32, f32[1024]{0:T(1024)S(1)} %bitcast.140, f32[2,512,1024]{2,1,0:T(8,128)} %param.9, f32[256,256]{1,0:T(8,128)S(1)} %get-tuple-element.37, f32[256,256]{1,0:T(8,128)} %collective-permute-done), kind=kOutput, calls=%fused_computation.16 | convolution fusion | flops 806486016 | bytes 5771264 | tf_op jit(solution)/shard_map/dot_general | solution.py:39
  25.1 0.9 convolution_add_fusion.2
  26.5 3.8 %collective-permute-start.1 = (f32[512,256]{0,1:T(8,128)S(1)}, f32[512,256]{0,1:T(8,128)S(1)}, u32[]{:S(2)}, u32[]{:S(2)}) collective-permute-start(f32[512,256]{0,1:T(8,128)S(1)} %convolution_add_fusion.2), channel_id=1, source_target_pairs={{0,4},{4,8},{8,12},{12,16},{16,20},{20,24},{24,28},{28,32},{32,36}... | collective-permute-start | bytes 1572872 | tf_op jit(solution)/shard_map/ppermute | solution.py:35
  30.3 1.7 fusion.46
  32.0 1.1 copy.152
  33.2 2.3 %fusion.29 = f32[512,1024]{0,1:T(8,128)S(1)} fusion(f32[512,256]{0,1:T(8,128)S(1)} %convolution_add_fusion.2, f32[2,512,1024]{2,1,0:T(8,128)} %param.9), kind=kOutput, calls=%fused_computation.45 | convolution fusion | flops 805306368 | bytes 3670016 | tf_op jit(solution)/shard_map/dot_general | solution.py:39
  35.5 8.7 %collective-permute-done.1 = f32[512,256]{0,1:T(8,128)S(1)} collective-permute-done((f32[512,256]{0,1:T(8,128)S(1)}, f32[512,256]{0,1:T(8,128)S(1)}, u32[]{:S(2)}, u32[]{:S(2)}) %collective-permute-start.1) | collective-permute-done | bytes 524320 | tf_op jit(solution)/shard_map/ppermute | solution.py:35
  44.2 0.8 copy-done.21
  45.0 2.7 %add_add_fusion = f32[512,1024]{0,1:T(8,128)S(1)} fusion(f32[512,1024]{0,1:T(8,128)S(1)} %fusion.29, f32[512,256]{0,1:T(8,128)S(1)} %collective-permute-done.1, f32[1024]{0:T(1024)S(1)} %bitcast.139, f32[2,512,1024]{2,1,0:T(8,128)} %param.9), kind=kOutput, calls=%fused_computation.15 | convolution fusion | flops 806354944 | bytes 5771264 | tf_op jit(solution)/shard_map/dot_general | solution.py:39
  47.8 1.1 subtract_multiply_fusion.3
  49.1 1.6 copy-done
  50.7 1.9 fusion.6
  52.6 1.0 copy-done.11
  53.6 0.8 slice.155
  54.5 3.8 %collective-permute-start.2 = (f32[512,256]{0,1:T(8,128)}, f32[512,256]{0,1:T(8,128)}, u32[]{:S(2)}, u32[]{:S(2)}) collective-permute-start(f32[512,256]{0,1:T(8,128)} %slice.155), channel_id=1, source_target_pairs={{4,0},{8,4},{12,8},{16,12},{20,16},{24,20},{28,24},{32,28},{36,32}... | collective-permute-start | bytes 1572872 | tf_op jit(solution)/shard_map/ppermute | solution.py:35
  58.7 1.5 reshape.95
  60.5 1.3 pad_maximum_fusion.11
  61.8 1.3 reshape.97
  63.1 2.3 %copy.188 = f32[512,2,2,8,2,2,4]{0,6,3,1,2,4,5:T(4,128)} copy(f32[512,2,2,8,2,2,4]{0,6,5,4,3,2,1:T(4,128)} %reshape.97) | data formatting | bytes 2097152 | tf_op jit(solution)/shard_map/reshape | solution.py:28
  65.4 1.6 reshape.98
  67.1 3.2 %fusion.13 = f32[8,1,64,1024]{3,2,0,1:T(8,128)} fusion(f32[8,64,512]{2,1,0:T(8,128)S(1)} %bitcast.130, f32[512,512]{0,1:T(8,128)S(1)} %get-tuple-element.31, f32[512,512]{0,1:T(8,128)S(1)} %get-tuple-element.30), kind=kOutput, calls=%fused_computation.18 | convolution fusion | flops 1611137024 | bytes 5242880 | tf_op jit(solution)/shard_map/dot_general | solution.py:43
  70.3 1.2 fusion.44
  71.5 1.4 concatenate.82
  72.9 3.0 %subtract_multiply_fusion.1 = (f32[512,512]{0,1:T(8,128)S(1)}, f32[512,512]{0,1:T(8,128)S(1)}) fusion(f32[512,1024]{0,1:T(8,128)} %copy-done.16, f32[512,512]{0,1:T(8,128)} %fusion.42, f32[512,256]{0,1:T(8,128)S(1)} %fusion.44, f32[512,512]{1,0:T(8,128)} %get-tuple-element.32), kind=kOutput, calls=%fused_computation.53 | convolution fusion | flops 405798912 | bytes 6291456 | tf_op jit(solution)/shard_map/dot_general | solution.py:43
  76.4 1.0 reshape.104
  77.5 2.9 %fusion.18 = (f32[512,2,2,2,2,8,4]{0,4,6,1,2,5,3:T(2,128)S(1)}, f32[512,2,2,2,2,8,4]{0,4,6,1,2,5,3:T(2,128)S(1)}) fusion(f32[512,1,2,8,2,2,4]{0,1,6,5,4,3,2:T(1,128)} %bitcast.133, f32[512,1,2,8,2,2,4]{0,1,6,5,4,3,2:T(1,128)} %concatenate.82, f32[512,1,2,8,2,2,4]{0,1,6,5,4,3,2:T(1,128)} %bitcast.132), kind=kLoop, calls=%fused_computation.28 | loop fusion | flops 524288 | bytes 3670016 | tf_op jit(solution)/shard_map/transpose | solution.py:28
  80.4 1.2 copy.167
  81.6 2.6 %reshape.102 = f32[512,512]{0,1:T(8,128)} reshape(f32[512,2,2,2,2,8,4]{0,6,5,4,3,2,1:T(4,128)} %copy.167) | data formatting | bytes 2097152 | tf_op jit(solution)/shard_map/reshape | solution.py:29
  84.2 4.1 %convolution_bitcast_fusion = f32[8,1,64,512]{3,2,0,1:T(8,128)} fusion(f32[8,64,512]{2,1,0:T(8,128)} %bitcast.136, f32[512,1024]{0,1:T(8,128)} %copy-done.17), kind=kOutput, calls=%fused_computation.19 | convolution fusion | flops 806354944 | bytes 4194304 | tf_op jit(solution)/shard_map/dot_general | solution.py:43
  88.3 1.3 copy.164
  89.5 1.6 reshape.100
  91.1 2.9 %convolution_bitcast_fusion.1 = f32[8,1,64,512]{3,2,0,1:T(8,128)S(1)} fusion(f32[8,64,512]{2,1,0:T(8,128)S(1)} %bitcast.137, f32[512,1024]{0,1:T(8,128)} %copy-done.16), kind=kOutput, calls=%fused_computation.20 | convolution fusion | flops 806354944 | bytes 4194304 | tf_op jit(solution)/shard_map/dot_general | solution.py:43
  94.8 0.7 copy-done.10
  95.5 1.9 fusion.10
  98.1 0.7 copy-done.22
  98.8 0.5 pad_maximum_fusion
  99.4 10.4 %all_to_all.20 = f32[2,512,1664]{2,1,0:T(8,128)} all-to-all(f32[2,512,1664]{2,1,0:T(8,128)S(1)} %pad_maximum_fusion), channel_id=1, replica_groups=mesh['y'=4,'xl'=2,'z'=8,'xh'=2,'c'=2] {'c'}, dimensions={0} | all-to-all | bytes 13631488 | tf_op jit(solution)/shard_map/all_to_all | solution.py:16
  109.8 3.7 %reduce_sum.56 = f32[512,1664]{1,0:T(8,128)S(1)} reduce(f32[2,512,1664]{2,1,0:T(8,128)} %all_to_all.20, f32[]{:T(128)} %constant.1.clone.1), dimensions={0}, to_apply=%region_2.3 | reduce | flops 851968 | bytes 10223620 | tf_op jit(solution)/shard_map/reduce_sum | solution.py:16
  113.5 44.5 %all_to_all.21 = f32[4,128,1664]{2,1,0:T(8,128)} all-to-all(f32[4,128,1664]{2,1,0:T(8,128)S(1)} %bitcast.127), channel_id=1, replica_groups=mesh['y'=4,'xl'=2,'z'=8,'xh'=2,'c'=2] {'xh','xl'}, dimensions={0} | all-to-all | bytes 6815744 | tf_op jit(solution)/shard_map/all_to_all | solution.py:16
  158.0 3.3 %reduce_sum.57 = f32[128,1664]{1,0:T(8,128)} reduce(f32[4,128,1664]{2,1,0:T(8,128)} %all_to_all.21, f32[]{:T(128)} %constant.1.clone.1), dimensions={0}, to_apply=%region_3.4 | reduce | flops 638976 | bytes 4259844 | tf_op jit(solution)/shard_map/reduce_sum | solution.py:16
  161.3 5.0 %all-to-all-start.2 = ((f32[4,32,1664]{2,1,0:T(8,128)}), f32[4,32,1664]{2,1,0:T(8,128)}, u32[]{:S(2)}, u32[]{:S(2)}) async-start(f32[4,32,1664]{2,1,0:T(8,128)} %bitcast.45), calls=%async_computation.2 | async-start | bytes 1703936 | tf_op jit(solution)/shard_map/all_to_all | solution.py:16
  166.3 3.4 %fusion.4 = f32[512,512]{0,1:T(8,128)S(1)} fusion(f32[2,512,1024]{2,1,0:T(8,128)} %param.9, f32[512,512]{0,1:T(8,128)S(1)} %copy-done.4, f32[512,512]{0,1:T(8,128)S(1)} %copy-done.2), kind=kOutput, calls=%fused_computation.9 | convolution fusion | flops 1611137024 | bytes 5242880 | tf_op jit(solution)/shard_map/dot_general | solution.py:43
  169.8 6.0 %collective-permute-start.3 = (f32[256,256]{0,1:T(8,128)S(1)}, f32[256,256]{0,1:T(8,128)S(1)}, u32[]{:S(2)}, u32[]{:S(2)}) collective-permute-start(f32[256,256]{0,1:T(8,128)S(1)} %get-tuple-element.35), channel_id=1, source_target_pairs={{4,0},{8,4},{12,8},{16,12},{20,16},{24,20},{28,24},{32,28},{36,32}... | collective-permute-start | bytes 786440 | tf_op jit(solution)/shard_map/ppermute | solution.py:35
  175.8 1.2 all-to-all-done.2
  177.0 1.2 reduce_sum.58
  178.3 0.8 reshape.107
  179.0 9.7 %all-to-all-start.3 = ((f32[8,4,1664]{2,1,0:T(4,128)}), f32[8,4,1664]{2,1,0:T(4,128)S(1)}, u32[]{:S(2)}, u32[]{:S(2)}) async-start(f32[8,4,1664]{2,1,0:T(4,128)} %reshape.107), calls=%async_computation.3 | async-start | bytes 425984 | tf_op jit(solution)/shard_map/all_to_all | solution.py:16
  188.9 1.0 copy.172
  189.9 8.8 %all-to-all-done.3 = f32[8,4,1664]{2,1,0:T(4,128)S(1)} async-done(((f32[8,4,1664]{2,1,0:T(4,128)}), f32[8,4,1664]{2,1,0:T(4,128)S(1)}, u32[]{:S(2)}, u32[]{:S(2)}) %all-to-all-start.3) | async-done | bytes 213024 | tf_op jit(solution)/shard_map/all_to_all | solution.py:16
  198.8 0.6 slice.160
  199.4 0.6 slice.161
  200.0 0.6 reshape.108
  (81 shorter events, 3.7 us)
Async XLA Ops:
  0.6 10.0 %copy-start.5 = (f32[1,512,256]{2,1,0:T(8,128)S(1)}, f32[1,512,256]{2,1,0:T(8,128)}, u32[]{:S(2)}) copy-start(f32[1,512,256]{2,1,0:T(8,128)} %param.6) | copy-start | bytes 1572868
  0.6 8.0 %copy-start.18 = (f32[1,512,256]{2,1,0:T(8,128)S(1)}, f32[1,512,256]{2,1,0:T(8,128)}, u32[]{:S(2)}) copy-start(f32[1,512,256]{2,1,0:T(8,128)} %param.7) | copy-start | bytes 1572868
  2.6 9.1 %copy-start.15 = (f32[2,512,512]{2,1,0:T(8,128)S(1)}, f32[2,512,512]{2,1,0:T(8,128)}, u32[]{:S(2)}) copy-start(f32[2,512,512]{2,1,0:T(8,128)} %param.11) | copy-start | bytes 6291460
  2.6 19.7 %collective-permute-start = (f32[256,256]{1,0:T(8,128)}, f32[256,256]{1,0:T(8,128)}, u32[]{:S(2)}, u32[]{:S(2)}) collective-permute-start(f32[256,256]{1,0:T(8,128)} %get-tuple-element.38), channel_id=1, source_target_pairs={{0,4},{4,8},{8,12},{12,16},{16,20},{20,24},{24,28},{28,32},{32,36}... | collective-permute-start | bytes 786440 | tf_op jit(solution)/shard_map/ppermute | solution.py:35
  13.3 2.3 %copy-start.30 = (f32[2,1024]{1,0:T(2,128)S(1)}, f32[2,1024]{1,0:T(2,128)}, u32[]{:S(2)}) copy-start(f32[2,1024]{1,0:T(2,128)} %param.10) | copy-start | bytes 24580
  13.3 2.3 %copy-start.7 = (f32[1,512,256]{2,1,0:T(8,128)S(1)}, f32[1,512,256]{2,1,0:T(8,128)}, u32[]{:S(2)}) copy-start(f32[1,512,256]{2,1,0:T(8,128)} %param.8) | copy-start | bytes 1572868
  15.6 3.1 %copy-start.25 = (f32[1,256,256]{2,1,0:T(8,128)S(1)}, f32[1,256,256]{2,1,0:T(8,128)}, u32[]{:S(2)}) copy-start(f32[1,256,256]{2,1,0:T(8,128)} %get-tuple-element.36) | copy-start | bytes 786436
  22.4 2.7 %copy-start.13 = (f32[512,512]{1,0:T(8,128)S(1)}, f32[512,512]{1,0:T(8,128)}, u32[]{:S(2)}) copy-start(f32[512,512]{1,0:T(8,128)} %get-tuple-element.32) | copy-start | bytes 3145732
  22.4 2.7 %copy-start.29 = (f32[1,512,256]{1,2,0:T(8,128)S(1)}, f32[1,512,256]{1,2,0:T(8,128)}, u32[]{:S(2)}) copy-start(f32[1,512,256]{1,2,0:T(8,128)} %copy.144) | copy-start | bytes 1572868
  25.1 1.3 copy-start.16
  25.1 5.2 %copy-start.14 = (f32[512,512]{1,0:T(8,128)S(1)}, f32[512,512]{1,0:T(8,128)}, u32[]{:S(2)}) copy-start(f32[512,512]{1,0:T(8,128)} %get-tuple-element.33) | copy-start | bytes 3145732
  26.5 9.0 %copy-start.20 = (f32[512,256]{0,1:T(8,128)}, f32[512,256]{0,1:T(8,128)S(1)}, u32[]{:S(2)}) copy-start(f32[512,256]{0,1:T(8,128)S(1)} %convolution_add_fusion.2) | copy-start | bytes 1572868
  26.5 17.7 %collective-permute-start.1 = (f32[512,256]{0,1:T(8,128)S(1)}, f32[512,256]{0,1:T(8,128)S(1)}, u32[]{:S(2)}, u32[]{:S(2)}) collective-permute-start(f32[512,256]{0,1:T(8,128)S(1)} %convolution_add_fusion.2), channel_id=1, source_target_pairs={{0,4},{4,8},{8,12},{12,16},{16,20},{20,24},{24,28},{28,32},{32,36}... | collective-permute-start | bytes 1572872 | tf_op jit(solution)/shard_map/ppermute | solution.py:35
  44.2 0.8 copy-start.21
  45.0 2.7 %copy-start.19 = (f32[1,512,256]{2,1,0:T(8,128)S(1)}, f32[1,512,256]{2,1,0:T(8,128)}, u32[]{:S(2)}) copy-start(f32[1,512,256]{2,1,0:T(8,128)} %param.7) | copy-start | bytes 1572868
  45.0 2.7 %copy-start.26 = (f32[512,512]{0,1:T(8,128)S(1)}, f32[512,512]{0,1:T(8,128)}, u32[]{:S(2)}) copy-start(f32[512,512]{0,1:T(8,128)} %fusion.46) | copy-start | bytes 3145732
  47.8 1.3 copy-start.17
  47.8 2.9 %copy-start = (f32[2,512,1024]{2,1,0:T(8,128)S(1)}, f32[2,512,1024]{2,1,0:T(8,128)}, u32[]{:S(2)}) copy-start(f32[2,512,1024]{2,1,0:T(8,128)} %param.9) | copy-start | bytes 12582916
  50.7 7.6 %copy-start.24 = (f32[512,1,2,8,2,2,4]{0,6,5,4,3,2,1:T(4,128)S(1)}, f32[512,1,2,8,2,2,4]{0,6,5,4,3,2,1:T(4,128)}, u32[]{:S(2)}) copy-start(f32[512,1,2,8,2,2,4]{0,6,5,4,3,2,1:T(4,128)} %copy.156) | copy-start | bytes 1572868
  50.7 7.6 %copy-start.28 = (f32[256,1,2,8,2,2,4]{0,6,5,4,3,2,1:T(4,128)S(1)}, f32[256,1,2,8,2,2,4]{0,6,5,4,3,2,1:T(4,128)}, u32[]{:S(2)}) copy-start(f32[256,1,2,8,2,2,4]{0,6,5,4,3,2,1:T(4,128)} %copy.154) | copy-start | bytes 786436
  52.6 1.0 copy-start.11
  54.5 15.8 %collective-permute-start.2 = (f32[512,256]{0,1:T(8,128)}, f32[512,256]{0,1:T(8,128)}, u32[]{:S(2)}, u32[]{:S(2)}) collective-permute-start(f32[512,256]{0,1:T(8,128)} %slice.155), channel_id=1, source_target_pairs={{4,0},{8,4},{12,8},{16,12},{20,16},{24,20},{28,24},{32,28},{36,32}... | collective-permute-start | bytes 1572872 | tf_op jit(solution)/shard_map/ppermute | solution.py:35
  67.0 3.2 %copy-start.12 = (f32[512,512]{0,1:T(8,128)S(1)}, f32[512,512]{0,1:T(8,128)}, u32[]{:S(2)}) copy-start(f32[512,512]{0,1:T(8,128)} %copy-done.11) | copy-start | bytes 3145732
  67.0 3.2 %copy-start.23 = (f32[1,512,256]{1,2,0:T(8,128)S(1)}, f32[1,512,256]{1,2,0:T(8,128)}, u32[]{:S(2)}) copy-start(f32[1,512,256]{1,2,0:T(8,128)} %copy.143) | copy-start | bytes 1572868
  71.5 4.5 %copy-start.8 = (f32[512,256]{0,1:T(8,128)}, f32[512,256]{0,1:T(8,128)S(1)}, u32[]{:S(2)}) copy-start(f32[512,256]{0,1:T(8,128)S(1)} %fusion.44) | copy-start | bytes 1572868
  76.0 18.8 %copy-start.1 = (f32[512,512]{0,1:T(8,128)}, f32[512,512]{0,1:T(8,128)S(1)}, u32[]{:S(2)}) copy-start(f32[512,512]{0,1:T(8,128)S(1)} %get-tuple-element.28) | copy-start | bytes 3145732
  76.0 18.8 %copy-start.3 = (f32[512,512]{0,1:T(8,128)}, f32[512,512]{0,1:T(8,128)S(1)}, u32[]{:S(2)}) copy-start(f32[512,512]{0,1:T(8,128)S(1)} %get-tuple-element.29) | copy-start | bytes 3145732
  91.1 2.9 %copy-start.27 = (f32[8,1,64,512]{3,2,0,1:T(8,128)S(1)}, f32[8,1,64,512]{3,2,0,1:T(8,128)}, u32[]{:S(2)}) copy-start(f32[8,1,64,512]{3,2,0,1:T(8,128)} %convolution_bitcast_fusion) | copy-start | bytes 3145732
  94.3 1.2 copy-start.10
  95.5 1.9 copy-start.6
  97.7 1.0 copy-start.22
  158.0 8.3 %copy-start.2 = (f32[512,512]{0,1:T(8,128)S(1)}, f32[512,512]{0,1:T(8,128)}, u32[]{:S(2)}) copy-start(f32[512,512]{0,1:T(8,128)} %copy-done.1) | copy-start | bytes 3145732
  158.0 8.3 %copy-start.4 = (f32[512,512]{0,1:T(8,128)S(1)}, f32[512,512]{0,1:T(8,128)}, u32[]{:S(2)}) copy-start(f32[512,512]{0,1:T(8,128)} %copy-done.3) | copy-start | bytes 3145732
  161.3 15.8 %all-to-all-start.2 = ((f32[4,32,1664]{2,1,0:T(8,128)}), f32[4,32,1664]{2,1,0:T(8,128)}, u32[]{:S(2)}, u32[]{:S(2)}) async-start(f32[4,32,1664]{2,1,0:T(8,128)} %bitcast.45), calls=%async_computation.2 | async-start | bytes 1703936 | tf_op jit(solution)/shard_map/all_to_all | solution.py:16
  169.7 19.0 %copy-start.9 = (f32[512,256]{0,1:T(8,128)S(1)}, f32[512,256]{0,1:T(8,128)}, u32[]{:S(2)}) copy-start(f32[512,256]{0,1:T(8,128)} %copy-done.8) | copy-start | bytes 1572868
  169.8 18.9 %collective-permute-start.3 = (f32[256,256]{0,1:T(8,128)S(1)}, f32[256,256]{0,1:T(8,128)S(1)}, u32[]{:S(2)}, u32[]{:S(2)}) collective-permute-start(f32[256,256]{0,1:T(8,128)S(1)} %get-tuple-element.35), channel_id=1, source_target_pairs={{4,0},{8,4},{12,8},{16,12},{20,16},{24,20},{28,24},{32,28},{36,32}... | collective-permute-start | bytes 786440 | tf_op jit(solution)/shard_map/ppermute | solution.py:35
  179.0 19.7 %all-to-all-start.3 = ((f32[8,4,1664]{2,1,0:T(4,128)}), f32[8,4,1664]{2,1,0:T(4,128)S(1)}, u32[]{:S(2)}, u32[]{:S(2)}) async-start(f32[8,4,1664]{2,1,0:T(4,128)} %reshape.107), calls=%async_computation.3 | async-start | bytes 425984 | tf_op jit(solution)/shard_map/all_to_all | solution.py:16

commit v5 on v3

--- a/solution.py
+++ b/solution.py
@@ -19,8 +19,8 @@
 def reduce_to_owner(packed):
     rows, width = packed.shape
     sizes = [lax.axis_size(a) for a in ("y", "xl", "z", "xh", "c")]
-    block = packed.reshape(*sizes, -1, width).transpose(4, 3, 1, 0, 2, 5, 6).reshape(rows, width)
-    for axis in ("c", ("xh", "xl"), "y", "z"):
+    block = packed.reshape(*sizes, -1, width).transpose(4, 1, 3, 0, 2, 5, 6).reshape(rows, width)
+    for axis in ("c", "xl", "xh", "y", "z"):
         block = reduce_rows(block, axis)
     return block
 

time: 198 us -> 223 us (1.13)
  blocking collectives: 55.8 us -> 79.6 us
    all_to_all x2 -> x3, blocking collectives: 55.8 us -> 79.6 us  [reduce_rows(): return lax.all_to_all(block, axis, 0, 0, tiled=True).sum(axis=0)]
    reduce_sum x4 -> x5, other arithmetic: 8.28 us -> 10.1 us  [reduce_rows(): return lax.all_to_all(block, axis, 0, 0, tiled=True).sum(axis=0)]
  transfers between devices with their start and end apart: 6 -> 6, of which waited for: 4 -> 4; matrix products, arithmetic and copies ran while one was open for 12% -> 10% of each run, Pallas kernels for 0% -> 0%
where the time goes in v5:
time: 223 us; the launch traced here: 222 us
  blocking collectives  79.6 us (36%)
  local copies, waits for them, and re-layouts  34.4 us (15%)
  waiting for transfers between devices  32.3 us (14%)
  matrix products  28.5 us (13%)
  starting transfers between devices  25.1 us (11%)
  other arithmetic  20.7 us (9%)
    all_to_all x3, blocking collectives, reduce_rows(): return lax.all_to_all(block, axis, 0, 0, tiled=True).sum(axis=0)  79.6 us
    dot_general x10, matrix products, contract(): lax.dot_general(left, right, (((left_dim,), (right_dim,)), ((), ())), pre...  21.5 us
    ppermute x4, waiting for transfers between devices, from_behind(): return lax.ppermute(block, axis, route)  21.2 us
    reshape x2, local copies, waits for them, and re-layouts, reduce_to_owner(): packed.reshape(*sizes, -1, width).transpose(4, 1, 3, 0, 2, 5, 6)  17.8 us
    ppermute x4, starting transfers between devices, from_behind(): return lax.ppermute(block, axis, route)  12.9 us
    all_to_all x2, starting transfers between devices, reduce_rows(): return lax.all_to_all(block, axis, 0, 0, tiled=True).sum(axis=0)  12.2 us
    all_to_all x2, waiting for transfers between devices, reduce_rows(): return lax.all_to_all(block, axis, 0, 0, tiled=True).sum(axis=0)  11.2 us
    reduce_sum x5, other arithmetic, reduce_rows(): return lax.all_to_all(block, axis, 0, 0, tiled=True).sum(axis=0)  10.1 us
  transfers between devices with their start and end apart: 6, of which 4 were waited for; matrix products, arithmetic and copies ran while one was open for 10% of the time, Pallas kernels for 0%

profile of v5, /device:TPU:10, one launch (start us, length us, event | category | flops | bytes accessed | tf_op | source)
XLA Modules:
  0.0 221.7 jit_solution(16377945126512708326)
XLA Ops:
  0.6 1.3 copy.89
  2.0 0.0 copy-start.15
  2.0 4.0 %collective-permute-start = (f32[256,256]{0,1:T(8,128)S(1)}, f32[256,256]{0,1:T(8,128)S(1)}, u32[]{:S(2)}, u32[]{:S(2)}) collective-permute-start(f32[256,256]{0,1:T(8,128)S(1)} %get-tuple-element.36), channel_id=1, source_target_pairs={{0,4},{4,8},{8,12},{12,16},{16,20},{20,24},{24,28},{28,32},{32,36}... | collective-permute-start | bytes 786440 | tf_op jit(solution)/shard_map/ppermute | solution.py:31
  6.0 0.0 copy-start.29
  6.0 2.3 %fusion.32 = f32[512,1024]{0,1:T(8,128)S(1)} fusion(f32[2,512,1024]{2,1,0:T(8,128)} %param.9, f32[1,512,256]{2,1,0:T(8,128)S(1)} %copy-done.14), kind=kOutput, calls=%fused_computation.46 | convolution fusion | flops 805306368 | bytes 3670016 | tf_op jit(solution)/shard_map/dot_general | solution.py:35
  8.3 0.0 copy-start
  8.3 0.2 slice_bitcast_fusion
  8.5 7.7 %collective-permute-done = f32[256,256]{0,1:T(8,128)S(1)} collective-permute-done((f32[256,256]{0,1:T(8,128)S(1)}, f32[256,256]{0,1:T(8,128)S(1)}, u32[]{:S(2)}, u32[]{:S(2)}) %collective-permute-start) | collective-permute-done | bytes 262176 | tf_op jit(solution)/shard_map/ppermute | solution.py:31
  16.2 1.4 add_add_fusion.1
  17.6 0.0 copy-start.6
  17.6 0.9 convolution_add_fusion.2
  18.5 0.4 copy-done.16
  18.9 1.9 collective-permute-start.1
  20.8 0.6 fusion.46
  21.4 1.0 fusion.29
  22.5 13.5 %collective-permute-done.1 = f32[512,256]{0,1:T(8,128)S(1)} collective-permute-done((f32[512,256]{0,1:T(8,128)S(1)}, f32[512,256]{0,1:T(8,128)S(1)}, u32[]{:S(2)}, u32[]{:S(2)}) %collective-permute-start.1) | collective-permute-done | bytes 524320 | tf_op jit(solution)/shard_map/ppermute | solution.py:31
  36.0 1.4 add_add_fusion
  37.4 1.1 subtract_multiply_fusion.3
  38.5 0.3 copy-done.18
  38.7 1.9 fusion.2
  40.6 1.0 copy-done.7
  41.7 0.8 slice.157
  42.5 2.1 collective-permute-start.2
  44.6 1.7 fusion.42
  46.3 2.0 copy.87
  48.3 1.0 copy.88
  49.3 0.2 fusion.8
  49.6 0.9 concatenate.52
  50.4 4.3 %fusion.9 = f32[512,1024]{1,0:T(8,128)} fusion(f32[512,512]{0,1:T(8,128)S(1)} %get-tuple-element.31, f32[512,512]{0,1:T(8,128)S(1)} %get-tuple-element.30, f32[512,256]{0,1:T(8,128)S(1)} %copy-done.12, f32[512,256]{0,1:T(8,128)} %copy-done.13), kind=kOutput, calls=%fused_computation.16 | convolution fusion | flops 1611399168 | bytes 5242880 | tf_op jit(solution)/shard_map/dot_general | solution.py:39
  54.8 2.2 %fusion.11 = f32[512,512]{1,0:T(8,128)} fusion(f32[512,256]{0,1:T(8,128)S(1)} %bitcast.63, f32[512,256]{0,1:T(8,128)S(1)} %bitcast.62, f32[512,1024]{0,1:T(8,128)S(1)} %copy-done.19), kind=kOutput, calls=%fused_computation.21 | convolution fusion | flops 806617088 | bytes 4194304 | tf_op jit(solution)/shard_map/dot_general | solution.py:39
  57.1 0.0 collective-permute-done.2
  57.1 1.3 fusion.44
  58.4 0.4 copy-done.17
  58.8 2.2 %fusion.10 = f32[512,512]{1,0:T(8,128)} fusion(f32[512,256]{0,1:T(8,128)S(1)} %bitcast.64, f32[512,256]{0,1:T(8,128)S(1)} %fusion.44, f32[512,1024]{0,1:T(8,128)S(1)} %copy-done.17), kind=kOutput, calls=%fused_computation.20 | convolution fusion | flops 806617088 | bytes 4194304 | tf_op jit(solution)/shard_map/dot_general | solution.py:39
  61.1 1.0 subtract_multiply_fusion.1
  62.1 0.2 fusion.6
  62.4 1.2 concatenate.51
  63.5 1.1 select_maximum_fusion
  64.6 3.0 %fusion.7 = f32[512,1024]{1,0:T(8,128)S(1)} fusion(f32[512,512]{0,1:T(8,128)S(1)} %get-tuple-element.29, f32[512,512]{0,1:T(8,128)S(1)} %get-tuple-element.28, f32[512,256]{0,1:T(8,128)S(1)} %bitcast.61, f32[256,256]{0,1:T(8,128)S(1)} %get-tuple-element.37, f32[256,256]{0,1:T(8,128)} %copy-done.23), kind=kOutput, calls=%fused_computation.14 | convolution fusion | flops 1611661312 | bytes 5242880 | tf_op jit(solution)/shard_map/dot_general | solution.py:39
  67.7 7.6 %pad_maximum_fusion = f32[1024,1664]{1,0:T(8,128)} fusion(f32[1024,128]{1,0:T(8,128)S(1)} %select_maximum_fusion, f32[512,512]{1,0:T(8,128)S(1)} %copy-done.25, f32[512,512]{1,0:T(8,128)S(1)} %copy-done.26, f32[512,1024]{1,0:T(8,128)S(1)} %copy-done.5, f32[512,1024]{1,0:T(8,128)S(1)} %fusion.7), kind=kLoop, calls=%fused_computation | loop fusion | flops 6815744 | bytes 13631488 | tf_op jit(solution)/shard_map/concatenate | solution.py:123
  75.3 8.5 %reshape.35 = f32[4,2,8,2,2,4,1664]{6,5,4,3,2,1,0:T(4,128)} reshape(f32[1024,1664]{1,0:T(8,128)} %pad_maximum_fusion) | data formatting | bytes 13631488 | tf_op jit(solution)/shard_map/reshape | solution.py:22
  83.8 9.3 %copy.99 = f32[4,2,8,2,2,4,1664]{6,4,5,2,0,3,1:T(2,128)} copy(f32[4,2,8,2,2,4,1664]{6,5,4,3,2,1,0:T(4,128)} %reshape.35) | data formatting | bytes 13631488 | tf_op jit(solution)/shard_map/reshape | solution.py:22
  93.1 3.4 %copy.100 = f32[2,512,1664]{2,1,0:T(8,128)S(1)} copy(f32[2,512,1664]{2,0,1:T(2,128)} %bitcast.58) | data formatting | bytes 13631488 | tf_op jit(solution)/shard_map/reshape;reshape | solution.py:15
  96.5 10.4 %all_to_all.25 = f32[2,512,1664]{2,1,0:T(8,128)} all-to-all(f32[2,512,1664]{2,1,0:T(8,128)S(1)} %copy.100), channel_id=1, replica_groups=mesh['y'=4,'xl'=2,'z'=8,'xh'=2,'c'=2] {'c'}, dimensions={0} | all-to-all | bytes 13631488 | tf_op jit(solution)/shard_map/all_to_all | solution.py:16
  106.9 3.7 %reduce_sum.65 = f32[512,1664]{1,0:T(8,128)S(1)} reduce(f32[2,512,1664]{2,1,0:T(8,128)} %all_to_all.25, f32[]{:T(128)} %constant.1.clone.1), dimensions={0}, to_apply=%region_2.3 | reduce | flops 851968 | bytes 10223620 | tf_op jit(solution)/shard_map/reduce_sum | solution.py:16
  110.6 43.7 %all_to_all.26 = f32[2,256,1664]{2,1,0:T(8,128)} all-to-all(f32[2,256,1664]{2,1,0:T(8,128)S(1)} %bitcast.59), channel_id=1, replica_groups=mesh['y'=4,'xl'=2,'z'=8,'xh'=2,'c'=2] {'xl'}, dimensions={0} | all-to-all | bytes 6815744 | tf_op jit(solution)/shard_map/all_to_all | solution.py:16
  154.3 2.4 %reduce_sum.66 = f32[256,1664]{1,0:T(8,128)S(1)} reduce(f32[2,256,1664]{2,1,0:T(8,128)} %all_to_all.26, f32[]{:T(128)} %constant.1.clone.1), dimensions={0}, to_apply=%region_3.4 | reduce | flops 425984 | bytes 5111812 | tf_op jit(solution)/shard_map/reduce_sum | solution.py:16
  156.7 25.5 %all_to_all.27 = f32[2,128,1664]{2,1,0:T(8,128)} all-to-all(f32[2,128,1664]{2,1,0:T(8,128)S(1)} %bitcast.60), channel_id=1, replica_groups=mesh['y'=4,'xl'=2,'z'=8,'xh'=2,'c'=2] {'xh'}, dimensions={0} | all-to-all | bytes 3407872 | tf_op jit(solution)/shard_map/all_to_all | solution.py:16
  182.2 2.7 %reduce_sum.67 = f32[128,1664]{1,0:T(8,128)} reduce(f32[2,128,1664]{2,1,0:T(8,128)} %all_to_all.27, f32[]{:T(128)} %constant.1.clone.1), dimensions={0}, to_apply=%region_4.5 | reduce | flops 212992 | bytes 2555908 | tf_op jit(solution)/shard_map/reduce_sum | solution.py:16
  184.9 5.0 %all-to-all-start.3 = ((f32[4,32,1664]{2,1,0:T(8,128)}), f32[4,32,1664]{2,1,0:T(8,128)}, u32[]{:S(2)}, u32[]{:S(2)}) async-start(f32[4,32,1664]{2,1,0:T(8,128)} %bitcast.20), calls=%async_computation.3 | async-start | bytes 1703936 | tf_op jit(solution)/shard_map/all_to_all | solution.py:16
  189.9 3.4 %fusion = f32[512,512]{0,1:T(8,128)S(1)} fusion(f32[2,512,1024]{2,1,0:T(8,128)} %param.9, f32[512,512]{0,1:T(8,128)S(1)} %copy-done.4, f32[512,512]{0,1:T(8,128)S(1)} %copy-done.2), kind=kOutput, calls=%fused_computation.3 | convolution fusion | flops 1611137024 | bytes 5242880 | tf_op jit(solution)/shard_map/dot_general | solution.py:39
  193.4 0.0 copy-start.22
  193.4 4.9 %collective-permute-start.3 = (f32[256,256]{0,1:T(8,128)S(1)}, f32[256,256]{0,1:T(8,128)S(1)}, u32[]{:S(2)}, u32[]{:S(2)}) collective-permute-start(f32[256,256]{0,1:T(8,128)S(1)} %get-tuple-element.35), channel_id=1, source_target_pairs={{4,0},{8,4},{12,8},{16,12},{20,16},{24,20},{28,24},{32,28},{36,32}... | collective-permute-start | bytes 786440 | tf_op jit(solution)/shard_map/ppermute | solution.py:31
  198.3 2.4 %all-to-all-done.3 = f32[4,32,1664]{2,1,0:T(8,128)} async-done(((f32[4,32,1664]{2,1,0:T(8,128)}), f32[4,32,1664]{2,1,0:T(8,128)}, u32[]{:S(2)}, u32[]{:S(2)}) %all-to-all-start.3) | async-done | bytes 852000 | tf_op jit(solution)/shard_map/all_to_all | solution.py:16
  200.7 1.2 reduce_sum.68
  201.9 0.7 reshape.39
  202.7 7.2 %all-to-all-start.4 = ((f32[8,4,1664]{2,1,0:T(4,128)}), f32[8,4,1664]{2,1,0:T(4,128)S(1)}, u32[]{:S(2)}, u32[]{:S(2)}) async-start(f32[8,4,1664]{2,1,0:T(4,128)} %reshape.39), calls=%async_computation.4 | async-start | bytes 425984 | tf_op jit(solution)/shard_map/all_to_all | solution.py:16
  209.9 0.0 collective-permute-done.3
  209.9 0.1 fusion.41
  210.0 1.0 copy.102
  211.0 8.8 %all-to-all-done.4 = f32[8,4,1664]{2,1,0:T(4,128)S(1)} async-done(((f32[8,4,1664]{2,1,0:T(4,128)}), f32[8,4,1664]{2,1,0:T(4,128)S(1)}, u32[]{:S(2)}, u32[]{:S(2)}) %all-to-all-start.4) | async-done | bytes 213024 | tf_op jit(solution)/shard_map/all_to_all | solution.py:16
  219.9 0.6 slice.162
  220.5 0.6 slice.163
  221.1 0.6 reshape.40
  (57 shorter events, 0.2 us)
Async XLA Ops:
  0.6 5.3 %copy-start.14 = (f32[1,512,256]{2,1,0:T(8,128)S(1)}, f32[1,512,256]{2,1,0:T(8,128)}, u32[]{:S(2)}) copy-start(f32[1,512,256]{2,1,0:T(8,128)} %param.6) | copy-start | bytes 1572868
  2.0 6.3 %copy-start.15 = (f32[2,512,512]{2,1,0:T(8,128)S(1)}, f32[2,512,512]{2,1,0:T(8,128)}, u32[]{:S(2)}) copy-start(f32[2,512,512]{2,1,0:T(8,128)} %param.11) | copy-start | bytes 6291460
  2.0 14.2 %collective-permute-start = (f32[256,256]{0,1:T(8,128)S(1)}, f32[256,256]{0,1:T(8,128)S(1)}, u32[]{:S(2)}, u32[]{:S(2)}) collective-permute-start(f32[256,256]{0,1:T(8,128)S(1)} %get-tuple-element.36), channel_id=1, source_target_pairs={{0,4},{4,8},{8,12},{12,16},{16,20},{20,24},{24,28},{28,32},{32,36}... | collective-permute-start | bytes 786440 | tf_op jit(solution)/shard_map/ppermute | solution.py:31
  6.0 2.5 %copy-start.29 = (f32[2,1024]{1,0:T(2,128)S(1)}, f32[2,1024]{1,0:T(2,128)}, u32[]{:S(2)}) copy-start(f32[2,1024]{1,0:T(2,128)} %param.10) | copy-start | bytes 24580
  8.3 7.9 %copy-start = (f32[2,512,1024]{2,1,0:T(8,128)S(1)}, f32[2,512,1024]{2,1,0:T(8,128)}, u32[]{:S(2)}) copy-start(f32[2,512,1024]{2,1,0:T(8,128)} %param.9) | copy-start | bytes 12582916
  8.5 36.1 %copy-start.9 = (f32[512,512]{1,0:T(8,128)}, f32[512,512]{1,0:T(8,128)S(1)}, u32[]{:S(2)}) copy-start(f32[512,512]{1,0:T(8,128)S(1)} %get-tuple-element.32) | copy-start | bytes 3145732
  16.2 1.4 copy-start.23
  17.6 1.3 copy-start.16
  17.6 3.2 %copy-start.6 = (f32[1,512,256]{2,1,0:T(8,128)S(1)}, f32[1,512,256]{2,1,0:T(8,128)}, u32[]{:S(2)}) copy-start(f32[1,512,256]{2,1,0:T(8,128)} %param.8) | copy-start | bytes 1572868
  18.9 3.6 %copy-start.11 = (f32[512,256]{0,1:T(8,128)}, f32[512,256]{0,1:T(8,128)S(1)}, u32[]{:S(2)}) copy-start(f32[512,256]{0,1:T(8,128)S(1)} %convolution_add_fusion.2) | copy-start | bytes 1572868
  18.9 17.1 %collective-permute-start.1 = (f32[512,256]{0,1:T(8,128)S(1)}, f32[512,256]{0,1:T(8,128)S(1)}, u32[]{:S(2)}, u32[]{:S(2)}) collective-permute-start(f32[512,256]{0,1:T(8,128)S(1)} %convolution_add_fusion.2), channel_id=1, source_target_pairs={{0,4},{4,8},{8,12},{12,16},{16,20},{20,24},{24,28},{28,32},{32,36}... | collective-permute-start | bytes 1572872 | tf_op jit(solution)/shard_map/ppermute | solution.py:31
  36.0 1.4 copy-start.13
  36.0 1.4 copy-start.27
  37.4 1.3 copy-start.18
  40.6 1.1 copy-start.7
  42.5 14.6 %collective-permute-start.2 = (f32[512,256]{0,1:T(8,128)}, f32[512,256]{0,1:T(8,128)}, u32[]{:S(2)}, u32[]{:S(2)}) collective-permute-start(f32[512,256]{0,1:T(8,128)} %slice.157), channel_id=1, source_target_pairs={{4,0},{8,4},{12,8},{16,12},{20,16},{24,20},{28,24},{32,28},{36,32}... | collective-permute-start | bytes 1572872 | tf_op jit(solution)/shard_map/ppermute | solution.py:31
  49.3 1.1 copy-start.12
  50.4 4.4 %copy-start.19 = (f32[512,1024]{0,1:T(8,128)S(1)}, f32[512,1024]{0,1:T(8,128)}, u32[]{:S(2)}) copy-start(f32[512,1024]{0,1:T(8,128)} %copy-done.18) | copy-start | bytes 6291460
  50.4 4.4 %copy-start.20 = (f32[1,512,256]{1,2,0:T(8,128)S(1)}, f32[1,512,256]{1,2,0:T(8,128)}, u32[]{:S(2)}) copy-start(f32[1,512,256]{1,2,0:T(8,128)} %copy.87) | copy-start | bytes 1572868
  50.4 4.4 %copy-start.28 = (f32[1,512,256]{1,2,0:T(8,128)S(1)}, f32[1,512,256]{1,2,0:T(8,128)}, u32[]{:S(2)}) copy-start(f32[1,512,256]{1,2,0:T(8,128)} %copy.88) | copy-start | bytes 1572868
  54.8 2.3 %copy-start.8 = (f32[512,512]{0,1:T(8,128)S(1)}, f32[512,512]{0,1:T(8,128)}, u32[]{:S(2)}) copy-start(f32[512,512]{0,1:T(8,128)} %copy-done.7) | copy-start | bytes 3145732
  57.1 1.7 copy-start.17
  58.8 2.3 %copy-start.21 = (f32[512,256]{0,1:T(8,128)}, f32[512,256]{0,1:T(8,128)S(1)}, u32[]{:S(2)}) copy-start(f32[512,256]{0,1:T(8,128)S(1)} %fusion.44) | copy-start | bytes 1572868
  58.8 2.3 %copy-start.10 = (f32[512,512]{1,0:T(8,128)S(1)}, f32[512,512]{1,0:T(8,128)}, u32[]{:S(2)}) copy-start(f32[512,512]{1,0:T(8,128)} %copy-done.9) | copy-start | bytes 3145732
  58.8 2.3 %copy-start.24 = (f32[512,512]{0,1:T(8,128)S(1)}, f32[512,512]{0,1:T(8,128)}, u32[]{:S(2)}) copy-start(f32[512,512]{0,1:T(8,128)} %fusion.42) | copy-start | bytes 3145732
  62.1 5.5 %copy-start.1 = (f32[512,512]{0,1:T(8,128)}, f32[512,512]{0,1:T(8,128)S(1)}, u32[]{:S(2)}) copy-start(f32[512,512]{0,1:T(8,128)S(1)} %get-tuple-element.28) | copy-start | bytes 3145732
  62.1 5.5 %copy-start.3 = (f32[512,512]{0,1:T(8,128)}, f32[512,512]{0,1:T(8,128)S(1)}, u32[]{:S(2)}) copy-start(f32[512,512]{0,1:T(8,128)S(1)} %get-tuple-element.29) | copy-start | bytes 3145732
  64.6 3.0 %copy-start.5 = (f32[512,1024]{1,0:T(8,128)S(1)}, f32[512,1024]{1,0:T(8,128)}, u32[]{:S(2)}) copy-start(f32[512,1024]{1,0:T(8,128)} %fusion.9) | copy-start | bytes 6291460
  64.6 3.0 %copy-start.25 = (f32[512,512]{1,0:T(8,128)S(1)}, f32[512,512]{1,0:T(8,128)}, u32[]{:S(2)}) copy-start(f32[512,512]{1,0:T(8,128)} %fusion.11) | copy-start | bytes 3145732
  64.6 3.0 %copy-start.26 = (f32[512,512]{1,0:T(8,128)S(1)}, f32[512,512]{1,0:T(8,128)}, u32[]{:S(2)}) copy-start(f32[512,512]{1,0:T(8,128)} %fusion.10) | copy-start | bytes 3145732
  182.2 7.7 %copy-start.2 = (f32[512,512]{0,1:T(8,128)S(1)}, f32[512,512]{0,1:T(8,128)}, u32[]{:S(2)}) copy-start(f32[512,512]{0,1:T(8,128)} %copy-done.1) | copy-start | bytes 3145732
  182.2 7.7 %copy-start.4 = (f32[512,512]{0,1:T(8,128)S(1)}, f32[512,512]{0,1:T(8,128)}, u32[]{:S(2)}) copy-start(f32[512,512]{0,1:T(8,128)} %copy-done.3) | copy-start | bytes 3145732
  184.9 15.8 %all-to-all-start.3 = ((f32[4,32,1664]{2,1,0:T(8,128)}), f32[4,32,1664]{2,1,0:T(8,128)}, u32[]{:S(2)}, u32[]{:S(2)}) async-start(f32[4,32,1664]{2,1,0:T(8,128)} %bitcast.20), calls=%async_computation.3 | async-start | bytes 1703936 | tf_op jit(solution)/shard_map/all_to_all | solution.py:16
  193.4 16.5 %copy-start.22 = (f32[512,256]{0,1:T(8,128)S(1)}, f32[512,256]{0,1:T(8,128)}, u32[]{:S(2)}) copy-start(f32[512,256]{0,1:T(8,128)} %copy-done.21) | copy-start | bytes 1572868
  193.4 16.5 %collective-permute-start.3 = (f32[256,256]{0,1:T(8,128)S(1)}, f32[256,256]{0,1:T(8,128)S(1)}, u32[]{:S(2)}, u32[]{:S(2)}) collective-permute-start(f32[256,256]{0,1:T(8,128)S(1)} %get-tuple-element.35), channel_id=1, source_target_pairs={{4,0},{8,4},{12,8},{16,12},{20,16},{24,20},{28,24},{32,28},{36,32}... | collective-permute-start | bytes 786440 | tf_op jit(solution)/shard_map/ppermute | solution.py:31
  202.7 17.2 %all-to-all-start.4 = ((f32[8,4,1664]{2,1,0:T(4,128)}), f32[8,4,1664]{2,1,0:T(4,128)S(1)}, u32[]{:S(2)}, u32[]{:S(2)}) async-start(f32[8,4,1664]{2,1,0:T(4,128)} %reshape.39), calls=%async_computation.4 | async-start | bytes 425984 | tf_op jit(solution)/shard_map/all_to_all | solution.py:16

commit v6 on v3

--- a/solution.py
+++ b/solution.py
@@ -16,10 +16,13 @@
     return lax.all_to_all(block, axis, 0, 0, tiled=True).sum(axis=0)
 
 
-def reduce_to_owner(packed):
-    rows, width = packed.shape
+def owner_rows(terms):
+    rows, width = terms.shape
     sizes = [lax.axis_size(a) for a in ("y", "xl", "z", "xh", "c")]
-    block = packed.reshape(*sizes, -1, width).transpose(4, 3, 1, 0, 2, 5, 6).reshape(rows, width)
+    return terms.reshape(*sizes, -1, width).transpose(4, 3, 1, 0, 2, 5, 6).reshape(rows, width)
+
+
+def reduce_to_owner(block):
     for axis in ("c", ("xh", "xl"), "y", "z"):
         block = reduce_rows(block, axis)
     return block
@@ -120,7 +123,7 @@
     bias_terms = jnp.concatenate([first_bias, second_bias], axis=0)
     bias_cols = bias_terms.reshape(conv_terms.shape[0], -1)
     bias_cols = jnp.pad(bias_cols, ((0, 0), (0, 128 - bias_cols.shape[1])))
-    packed = jnp.concatenate([conv_terms, out_terms, bias_cols], axis=1)
+    packed = jnp.concatenate([owner_rows(conv_terms), owner_rows(out_terms), owner_rows(bias_cols)], axis=1)
     summed = reduce_to_owner(packed) * factor
     conv_width, out_width = conv_terms.shape[1], out_terms.shape[1]
     conv_grad = summed[:, :conv_width]

time: 198 us -> 196 us (0.990); the launches traced: 197 us -> 193 us
  starting transfers between devices: 25.8 us -> 23.1 us
    another operation x1 -> x0, local copies, waits for them, and re-layouts: 3.37 us -> none  [reduce_rows(): block = block.reshape(parts, block.shape[0] // parts, block.shape[1])]
    all_to_all x2, starting transfers between devices: 13.3 us -> 10.6 us  [reduce_rows(): return lax.all_to_all(block, axis, 0, 0, tiled=True).sum(axis=0)]
    reshape x2 -> x4, local copies, waits for them, and re-layouts: 17.8 us -> 18.7 us  [owner_rows(): terms.reshape(*sizes, -1, width).transpose(4, 3, 1, 0, 2, 5, 6)]
    unnamed x64 -> x70, local copies, waits for them, and re-layouts: 7.59 us -> 7.52 us
    concatenate x1 -> x3, other arithmetic: 7.65 us -> 7.65 us  [the longest x1 3.63 us: local(): jnp.concatenate([owner_rows(conv_terms), owner_rows(out_terms), owner_row...]
where the time goes in v6:
time: 196 us; the launch traced here: 193 us
  blocking collectives  55.8 us (28%)
  local copies, waits for them, and re-layouts  33.5 us (17%)
  waiting for transfers between devices  32.9 us (17%)
  matrix products  27.6 us (14%)
  starting transfers between devices  23.1 us (12%)
  other arithmetic  19.1 us (10%)
    all_to_all x2, blocking collectives, reduce_rows(): return lax.all_to_all(block, axis, 0, 0, tiled=True).sum(axis=0)  55.8 us
    ppermute x4, waiting for transfers between devices, from_behind(): return lax.ppermute(block, axis, route)  21.2 us
    dot_general x10, matrix products, contract(): lax.dot_general(left, right, (((left_dim,), (right_dim,)), ((), ())), pre...  20.6 us
    reshape x4, local copies, waits for them, and re-layouts, owner_rows(): terms.reshape(*sizes, -1, width).transpose(4, 3, 1, 0, 2, 5, 6)  18.7 us
    ppermute x4, starting transfers between devices, from_behind(): return lax.ppermute(block, axis, route)  12.5 us
    all_to_all x2, waiting for transfers between devices, reduce_rows(): return lax.all_to_all(block, axis, 0, 0, tiled=True).sum(axis=0)  11.8 us
    all_to_all x2, starting transfers between devices, reduce_rows(): return lax.all_to_all(block, axis, 0, 0, tiled=True).sum(axis=0)  10.6 us
    reduce_sum x4, other arithmetic, reduce_rows(): return lax.all_to_all(block, axis, 0, 0, tiled=True).sum(axis=0)  8.27 us
  transfers between devices with their start and end apart: 6, of which 4 were waited for; matrix products, arithmetic and copies ran while one was open for 12% of the time, Pallas kernels for 0%

profile of v6, /device:TPU:10, one launch (start us, length us, event | category | flops | bytes accessed | tf_op | source)
XLA Modules:
  0.0 193.1 jit_solution(9302548743642285631)
XLA Ops:
  0.6 1.3 copy.97
  2.0 0.0 copy-start.16
  2.0 4.0 %collective-permute-start = (f32[256,256]{0,1:T(8,128)S(1)}, f32[256,256]{0,1:T(8,128)S(1)}, u32[]{:S(2)}, u32[]{:S(2)}) collective-permute-start(f32[256,256]{0,1:T(8,128)S(1)} %get-tuple-element.36), channel_id=1, source_target_pairs={{0,4},{4,8},{8,12},{12,16},{16,20},{20,24},{24,28},{28,32},{32,36}... | collective-permute-start | bytes 786440 | tf_op jit(solution)/shard_map/ppermute | solution.py:34
  6.0 0.0 copy-start.32
  6.0 2.3 %fusion.32 = f32[512,1024]{0,1:T(8,128)S(1)} fusion(f32[2,512,1024]{2,1,0:T(8,128)} %param.9, f32[1,512,256]{2,1,0:T(8,128)S(1)} %copy-done.15), kind=kOutput, calls=%fused_computation.48 | convolution fusion | flops 805306368 | bytes 3670016 | tf_op jit(solution)/shard_map/dot_general | solution.py:38
  8.3 0.0 copy-start
  8.3 0.2 slice_bitcast_fusion
  8.5 7.7 %collective-permute-done = f32[256,256]{0,1:T(8,128)S(1)} collective-permute-done((f32[256,256]{0,1:T(8,128)S(1)}, f32[256,256]{0,1:T(8,128)S(1)}, u32[]{:S(2)}, u32[]{:S(2)}) %collective-permute-start) | collective-permute-done | bytes 262176 | tf_op jit(solution)/shard_map/ppermute | solution.py:34
  16.2 1.4 add_add_fusion.1
  17.6 0.0 copy-start.7
  17.6 0.9 convolution_add_fusion.2
  18.5 0.3 copy-done.17
  18.9 1.9 collective-permute-start.1
  20.8 0.6 fusion.46
  21.4 1.0 fusion.29
  22.5 13.5 %collective-permute-done.1 = f32[512,256]{0,1:T(8,128)S(1)} collective-permute-done((f32[512,256]{0,1:T(8,128)S(1)}, f32[512,256]{0,1:T(8,128)S(1)}, u32[]{:S(2)}, u32[]{:S(2)}) %collective-permute-start.1) | collective-permute-done | bytes 524320 | tf_op jit(solution)/shard_map/ppermute | solution.py:34
  36.0 1.4 add_add_fusion
  37.4 1.1 subtract_multiply_fusion.3
  38.5 0.3 copy-done.19
  38.7 1.9 fusion.2
  40.6 1.0 copy-done.8
  41.7 0.8 slice.157
  42.5 2.1 %collective-permute-start.2 = (f32[512,256]{0,1:T(8,128)}, f32[512,256]{0,1:T(8,128)}, u32[]{:S(2)}, u32[]{:S(2)}) collective-permute-start(f32[512,256]{0,1:T(8,128)} %slice.157), channel_id=1, source_target_pairs={{4,0},{8,4},{12,8},{16,12},{20,16},{24,20},{28,24},{32,28},{36,32}... | collective-permute-start | bytes 1572872 | tf_op jit(solution)/shard_map/ppermute | solution.py:34
  44.6 1.7 fusion.42
  46.3 2.0 %copy.95 = f32[1,512,256]{1,2,0:T(8,128)} copy(f32[1,512,256]{2,1,0:T(8,128)} %param.7) | data formatting | bytes 1048576 | tf_op args[1]
  48.3 1.0 copy.96
  49.4 0.2 fusion.8
  49.6 0.9 concatenate.61
  50.5 4.4 %fusion.9 = f32[512,1024]{1,0:T(8,128)} fusion(f32[512,512]{0,1:T(8,128)S(1)} %get-tuple-element.31, f32[512,512]{0,1:T(8,128)S(1)} %get-tuple-element.30, f32[512,256]{0,1:T(8,128)S(1)} %copy-done.13, f32[512,256]{0,1:T(8,128)} %copy-done.14), kind=kOutput, calls=%fused_computation.18 | convolution fusion | flops 1611399168 | bytes 5242880 | tf_op jit(solution)/shard_map/dot_general | solution.py:42
  54.9 2.3 %fusion.11 = f32[512,512]{1,0:T(8,128)} fusion(f32[512,256]{0,1:T(8,128)S(1)} %bitcast.71, f32[512,256]{0,1:T(8,128)S(1)} %bitcast.69, f32[512,1024]{0,1:T(8,128)S(1)} %copy-done.20), kind=kOutput, calls=%fused_computation.23 | convolution fusion | flops 806617088 | bytes 4194304 | tf_op jit(solution)/shard_map/dot_general | solution.py:42
  57.2 1.3 fusion.44
  58.5 0.4 copy-done.18
  58.9 2.3 %fusion.10 = f32[512,512]{1,0:T(8,128)} fusion(f32[512,256]{0,1:T(8,128)S(1)} %bitcast.72, f32[512,256]{0,1:T(8,128)S(1)} %fusion.44, f32[512,1024]{0,1:T(8,128)S(1)} %copy-done.18), kind=kOutput, calls=%fused_computation.22 | convolution fusion | flops 806617088 | bytes 4194304 | tf_op jit(solution)/shard_map/dot_general | solution.py:42
  61.2 1.0 subtract_multiply_fusion.1
  62.3 0.2 fusion.6
  62.5 1.2 concatenate.60
  63.7 1.2 select_maximum_fusion
  65.0 1.1 copy.109
  66.1 1.5 pad_maximum_fusion.4
  67.6 2.8 %reshape.49 = f32[4,2,8,2,2,4,512]{6,5,4,3,2,1,0:T(4,128)} reshape(f32[1024,512]{1,0:T(8,128)} %pad_maximum_fusion.4) | data formatting | bytes 4194304 | tf_op jit(solution)/shard_map/reshape | solution.py:22
  70.5 4.1 %copy.108 = f32[4,2,8,2,2,4,512]{6,4,5,2,0,1,3:T(2,128)} copy(f32[4,2,8,2,2,4,512]{6,5,4,3,2,1,0:T(4,128)} %reshape.49) | data formatting | bytes 4194304 | tf_op jit(solution)/shard_map/reshape | solution.py:22
  74.6 1.9 fusion.7
  76.5 2.5 %pad_maximum_fusion.1 = f32[1024,1024]{1,0:T(8,128)} fusion(f32[512,1024]{1,0:T(8,128)S(1)} %copy-done.5, f32[512,1024]{1,0:T(8,128)S(1)} %fusion.7), kind=kLoop, calls=%fused_computation.1 | loop fusion | flops 1048576 | bytes 8388608 | tf_op jit(solution)/shard_map/concatenate | solution.py:121
  79.0 5.3 %reshape.48 = f32[4,2,8,2,2,4,1024]{6,5,4,3,2,1,0:T(4,128)} reshape(f32[1024,1024]{1,0:T(8,128)} %pad_maximum_fusion.1) | data formatting | bytes 8388608 | tf_op jit(solution)/shard_map/reshape | solution.py:22
  84.3 6.4 %copy.107 = f32[4,2,8,2,2,4,1024]{6,4,5,2,0,1,3:T(2,128)S(1)} copy(f32[4,2,8,2,2,4,1024]{6,5,4,3,2,1,0:T(4,128)} %reshape.48) | data formatting | bytes 8388608 | tf_op jit(solution)/shard_map/reshape | solution.py:22
  90.7 3.6 %pad_maximum_fusion = f32[2,512,1664]{2,0,1:T(2,128)S(1)} fusion(f32[2,512,128]{2,0,1:T(2,128)S(1)} %bitcast.70, f32[2,512,512]{2,0,1:T(2,128)S(1)} %bitcast.66, f32[2,512,1024]{2,0,1:T(2,128)S(1)} %bitcast.64), kind=kLoop, calls=%fused_computation | loop fusion | flops 3407872 | bytes 13631488 | tf_op jit(solution)/shard_map/concatenate | solution.py:126
  94.4 0.4 copy.110
  94.8 10.4 %all_to_all.20 = f32[2,512,1664]{2,1,0:T(8,128)} all-to-all(f32[2,512,1664]{2,1,0:T(8,128)S(1)} %copy.110), channel_id=1, replica_groups=mesh['y'=4,'xl'=2,'z'=8,'xh'=2,'c'=2] {'c'}, dimensions={0} | all-to-all | bytes 13631488 | tf_op jit(solution)/shard_map/all_to_all | solution.py:16
  105.2 3.7 %reduce_sum.56 = f32[512,1664]{1,0:T(8,128)S(1)} reduce(f32[2,512,1664]{2,1,0:T(8,128)} %all_to_all.20, f32[]{:T(128)} %constant.1.clone.1), dimensions={0}, to_apply=%region_2.3 | reduce | flops 851968 | bytes 10223620 | tf_op jit(solution)/shard_map/reduce_sum | solution.py:16
  109.0 45.4 %all_to_all.21 = f32[4,128,1664]{2,1,0:T(8,128)} all-to-all(f32[4,128,1664]{2,1,0:T(8,128)S(1)} %bitcast.65), channel_id=1, replica_groups=mesh['y'=4,'xl'=2,'z'=8,'xh'=2,'c'=2] {'xh','xl'}, dimensions={0} | all-to-all | bytes 6815744 | tf_op jit(solution)/shard_map/all_to_all | solution.py:16
  154.4 3.3 %reduce_sum.57 = f32[128,1664]{1,0:T(8,128)} reduce(f32[4,128,1664]{2,1,0:T(8,128)} %all_to_all.21, f32[]{:T(128)} %constant.1.clone.1), dimensions={0}, to_apply=%region_3.4 | reduce | flops 638976 | bytes 4259844 | tf_op jit(solution)/shard_map/reduce_sum | solution.py:16
  157.7 5.0 %all-to-all-start.2 = ((f32[4,32,1664]{2,1,0:T(8,128)}), f32[4,32,1664]{2,1,0:T(8,128)}, u32[]{:S(2)}, u32[]{:S(2)}) async-start(f32[4,32,1664]{2,1,0:T(8,128)} %bitcast.24), calls=%async_computation.2 | async-start | bytes 1703936 | tf_op jit(solution)/shard_map/all_to_all | solution.py:16
  162.7 3.4 %fusion = f32[512,512]{0,1:T(8,128)S(1)} fusion(f32[2,512,1024]{2,1,0:T(8,128)} %param.9, f32[512,512]{0,1:T(8,128)S(1)} %copy-done.4, f32[512,512]{0,1:T(8,128)S(1)} %copy-done.2), kind=kOutput, calls=%fused_computation.5 | convolution fusion | flops 1611137024 | bytes 5242880 | tf_op jit(solution)/shard_map/dot_general | solution.py:42
  166.2 4.6 %collective-permute-start.3 = (f32[256,256]{0,1:T(8,128)S(1)}, f32[256,256]{0,1:T(8,128)S(1)}, u32[]{:S(2)}, u32[]{:S(2)}) collective-permute-start(f32[256,256]{0,1:T(8,128)S(1)} %get-tuple-element.35), channel_id=1, source_target_pairs={{4,0},{8,4},{12,8},{16,12},{20,16},{24,20},{28,24},{32,28},{36,32}... | collective-permute-start | bytes 786440 | tf_op jit(solution)/shard_map/ppermute | solution.py:34
  170.7 2.9 %all-to-all-done.2 = f32[4,32,1664]{2,1,0:T(8,128)} async-done(((f32[4,32,1664]{2,1,0:T(8,128)}), f32[4,32,1664]{2,1,0:T(8,128)}, u32[]{:S(2)}, u32[]{:S(2)}) %all-to-all-start.2) | async-done | bytes 852000 | tf_op jit(solution)/shard_map/all_to_all | solution.py:16
  173.7 1.2 reduce_sum.58
  174.9 0.7 reshape.53
  175.6 5.6 %all-to-all-start.3 = ((f32[8,4,1664]{2,1,0:T(4,128)}), f32[8,4,1664]{2,1,0:T(4,128)S(1)}, u32[]{:S(2)}, u32[]{:S(2)}) async-start(f32[8,4,1664]{2,1,0:T(4,128)} %reshape.53), calls=%async_computation.3 | async-start | bytes 425984 | tf_op jit(solution)/shard_map/all_to_all | solution.py:16
  181.3 0.1 fusion.41
  181.4 1.0 copy.112
  182.4 8.8 %all-to-all-done.3 = f32[8,4,1664]{2,1,0:T(4,128)S(1)} async-done(((f32[8,4,1664]{2,1,0:T(4,128)}), f32[8,4,1664]{2,1,0:T(4,128)S(1)}, u32[]{:S(2)}, u32[]{:S(2)}) %all-to-all-start.3) | async-done | bytes 213024 | tf_op jit(solution)/shard_map/all_to_all | solution.py:16
  191.3 0.6 slice.162
  191.9 0.6 slice.163
  192.5 0.6 reshape.54
  (66 shorter events, 0.3 us)
Async XLA Ops:
  0.6 5.3 %copy-start.15 = (f32[1,512,256]{2,1,0:T(8,128)S(1)}, f32[1,512,256]{2,1,0:T(8,128)}, u32[]{:S(2)}) copy-start(f32[1,512,256]{2,1,0:T(8,128)} %param.6) | copy-start | bytes 1572868
  2.0 6.3 %copy-start.16 = (f32[2,512,512]{2,1,0:T(8,128)S(1)}, f32[2,512,512]{2,1,0:T(8,128)}, u32[]{:S(2)}) copy-start(f32[2,512,512]{2,1,0:T(8,128)} %param.11) | copy-start | bytes 6291460
  2.0 14.2 %collective-permute-start = (f32[256,256]{0,1:T(8,128)S(1)}, f32[256,256]{0,1:T(8,128)S(1)}, u32[]{:S(2)}, u32[]{:S(2)}) collective-permute-start(f32[256,256]{0,1:T(8,128)S(1)} %get-tuple-element.36), channel_id=1, source_target_pairs={{0,4},{4,8},{8,12},{12,16},{16,20},{20,24},{24,28},{28,32},{32,36}... | collective-permute-start | bytes 786440 | tf_op jit(solution)/shard_map/ppermute | solution.py:34
  6.0 2.5 %copy-start.32 = (f32[2,1024]{1,0:T(2,128)S(1)}, f32[2,1024]{1,0:T(2,128)}, u32[]{:S(2)}) copy-start(f32[2,1024]{1,0:T(2,128)} %param.10) | copy-start | bytes 24580
  8.3 7.9 %copy-start = (f32[2,512,1024]{2,1,0:T(8,128)S(1)}, f32[2,512,1024]{2,1,0:T(8,128)}, u32[]{:S(2)}) copy-start(f32[2,512,1024]{2,1,0:T(8,128)} %param.9) | copy-start | bytes 12582916
  8.5 36.1 %copy-start.10 = (f32[512,512]{1,0:T(8,128)}, f32[512,512]{1,0:T(8,128)S(1)}, u32[]{:S(2)}) copy-start(f32[512,512]{1,0:T(8,128)S(1)} %get-tuple-element.32) | copy-start | bytes 3145732
  16.2 1.4 copy-start.25
  17.6 1.3 copy-start.17
  17.6 3.2 %copy-start.7 = (f32[1,512,256]{2,1,0:T(8,128)S(1)}, f32[1,512,256]{2,1,0:T(8,128)}, u32[]{:S(2)}) copy-start(f32[1,512,256]{2,1,0:T(8,128)} %param.8) | copy-start | bytes 1572868
  18.9 3.6 %copy-start.12 = (f32[512,256]{0,1:T(8,128)}, f32[512,256]{0,1:T(8,128)S(1)}, u32[]{:S(2)}) copy-start(f32[512,256]{0,1:T(8,128)S(1)} %convolution_add_fusion.2) | copy-start | bytes 1572868
  18.9 17.1 %collective-permute-start.1 = (f32[512,256]{0,1:T(8,128)S(1)}, f32[512,256]{0,1:T(8,128)S(1)}, u32[]{:S(2)}, u32[]{:S(2)}) collective-permute-start(f32[512,256]{0,1:T(8,128)S(1)} %convolution_add_fusion.2), channel_id=1, source_target_pairs={{0,4},{4,8},{8,12},{12,16},{16,20},{20,24},{24,28},{28,32},{32,36}... | collective-permute-start | bytes 1572872 | tf_op jit(solution)/shard_map/ppermute | solution.py:34
  36.0 1.4 copy-start.14
  36.0 1.4 copy-start.30
  37.4 1.4 copy-start.19
  40.6 1.1 copy-start.8
  42.5 14.7 %collective-permute-start.2 = (f32[512,256]{0,1:T(8,128)}, f32[512,256]{0,1:T(8,128)}, u32[]{:S(2)}, u32[]{:S(2)}) collective-permute-start(f32[512,256]{0,1:T(8,128)} %slice.157), channel_id=1, source_target_pairs={{4,0},{8,4},{12,8},{16,12},{20,16},{24,20},{28,24},{32,28},{36,32}... | collective-permute-start | bytes 1572872 | tf_op jit(solution)/shard_map/ppermute | solution.py:34
  49.4 1.1 copy-start.13
  50.5 4.4 %copy-start.20 = (f32[512,1024]{0,1:T(8,128)S(1)}, f32[512,1024]{0,1:T(8,128)}, u32[]{:S(2)}) copy-start(f32[512,1024]{0,1:T(8,128)} %copy-done.19) | copy-start | bytes 6291460
  50.5 4.4 %copy-start.21 = (f32[1,512,256]{1,2,0:T(8,128)S(1)}, f32[1,512,256]{1,2,0:T(8,128)}, u32[]{:S(2)}) copy-start(f32[1,512,256]{1,2,0:T(8,128)} %copy.95) | copy-start | bytes 1572868
  50.5 4.4 %copy-start.31 = (f32[1,512,256]{1,2,0:T(8,128)S(1)}, f32[1,512,256]{1,2,0:T(8,128)}, u32[]{:S(2)}) copy-start(f32[1,512,256]{1,2,0:T(8,128)} %copy.96) | copy-start | bytes 1572868
  54.9 2.3 %copy-start.9 = (f32[512,512]{0,1:T(8,128)S(1)}, f32[512,512]{0,1:T(8,128)}, u32[]{:S(2)}) copy-start(f32[512,512]{0,1:T(8,128)} %copy-done.8) | copy-start | bytes 3145732
  57.2 1.7 copy-start.18
  58.9 2.3 %copy-start.22 = (f32[512,256]{0,1:T(8,128)}, f32[512,256]{0,1:T(8,128)S(1)}, u32[]{:S(2)}) copy-start(f32[512,256]{0,1:T(8,128)S(1)} %fusion.44) | copy-start | bytes 1572868
  58.9 2.3 %copy-start.11 = (f32[512,512]{1,0:T(8,128)S(1)}, f32[512,512]{1,0:T(8,128)}, u32[]{:S(2)}) copy-start(f32[512,512]{1,0:T(8,128)} %copy-done.10) | copy-start | bytes 3145732
  58.9 2.3 %copy-start.27 = (f32[512,512]{0,1:T(8,128)S(1)}, f32[512,512]{0,1:T(8,128)}, u32[]{:S(2)}) copy-start(f32[512,512]{0,1:T(8,128)} %fusion.42) | copy-start | bytes 3145732
  62.3 12.3 %copy-start.1 = (f32[512,512]{0,1:T(8,128)}, f32[512,512]{0,1:T(8,128)S(1)}, u32[]{:S(2)}) copy-start(f32[512,512]{0,1:T(8,128)S(1)} %get-tuple-element.28) | copy-start | bytes 3145732
  62.3 12.3 %copy-start.3 = (f32[512,512]{0,1:T(8,128)}, f32[512,512]{0,1:T(8,128)S(1)}, u32[]{:S(2)}) copy-start(f32[512,512]{0,1:T(8,128)S(1)} %get-tuple-element.29) | copy-start | bytes 3145732
  63.7 2.4 %copy-start.28 = (f32[512,512]{1,0:T(8,128)S(1)}, f32[512,512]{1,0:T(8,128)}, u32[]{:S(2)}) copy-start(f32[512,512]{1,0:T(8,128)} %fusion.11) | copy-start | bytes 3145732
  63.7 2.4 %copy-start.29 = (f32[512,512]{1,0:T(8,128)S(1)}, f32[512,512]{1,0:T(8,128)}, u32[]{:S(2)}) copy-start(f32[512,512]{1,0:T(8,128)} %fusion.10) | copy-start | bytes 3145732
  70.5 4.1 %copy-start.26 = (f32[256,256]{0,1:T(8,128)S(1)}, f32[256,256]{0,1:T(8,128)}, u32[]{:S(2)}) copy-start(f32[256,256]{0,1:T(8,128)} %copy-done.25) | copy-start | bytes 786436
  74.6 1.9 copy-start.5
  84.3 6.4 %copy-start.6 = (f32[4,2,8,2,2,4,512]{6,4,5,2,0,1,3:T(2,128)S(1)}, f32[4,2,8,2,2,4,512]{6,4,5,2,0,1,3:T(2,128)}, u32[]{:S(2)}) copy-start(f32[4,2,8,2,2,4,512]{6,4,5,2,0,1,3:T(2,128)} %copy.108) | copy-start | bytes 6291460
  84.3 6.4 %copy-start.24 = (f32[2,2,2,4,8,4,128]{6,0,5,4,3,2,1:T(2,128)S(1)}, f32[2,2,2,4,8,4,128]{6,0,5,4,3,2,1:T(2,128)}, u32[]{:S(2)}) copy-start(f32[2,2,2,4,8,4,128]{6,0,5,4,3,2,1:T(2,128)} %copy.109) | copy-start | bytes 1572868
  154.4 8.3 %copy-start.2 = (f32[512,512]{0,1:T(8,128)S(1)}, f32[512,512]{0,1:T(8,128)}, u32[]{:S(2)}) copy-start(f32[512,512]{0,1:T(8,128)} %copy-done.1) | copy-start | bytes 3145732
  154.4 8.3 %copy-start.4 = (f32[512,512]{0,1:T(8,128)S(1)}, f32[512,512]{0,1:T(8,128)}, u32[]{:S(2)}) copy-start(f32[512,512]{0,1:T(8,128)} %copy-done.3) | copy-start | bytes 3145732
  157.7 16.0 %all-to-all-start.2 = ((f32[4,32,1664]{2,1,0:T(8,128)}), f32[4,32,1664]{2,1,0:T(8,128)}, u32[]{:S(2)}, u32[]{:S(2)}) async-start(f32[4,32,1664]{2,1,0:T(8,128)} %bitcast.24), calls=%async_computation.2 | async-start | bytes 1703936 | tf_op jit(solution)/shard_map/all_to_all | solution.py:16
  166.1 15.1 %copy-start.23 = (f32[512,256]{0,1:T(8,128)S(1)}, f32[512,256]{0,1:T(8,128)}, u32[]{:S(2)}) copy-start(f32[512,256]{0,1:T(8,128)} %copy-done.22) | copy-start | bytes 1572868
  166.2 15.1 %collective-permute-start.3 = (f32[256,256]{0,1:T(8,128)S(1)}, f32[256,256]{0,1:T(8,128)S(1)}, u32[]{:S(2)}, u32[]{:S(2)}) collective-permute-start(f32[256,256]{0,1:T(8,128)S(1)} %get-tuple-element.35), channel_id=1, source_target_pairs={{4,0},{8,4},{12,8},{16,12},{20,16},{24,20},{28,24},{32,28},{36,32}... | collective-permute-start | bytes 786440 | tf_op jit(solution)/shard_map/ppermute | solution.py:34
  175.6 15.6 %all-to-all-start.3 = ((f32[8,4,1664]{2,1,0:T(4,128)}), f32[8,4,1664]{2,1,0:T(4,128)S(1)}, u32[]{:S(2)}, u32[]{:S(2)}) async-start(f32[8,4,1664]{2,1,0:T(4,128)} %reshape.53), calls=%async_computation.3 | async-start | bytes 425984 | tf_op jit(solution)/shard_map/all_to_all | solution.py:16

commit v7 on v6

--- a/solution.py
+++ b/solution.py
@@ -121,9 +121,9 @@
     conv_terms = jnp.concatenate([first_conv_output, second_conv_output], axis=0)
     out_terms = jnp.concatenate([first_output, second_output], axis=0)
     bias_terms = jnp.concatenate([first_bias, second_bias], axis=0)
-    bias_cols = bias_terms.reshape(conv_terms.shape[0], -1)
+    bias_cols = owner_rows(bias_terms.reshape(conv_terms.shape[0], -1))
     bias_cols = jnp.pad(bias_cols, ((0, 0), (0, 128 - bias_cols.shape[1])))
-    packed = jnp.concatenate([owner_rows(conv_terms), owner_rows(out_terms), owner_rows(bias_cols)], axis=1)
+    packed = jnp.concatenate([owner_rows(conv_terms), owner_rows(out_terms), bias_cols], axis=1)
     summed = reduce_to_owner(packed) * factor
     conv_width, out_width = conv_terms.shape[1], out_terms.shape[1]
     conv_grad = summed[:, :conv_width]

time: 196 us -> 195 us (level)
  starting transfers between devices: 23.1 us -> 18.8 us
  local copies, waits for them, and re-layouts: 33.5 us -> 36.4 us
  waiting for transfers between devices: 32.9 us -> 34.9 us
    all_to_all x2, starting transfers between devices: 10.6 us -> 8.42 us  [reduce_rows(): return lax.all_to_all(block, axis, 0, 0, tiled=True).sum(axis=0)]
    ppermute x4, starting transfers between devices: 12.5 us -> 10.4 us  [from_behind(): return lax.ppermute(block, axis, route)]
    all_to_all x2, waiting for transfers between devices: 11.8 us -> 13.8 us  [reduce_rows(): return lax.all_to_all(block, axis, 0, 0, tiled=True).sum(axis=0)]
    unnamed x70 -> x71, local copies, waits for them, and re-layouts: 7.52 us -> 9.42 us
    concatenate x2 -> x1, other arithmetic: 4.86 us -> 3.63 us  [local(): jnp.concatenate([owner_rows(conv_terms), owner_rows(out_terms), bias_cols...]
  transfers between devices with their start and end apart: 6 -> 6, of which waited for: 4 -> 4; matrix products, arithmetic and copies ran while one was open for 12% -> 13% of each run, Pallas kernels for 0% -> 0%
where the time goes in v7:
time: 195 us; the launch traced here: 193 us
  blocking collectives  55.8 us (29%)
  local copies, waits for them, and re-layouts  36.4 us (19%)
  waiting for transfers between devices  34.9 us (18%)
  matrix products  27.6 us (14%)
  starting transfers between devices  18.8 us (10%)
  other arithmetic  17.9 us (9%)
    all_to_all x2, blocking collectives, reduce_rows(): return lax.all_to_all(block, axis, 0, 0, tiled=True).sum(axis=0)  55.8 us
    ppermute x4, waiting for transfers between devices, from_behind(): return lax.ppermute(block, axis, route)  21.2 us
    dot_general x10, matrix products, contract(): lax.dot_general(left, right, (((left_dim,), (right_dim,)), ((), ())), pre...  20.6 us
    reshape x4, local copies, waits for them, and re-layouts, owner_rows(): terms.reshape(*sizes, -1, width).transpose(4, 3, 1, 0, 2, 5, 6)  18.7 us
    all_to_all x2, waiting for transfers between devices, reduce_rows(): return lax.all_to_all(block, axis, 0, 0, tiled=True).sum(axis=0)  13.8 us
    ppermute x4, starting transfers between devices, from_behind(): return lax.ppermute(block, axis, route)  10.4 us
    unnamed x71, local copies, waits for them, and re-layouts  9.42 us
    all_to_all x2, starting transfers between devices, reduce_rows(): return lax.all_to_all(block, axis, 0, 0, tiled=True).sum(axis=0)  8.42 us
  transfers between devices with their start and end apart: 6, of which 4 were waited for; matrix products, arithmetic and copies ran while one was open for 13% of the time, Pallas kernels for 0%

profile of v7, /device:TPU:10, one launch (start us, length us, event | category | flops | bytes accessed | tf_op | source)
XLA Modules:
  0.0 192.5 jit_solution(6228869087715659554)
XLA Ops:
  0.6 1.3 copy.123
  2.0 4.0 %collective-permute-start = (f32[256,256]{0,1:T(8,128)S(1)}, f32[256,256]{0,1:T(8,128)S(1)}, u32[]{:S(2)}, u32[]{:S(2)}) collective-permute-start(f32[256,256]{0,1:T(8,128)S(1)} %get-tuple-element.40), channel_id=1, source_target_pairs={{0,4},{4,8},{8,12},{12,16},{16,20},{20,24},{24,28},{28,32},{32,36}... | collective-permute-start | bytes 786440 | tf_op jit(solution)/shard_map/ppermute | solution.py:34
  6.0 2.3 %fusion.32 = f32[512,1024]{0,1:T(8,128)S(1)} fusion(f32[2,512,1024]{2,1,0:T(8,128)} %param.9, f32[1,512,256]{2,1,0:T(8,128)S(1)} %copy-done.15), kind=kOutput, calls=%fused_computation.48 | convolution fusion | flops 805306368 | bytes 3670016 | tf_op jit(solution)/shard_map/dot_general | solution.py:38
  8.3 0.2 slice_bitcast_fusion
  8.5 7.7 %collective-permute-done = f32[256,256]{0,1:T(8,128)S(1)} collective-permute-done((f32[256,256]{0,1:T(8,128)S(1)}, f32[256,256]{0,1:T(8,128)S(1)}, u32[]{:S(2)}, u32[]{:S(2)}) %collective-permute-start) | collective-permute-done | bytes 262176 | tf_op jit(solution)/shard_map/ppermute | solution.py:34
  16.2 1.4 add_add_fusion.1
  17.6 0.9 convolution_add_fusion.2
  18.5 0.3 copy-done.17
  18.9 1.9 collective-permute-start.1
  20.8 0.6 fusion.46
  21.4 1.0 fusion.29
  22.5 13.5 %collective-permute-done.1 = f32[512,256]{0,1:T(8,128)S(1)} collective-permute-done((f32[512,256]{0,1:T(8,128)S(1)}, f32[512,256]{0,1:T(8,128)S(1)}, u32[]{:S(2)}, u32[]{:S(2)}) %collective-permute-start.1) | collective-permute-done | bytes 524320 | tf_op jit(solution)/shard_map/ppermute | solution.py:34
  36.0 1.4 add_add_fusion
  37.4 1.1 subtract_multiply_fusion.3
  38.5 0.3 copy-done.19
  38.7 1.9 fusion.2
  40.6 1.0 copy-done.8
  41.7 0.8 slice.157
  42.5 2.1 %collective-permute-start.2 = (f32[512,256]{0,1:T(8,128)}, f32[512,256]{0,1:T(8,128)}, u32[]{:S(2)}, u32[]{:S(2)}) collective-permute-start(f32[512,256]{0,1:T(8,128)} %slice.157), channel_id=1, source_target_pairs={{4,0},{8,4},{12,8},{16,12},{20,16},{24,20},{28,24},{32,28},{36,32}... | collective-permute-start | bytes 1572872 | tf_op jit(solution)/shard_map/ppermute | solution.py:34
  44.6 1.7 fusion.42
  46.3 2.0 %copy.121 = f32[1,512,256]{1,2,0:T(8,128)} copy(f32[1,512,256]{2,1,0:T(8,128)} %param.7) | data formatting | bytes 1048576 | tf_op args[1]
  48.3 1.0 copy.122
  49.4 0.2 fusion.8
  49.6 1.0 concatenate.61
  50.6 2.0 %copy.136 = f32[2,2,8,2,2,4,2]{2,5,6,4,3,1,0:T(4,128)} copy(f32[2,2,8,2,2,4,2]{6,5,4,3,2,1,0:T(4,128)} %concatenate.61) | data formatting | bytes 8192 | tf_op jit(solution)/shard_map/concatenate | solution.py:123
  52.6 4.4 %fusion.9 = f32[512,1024]{1,0:T(8,128)} fusion(f32[512,512]{0,1:T(8,128)S(1)} %get-tuple-element.35, f32[512,512]{0,1:T(8,128)S(1)} %get-tuple-element.34, f32[512,256]{0,1:T(8,128)S(1)} %copy-done.13, f32[512,256]{0,1:T(8,128)} %copy-done.14), kind=kOutput, calls=%fused_computation.18 | convolution fusion | flops 1611399168 | bytes 5242880 | tf_op jit(solution)/shard_map/dot_general | solution.py:42
  57.0 2.3 %fusion.11 = f32[512,512]{1,0:T(8,128)} fusion(f32[512,256]{0,1:T(8,128)S(1)} %bitcast.71, f32[512,256]{0,1:T(8,128)S(1)} %bitcast.70, f32[512,1024]{0,1:T(8,128)S(1)} %copy-done.20), kind=kOutput, calls=%fused_computation.23 | convolution fusion | flops 806617088 | bytes 4194304 | tf_op jit(solution)/shard_map/dot_general | solution.py:42
  59.3 1.3 fusion.44
  60.6 0.4 copy-done.18
  61.0 2.3 %fusion.10 = f32[512,512]{1,0:T(8,128)} fusion(f32[512,256]{0,1:T(8,128)S(1)} %bitcast.72, f32[512,256]{0,1:T(8,128)S(1)} %fusion.44, f32[512,1024]{0,1:T(8,128)S(1)} %copy-done.18), kind=kOutput, calls=%fused_computation.22 | convolution fusion | flops 806617088 | bytes 4194304 | tf_op jit(solution)/shard_map/dot_general | solution.py:42
  63.4 1.0 subtract_multiply_fusion.1
  64.4 0.2 fusion.6
  64.7 0.3 concatenate.60
  65.0 0.5 copy.135
  65.5 0.8 copy.150
  66.4 0.4 copy.139
  66.8 0.8 copy-done.27
  67.5 0.3 copy-done.28
  67.9 1.5 pad_maximum_fusion.4
  69.4 2.8 %reshape.46 = f32[4,2,8,2,2,4,512]{6,5,4,3,2,1,0:T(4,128)} reshape(f32[1024,512]{1,0:T(8,128)} %pad_maximum_fusion.4) | data formatting | bytes 4194304 | tf_op jit(solution)/shard_map/reshape | solution.py:22
  72.2 4.1 %copy.134 = f32[4,2,8,2,2,4,512]{6,4,5,2,0,1,3:T(2,128)} copy(f32[4,2,8,2,2,4,512]{6,5,4,3,2,1,0:T(4,128)} %reshape.46) | data formatting | bytes 4194304 | tf_op jit(solution)/shard_map/reshape | solution.py:22
  76.4 1.9 fusion.7
  78.3 2.5 %pad_maximum_fusion.1 = f32[1024,1024]{1,0:T(8,128)} fusion(f32[512,1024]{1,0:T(8,128)S(1)} %copy-done.5, f32[512,1024]{1,0:T(8,128)S(1)} %fusion.7), kind=kLoop, calls=%fused_computation.1 | loop fusion | flops 1048576 | bytes 8388608 | tf_op jit(solution)/shard_map/concatenate | solution.py:121
  80.8 5.3 %reshape.45 = f32[4,2,8,2,2,4,1024]{6,5,4,3,2,1,0:T(4,128)} reshape(f32[1024,1024]{1,0:T(8,128)} %pad_maximum_fusion.1) | data formatting | bytes 8388608 | tf_op jit(solution)/shard_map/reshape | solution.py:22
  86.0 6.4 %copy.133 = f32[4,2,8,2,2,4,1024]{6,4,5,2,0,1,3:T(2,128)S(1)} copy(f32[4,2,8,2,2,4,1024]{6,5,4,3,2,1,0:T(4,128)} %reshape.45) | data formatting | bytes 8388608 | tf_op jit(solution)/shard_map/reshape | solution.py:22
  92.5 3.6 %pad_maximum_fusion = f32[2,512,1664]{2,0,1:T(2,128)S(1)} fusion(f32[2,512,128]{2,0,1:T(2,128)S(1)} %copy.139, f32[2,512,512]{2,0,1:T(2,128)S(1)} %bitcast.66, f32[2,512,1024]{2,0,1:T(2,128)S(1)} %bitcast.64), kind=kLoop, calls=%fused_computation | loop fusion | flops 3407872 | bytes 13631488 | tf_op jit(solution)/shard_map/concatenate | solution.py:126
  96.1 0.4 copy.140
  96.6 10.4 %all_to_all.20 = f32[2,512,1664]{2,1,0:T(8,128)} all-to-all(f32[2,512,1664]{2,1,0:T(8,128)S(1)} %copy.140), channel_id=1, replica_groups=mesh['y'=4,'xl'=2,'z'=8,'xh'=2,'c'=2] {'c'}, dimensions={0} | all-to-all | bytes 13631488 | tf_op jit(solution)/shard_map/all_to_all | solution.py:16
  107.0 3.7 %reduce_sum.56 = f32[512,1664]{1,0:T(8,128)S(1)} reduce(f32[2,512,1664]{2,1,0:T(8,128)} %all_to_all.20, f32[]{:T(128)} %constant.1.clone.1), dimensions={0}, to_apply=%region_2.3 | reduce | flops 851968 | bytes 10223620 | tf_op jit(solution)/shard_map/reduce_sum | solution.py:16
  110.7 45.4 %all_to_all.21 = f32[4,128,1664]{2,1,0:T(8,128)} all-to-all(f32[4,128,1664]{2,1,0:T(8,128)S(1)} %bitcast.65), channel_id=1, replica_groups=mesh['y'=4,'xl'=2,'z'=8,'xh'=2,'c'=2] {'xh','xl'}, dimensions={0} | all-to-all | bytes 6815744 | tf_op jit(solution)/shard_map/all_to_all | solution.py:16
  156.1 3.3 %reduce_sum.57 = f32[128,1664]{1,0:T(8,128)} reduce(f32[4,128,1664]{2,1,0:T(8,128)} %all_to_all.21, f32[]{:T(128)} %constant.1.clone.1), dimensions={0}, to_apply=%region_3.4 | reduce | flops 638976 | bytes 4259844 | tf_op jit(solution)/shard_map/reduce_sum | solution.py:16
  159.4 5.0 %all-to-all-start.2 = ((f32[4,32,1664]{2,1,0:T(8,128)}), f32[4,32,1664]{2,1,0:T(8,128)}, u32[]{:S(2)}, u32[]{:S(2)}) async-start(f32[4,32,1664]{2,1,0:T(8,128)} %bitcast.23), calls=%async_computation.2 | async-start | bytes 1703936 | tf_op jit(solution)/shard_map/all_to_all | solution.py:16
  164.4 3.4 %fusion = f32[512,512]{0,1:T(8,128)S(1)} fusion(f32[2,512,1024]{2,1,0:T(8,128)} %param.9, f32[512,512]{0,1:T(8,128)S(1)} %copy-done.4, f32[512,512]{0,1:T(8,128)S(1)} %copy-done.2), kind=kOutput, calls=%fused_computation.5 | convolution fusion | flops 1611137024 | bytes 5242880 | tf_op jit(solution)/shard_map/dot_general | solution.py:42
  167.9 2.4 %collective-permute-start.3 = (f32[256,256]{0,1:T(8,128)S(1)}, f32[256,256]{0,1:T(8,128)S(1)}, u32[]{:S(2)}, u32[]{:S(2)}) collective-permute-start(f32[256,256]{0,1:T(8,128)S(1)} %get-tuple-element.39), channel_id=1, source_target_pairs={{4,0},{8,4},{12,8},{16,12},{20,16},{24,20},{28,24},{32,28},{36,32}... | collective-permute-start | bytes 786440 | tf_op jit(solution)/shard_map/ppermute | solution.py:34
  170.3 5.1 %all-to-all-done.2 = f32[4,32,1664]{2,1,0:T(8,128)} async-done(((f32[4,32,1664]{2,1,0:T(8,128)}), f32[4,32,1664]{2,1,0:T(8,128)}, u32[]{:S(2)}, u32[]{:S(2)}) %all-to-all-start.2) | async-done | bytes 852000 | tf_op jit(solution)/shard_map/all_to_all | solution.py:16
  175.4 1.2 reduce_sum.58
  176.6 0.7 reshape.50
  177.4 3.4 %all-to-all-start.3 = ((f32[8,4,1664]{2,1,0:T(4,128)}), f32[8,4,1664]{2,1,0:T(4,128)S(1)}, u32[]{:S(2)}, u32[]{:S(2)}) async-start(f32[8,4,1664]{2,1,0:T(4,128)} %reshape.50), calls=%async_computation.3 | async-start | bytes 425984 | tf_op jit(solution)/shard_map/all_to_all | solution.py:16
  180.8 0.1 fusion.41
  180.9 1.0 copy.142
  181.9 8.7 %all-to-all-done.3 = f32[8,4,1664]{2,1,0:T(4,128)S(1)} async-done(((f32[8,4,1664]{2,1,0:T(4,128)}), f32[8,4,1664]{2,1,0:T(4,128)S(1)}, u32[]{:S(2)}, u32[]{:S(2)}) %all-to-all-start.3) | async-done | bytes 213024 | tf_op jit(solution)/shard_map/all_to_all | solution.py:16
  190.7 0.6 slice.162
  191.3 0.6 slice.163
  191.9 0.6 reshape.51
  (70 shorter events, 0.3 us)
Async XLA Ops:
  0.6 5.3 %copy-start.15 = (f32[1,512,256]{2,1,0:T(8,128)S(1)}, f32[1,512,256]{2,1,0:T(8,128)}, u32[]{:S(2)}) copy-start(f32[1,512,256]{2,1,0:T(8,128)} %param.6) | copy-start | bytes 1572868
  2.0 6.3 %copy-start.16 = (f32[2,512,512]{2,1,0:T(8,128)S(1)}, f32[2,512,512]{2,1,0:T(8,128)}, u32[]{:S(2)}) copy-start(f32[2,512,512]{2,1,0:T(8,128)} %param.11) | copy-start | bytes 6291460
  2.0 14.2 %collective-permute-start = (f32[256,256]{0,1:T(8,128)S(1)}, f32[256,256]{0,1:T(8,128)S(1)}, u32[]{:S(2)}, u32[]{:S(2)}) collective-permute-start(f32[256,256]{0,1:T(8,128)S(1)} %get-tuple-element.40), channel_id=1, source_target_pairs={{0,4},{4,8},{8,12},{12,16},{16,20},{20,24},{24,28},{28,32},{32,36}... | collective-permute-start | bytes 786440 | tf_op jit(solution)/shard_map/ppermute | solution.py:34
  6.0 2.5 %copy-start.32 = (f32[2,1024]{1,0:T(2,128)S(1)}, f32[2,1024]{1,0:T(2,128)}, u32[]{:S(2)}) copy-start(f32[2,1024]{1,0:T(2,128)} %param.10) | copy-start | bytes 24580
  8.3 7.9 %copy-start = (f32[2,512,1024]{2,1,0:T(8,128)S(1)}, f32[2,512,1024]{2,1,0:T(8,128)}, u32[]{:S(2)}) copy-start(f32[2,512,1024]{2,1,0:T(8,128)} %param.9) | copy-start | bytes 12582916
  8.5 36.1 %copy-start.10 = (f32[512,512]{1,0:T(8,128)}, f32[512,512]{1,0:T(8,128)S(1)}, u32[]{:S(2)}) copy-start(f32[512,512]{1,0:T(8,128)S(1)} %get-tuple-element.36) | copy-start | bytes 3145732
  16.2 1.4 copy-start.24
  17.6 1.3 copy-start.17
  17.6 3.2 %copy-start.7 = (f32[1,512,256]{2,1,0:T(8,128)S(1)}, f32[1,512,256]{2,1,0:T(8,128)}, u32[]{:S(2)}) copy-start(f32[1,512,256]{2,1,0:T(8,128)} %param.8) | copy-start | bytes 1572868
  18.9 3.6 %copy-start.12 = (f32[512,256]{0,1:T(8,128)}, f32[512,256]{0,1:T(8,128)S(1)}, u32[]{:S(2)}) copy-start(f32[512,256]{0,1:T(8,128)S(1)} %convolution_add_fusion.2) | copy-start | bytes 1572868
  18.9 17.1 %collective-permute-start.1 = (f32[512,256]{0,1:T(8,128)S(1)}, f32[512,256]{0,1:T(8,128)S(1)}, u32[]{:S(2)}, u32[]{:S(2)}) collective-permute-start(f32[512,256]{0,1:T(8,128)S(1)} %convolution_add_fusion.2), channel_id=1, source_target_pairs={{0,4},{4,8},{8,12},{12,16},{16,20},{20,24},{24,28},{28,32},{32,36}... | collective-permute-start | bytes 1572872 | tf_op jit(solution)/shard_map/ppermute | solution.py:34
  36.0 1.4 copy-start.14
  36.0 1.4 copy-start.29
  37.4 1.4 copy-start.19
  40.6 1.1 copy-start.8
  42.5 16.8 %collective-permute-start.2 = (f32[512,256]{0,1:T(8,128)}, f32[512,256]{0,1:T(8,128)}, u32[]{:S(2)}, u32[]{:S(2)}) collective-permute-start(f32[512,256]{0,1:T(8,128)} %slice.157), channel_id=1, source_target_pairs={{4,0},{8,4},{12,8},{16,12},{20,16},{24,20},{28,24},{32,28},{36,32}... | collective-permute-start | bytes 1572872 | tf_op jit(solution)/shard_map/ppermute | solution.py:34
  49.4 3.3 %copy-start.13 = (f32[512,256]{0,1:T(8,128)S(1)}, f32[512,256]{0,1:T(8,128)}, u32[]{:S(2)}) copy-start(f32[512,256]{0,1:T(8,128)} %copy-done.12) | copy-start | bytes 1572868
  52.6 4.4 %copy-start.20 = (f32[512,1024]{0,1:T(8,128)S(1)}, f32[512,1024]{0,1:T(8,128)}, u32[]{:S(2)}) copy-start(f32[512,1024]{0,1:T(8,128)} %copy-done.19) | copy-start | bytes 6291460
  52.6 4.4 %copy-start.21 = (f32[1,512,256]{1,2,0:T(8,128)S(1)}, f32[1,512,256]{1,2,0:T(8,128)}, u32[]{:S(2)}) copy-start(f32[1,512,256]{1,2,0:T(8,128)} %copy.121) | copy-start | bytes 1572868
  52.6 4.4 %copy-start.30 = (f32[1,512,256]{1,2,0:T(8,128)S(1)}, f32[1,512,256]{1,2,0:T(8,128)}, u32[]{:S(2)}) copy-start(f32[1,512,256]{1,2,0:T(8,128)} %copy.122) | copy-start | bytes 1572868
  57.0 2.3 %copy-start.9 = (f32[512,512]{0,1:T(8,128)S(1)}, f32[512,512]{0,1:T(8,128)}, u32[]{:S(2)}) copy-start(f32[512,512]{0,1:T(8,128)} %copy-done.8) | copy-start | bytes 3145732
  59.3 1.7 copy-start.18
  61.0 2.3 %copy-start.22 = (f32[512,256]{0,1:T(8,128)}, f32[512,256]{0,1:T(8,128)S(1)}, u32[]{:S(2)}) copy-start(f32[512,256]{0,1:T(8,128)S(1)} %fusion.44) | copy-start | bytes 1572868
  61.0 2.3 %copy-start.11 = (f32[512,512]{1,0:T(8,128)S(1)}, f32[512,512]{1,0:T(8,128)}, u32[]{:S(2)}) copy-start(f32[512,512]{1,0:T(8,128)} %copy-done.10) | copy-start | bytes 3145732
  61.0 2.3 %copy-start.26 = (f32[512,512]{0,1:T(8,128)S(1)}, f32[512,512]{0,1:T(8,128)}, u32[]{:S(2)}) copy-start(f32[512,512]{0,1:T(8,128)} %fusion.42) | copy-start | bytes 3145732
  64.4 12.0 %copy-start.1 = (f32[512,512]{0,1:T(8,128)}, f32[512,512]{0,1:T(8,128)S(1)}, u32[]{:S(2)}) copy-start(f32[512,512]{0,1:T(8,128)S(1)} %get-tuple-element.32) | copy-start | bytes 3145732
  64.4 11.9 %copy-start.3 = (f32[512,512]{0,1:T(8,128)}, f32[512,512]{0,1:T(8,128)S(1)}, u32[]{:S(2)}) copy-start(f32[512,512]{0,1:T(8,128)S(1)} %get-tuple-element.33) | copy-start | bytes 3145732
  64.4 1.0 copy-start.31
  66.3 1.2 copy-start.27
  66.3 1.5 copy-start.28
  72.2 4.1 %copy-start.25 = (f32[256,256]{0,1:T(8,128)S(1)}, f32[256,256]{0,1:T(8,128)}, u32[]{:S(2)}) copy-start(f32[256,256]{0,1:T(8,128)} %copy-done.24) | copy-start | bytes 786436
  76.4 1.9 copy-start.5
  86.0 6.4 %copy-start.6 = (f32[4,2,8,2,2,4,512]{6,4,5,2,0,1,3:T(2,128)S(1)}, f32[4,2,8,2,2,4,512]{6,4,5,2,0,1,3:T(2,128)}, u32[]{:S(2)}) copy-start(f32[4,2,8,2,2,4,512]{6,4,5,2,0,1,3:T(2,128)} %copy.134) | copy-start | bytes 6291460
  156.1 8.3 %copy-start.2 = (f32[512,512]{0,1:T(8,128)S(1)}, f32[512,512]{0,1:T(8,128)}, u32[]{:S(2)}) copy-start(f32[512,512]{0,1:T(8,128)} %copy-done.1) | copy-start | bytes 3145732
  156.1 8.3 %copy-start.4 = (f32[512,512]{0,1:T(8,128)S(1)}, f32[512,512]{0,1:T(8,128)}, u32[]{:S(2)}) copy-start(f32[512,512]{0,1:T(8,128)} %copy-done.3) | copy-start | bytes 3145732
  159.4 16.0 %all-to-all-start.2 = ((f32[4,32,1664]{2,1,0:T(8,128)}), f32[4,32,1664]{2,1,0:T(8,128)}, u32[]{:S(2)}, u32[]{:S(2)}) async-start(f32[4,32,1664]{2,1,0:T(8,128)} %bitcast.23), calls=%async_computation.2 | async-start | bytes 1703936 | tf_op jit(solution)/shard_map/all_to_all | solution.py:16
  167.8 12.9 %copy-start.23 = (f32[512,256]{0,1:T(8,128)S(1)}, f32[512,256]{0,1:T(8,128)}, u32[]{:S(2)}) copy-start(f32[512,256]{0,1:T(8,128)} %copy-done.22) | copy-start | bytes 1572868
  167.9 12.9 %collective-permute-start.3 = (f32[256,256]{0,1:T(8,128)S(1)}, f32[256,256]{0,1:T(8,128)S(1)}, u32[]{:S(2)}, u32[]{:S(2)}) collective-permute-start(f32[256,256]{0,1:T(8,128)S(1)} %get-tuple-element.39), channel_id=1, source_target_pairs={{4,0},{8,4},{12,8},{16,12},{20,16},{24,20},{28,24},{32,28},{36,32}... | collective-permute-start | bytes 786440 | tf_op jit(solution)/shard_map/ppermute | solution.py:34
  177.4 13.3 %all-to-all-start.3 = ((f32[8,4,1664]{2,1,0:T(4,128)}), f32[8,4,1664]{2,1,0:T(4,128)S(1)}, u32[]{:S(2)}, u32[]{:S(2)}) async-start(f32[8,4,1664]{2,1,0:T(4,128)} %reshape.50), calls=%async_computation.3 | async-start | bytes 425984 | tf_op jit(solution)/shard_map/all_to_all | solution.py:16

commit v8 on v6

--- a/solution.py
+++ b/solution.py
@@ -19,11 +19,11 @@
 def owner_rows(terms):
     rows, width = terms.shape
     sizes = [lax.axis_size(a) for a in ("y", "xl", "z", "xh", "c")]
-    return terms.reshape(*sizes, -1, width).transpose(4, 3, 1, 0, 2, 5, 6).reshape(rows, width)
+    return terms.reshape(*sizes, -1, width).transpose(4, 0, 3, 1, 2, 5, 6).reshape(rows, width)
 
 
 def reduce_to_owner(block):
-    for axis in ("c", ("xh", "xl"), "y", "z"):
+    for axis in ("c", "y", ("xh", "xl"), "z"):
         block = reduce_rows(block, axis)
     return block
 

time: 196 us -> 198 us (1.010)
  starting transfers between devices: 23.1 us -> 26 us
    all_to_all x2, starting transfers between devices: 10.6 us -> 15.1 us  [reduce_rows(): return lax.all_to_all(block, axis, 0, 0, tiled=True).sum(axis=0)]
where the time goes in v8:
time: 198 us; the launch traced here: 196 us
  blocking collectives  54.5 us (28%)
  waiting for transfers between devices  34.3 us (17%)
  local copies, waits for them, and re-layouts  33.5 us (17%)
  matrix products  27.6 us (14%)
  starting transfers between devices  26 us (13%)
  other arithmetic  19.1 us (10%)
    all_to_all x2, blocking collectives, reduce_rows(): return lax.all_to_all(block, axis, 0, 0, tiled=True).sum(axis=0)  54.5 us
    ppermute x4, waiting for transfers between devices, from_behind(): return lax.ppermute(block, axis, route)  21.2 us
    dot_general x10, matrix products, contract(): lax.dot_general(left, right, (((left_dim,), (right_dim,)), ((), ())), pre...  20.6 us
    reshape x4, local copies, waits for them, and re-layouts, owner_rows(): terms.reshape(*sizes, -1, width).transpose(4, 0, 3, 1, 2, 5, 6)  18.7 us
    all_to_all x2, starting transfers between devices, reduce_rows(): return lax.all_to_all(block, axis, 0, 0, tiled=True).sum(axis=0)  15.1 us
    all_to_all x2, waiting for transfers between devices, reduce_rows(): return lax.all_to_all(block, axis, 0, 0, tiled=True).sum(axis=0)  13.2 us
    ppermute x4, starting transfers between devices, from_behind(): return lax.ppermute(block, axis, route)  10.9 us
    reduce_sum x4, other arithmetic, reduce_rows(): return lax.all_to_all(block, axis, 0, 0, tiled=True).sum(axis=0)  8.27 us
  transfers between devices with their start and end apart: 6, of which 4 were waited for; matrix products, arithmetic and copies ran while one was open for 12% of the time, Pallas kernels for 0%

profile of v8, /device:TPU:10, one launch (start us, length us, event | category | flops | bytes accessed | tf_op | source)
XLA Modules:
  0.0 196.0 jit_solution(14979093411891284463)
XLA Ops:
  0.6 1.3 copy.97
  2.0 0.0 copy-start.16
  2.0 4.0 %collective-permute-start = (f32[256,256]{0,1:T(8,128)S(1)}, f32[256,256]{0,1:T(8,128)S(1)}, u32[]{:S(2)}, u32[]{:S(2)}) collective-permute-start(f32[256,256]{0,1:T(8,128)S(1)} %get-tuple-element.36), channel_id=1, source_target_pairs={{0,4},{4,8},{8,12},{12,16},{16,20},{20,24},{24,28},{28,32},{32,36}... | collective-permute-start | bytes 786440 | tf_op jit(solution)/shard_map/ppermute | solution.py:34
  6.0 0.0 copy-start.32
  6.0 2.3 %fusion.32 = f32[512,1024]{0,1:T(8,128)S(1)} fusion(f32[2,512,1024]{2,1,0:T(8,128)} %param.9, f32[1,512,256]{2,1,0:T(8,128)S(1)} %copy-done.15), kind=kOutput, calls=%fused_computation.48 | convolution fusion | flops 805306368 | bytes 3670016 | tf_op jit(solution)/shard_map/dot_general | solution.py:38
  8.3 0.0 copy-start
  8.3 0.2 slice_bitcast_fusion
  8.5 7.7 %collective-permute-done = f32[256,256]{0,1:T(8,128)S(1)} collective-permute-done((f32[256,256]{0,1:T(8,128)S(1)}, f32[256,256]{0,1:T(8,128)S(1)}, u32[]{:S(2)}, u32[]{:S(2)}) %collective-permute-start) | collective-permute-done | bytes 262176 | tf_op jit(solution)/shard_map/ppermute | solution.py:34
  16.2 1.4 add_add_fusion.1
  17.6 0.0 copy-start.7
  17.6 0.9 convolution_add_fusion.2
  18.5 0.3 copy-done.17
  18.9 1.9 collective-permute-start.1
  20.8 0.6 fusion.46
  21.4 1.0 fusion.29
  22.5 13.5 %collective-permute-done.1 = f32[512,256]{0,1:T(8,128)S(1)} collective-permute-done((f32[512,256]{0,1:T(8,128)S(1)}, f32[512,256]{0,1:T(8,128)S(1)}, u32[]{:S(2)}, u32[]{:S(2)}) %collective-permute-start.1) | collective-permute-done | bytes 524320 | tf_op jit(solution)/shard_map/ppermute | solution.py:34
  36.0 1.4 add_add_fusion
  37.4 1.1 subtract_multiply_fusion.3
  38.5 0.3 copy-done.19
  38.7 1.9 fusion.2
  40.6 1.0 copy-done.8
  41.7 0.8 slice.157
  42.5 2.1 %collective-permute-start.2 = (f32[512,256]{0,1:T(8,128)}, f32[512,256]{0,1:T(8,128)}, u32[]{:S(2)}, u32[]{:S(2)}) collective-permute-start(f32[512,256]{0,1:T(8,128)} %slice.157), channel_id=1, source_target_pairs={{4,0},{8,4},{12,8},{16,12},{20,16},{24,20},{28,24},{32,28},{36,32}... | collective-permute-start | bytes 1572872 | tf_op jit(solution)/shard_map/ppermute | solution.py:34
  44.6 1.7 fusion.42
  46.3 2.0 %copy.95 = f32[1,512,256]{1,2,0:T(8,128)} copy(f32[1,512,256]{2,1,0:T(8,128)} %param.7) | data formatting | bytes 1048576 | tf_op args[1]
  48.3 1.0 copy.96
  49.4 0.2 fusion.8
  49.6 0.9 concatenate.61
  50.5 4.4 %fusion.9 = f32[512,1024]{1,0:T(8,128)} fusion(f32[512,512]{0,1:T(8,128)S(1)} %get-tuple-element.31, f32[512,512]{0,1:T(8,128)S(1)} %get-tuple-element.30, f32[512,256]{0,1:T(8,128)S(1)} %copy-done.13, f32[512,256]{0,1:T(8,128)} %copy-done.14), kind=kOutput, calls=%fused_computation.18 | convolution fusion | flops 1611399168 | bytes 5242880 | tf_op jit(solution)/shard_map/dot_general | solution.py:42
  54.9 2.3 %fusion.11 = f32[512,512]{1,0:T(8,128)} fusion(f32[512,256]{0,1:T(8,128)S(1)} %bitcast.71, f32[512,256]{0,1:T(8,128)S(1)} %bitcast.69, f32[512,1024]{0,1:T(8,128)S(1)} %copy-done.20), kind=kOutput, calls=%fused_computation.23 | convolution fusion | flops 806617088 | bytes 4194304 | tf_op jit(solution)/shard_map/dot_general | solution.py:42
  57.2 1.3 fusion.44
  58.5 0.4 copy-done.18
  58.9 2.3 %fusion.10 = f32[512,512]{1,0:T(8,128)} fusion(f32[512,256]{0,1:T(8,128)S(1)} %bitcast.72, f32[512,256]{0,1:T(8,128)S(1)} %fusion.44, f32[512,1024]{0,1:T(8,128)S(1)} %copy-done.18), kind=kOutput, calls=%fused_computation.22 | convolution fusion | flops 806617088 | bytes 4194304 | tf_op jit(solution)/shard_map/dot_general | solution.py:42
  61.2 1.0 subtract_multiply_fusion.1
  62.3 0.2 fusion.6
  62.5 1.2 concatenate.60
  63.7 1.2 select_maximum_fusion
  65.0 1.1 copy.109
  66.1 1.5 pad_maximum_fusion.4
  67.7 2.8 %reshape.49 = f32[4,2,8,2,2,4,512]{6,5,4,3,2,1,0:T(4,128)} reshape(f32[1024,512]{1,0:T(8,128)} %pad_maximum_fusion.4) | data formatting | bytes 4194304 | tf_op jit(solution)/shard_map/reshape | solution.py:22
  70.5 4.2 %copy.108 = f32[4,2,8,2,2,4,512]{6,4,5,2,1,3,0:T(2,128)} copy(f32[4,2,8,2,2,4,512]{6,5,4,3,2,1,0:T(4,128)} %reshape.49) | data formatting | bytes 4194304 | tf_op jit(solution)/shard_map/reshape | solution.py:22
  74.7 1.9 fusion.7
  76.6 2.5 %pad_maximum_fusion.1 = f32[1024,1024]{1,0:T(8,128)} fusion(f32[512,1024]{1,0:T(8,128)S(1)} %copy-done.5, f32[512,1024]{1,0:T(8,128)S(1)} %fusion.7), kind=kLoop, calls=%fused_computation.1 | loop fusion | flops 1048576 | bytes 8388608 | tf_op jit(solution)/shard_map/concatenate | solution.py:121
  79.0 5.3 %reshape.48 = f32[4,2,8,2,2,4,1024]{6,5,4,3,2,1,0:T(4,128)} reshape(f32[1024,1024]{1,0:T(8,128)} %pad_maximum_fusion.1) | data formatting | bytes 8388608 | tf_op jit(solution)/shard_map/reshape | solution.py:22
  84.3 6.4 %copy.107 = f32[4,2,8,2,2,4,1024]{6,4,5,2,1,3,0:T(2,128)S(1)} copy(f32[4,2,8,2,2,4,1024]{6,5,4,3,2,1,0:T(4,128)} %reshape.48) | data formatting | bytes 8388608 | tf_op jit(solution)/shard_map/reshape | solution.py:22
  90.8 3.6 %pad_maximum_fusion = f32[2,512,1664]{2,0,1:T(2,128)S(1)} fusion(f32[2,512,128]{2,0,1:T(2,128)S(1)} %bitcast.70, f32[2,512,512]{2,0,1:T(2,128)S(1)} %bitcast.66, f32[2,512,1024]{2,0,1:T(2,128)S(1)} %bitcast.64), kind=kLoop, calls=%fused_computation | loop fusion | flops 3407872 | bytes 13631488 | tf_op jit(solution)/shard_map/concatenate | solution.py:126
  94.4 0.4 copy.110
  94.8 10.4 %all_to_all.20 = f32[2,512,1664]{2,1,0:T(8,128)} all-to-all(f32[2,512,1664]{2,1,0:T(8,128)S(1)} %copy.110), channel_id=1, replica_groups=mesh['y'=4,'xl'=2,'z'=8,'xh'=2,'c'=2] {'c'}, dimensions={0} | all-to-all | bytes 13631488 | tf_op jit(solution)/shard_map/all_to_all | solution.py:16
  105.3 3.7 %reduce_sum.56 = f32[512,1664]{1,0:T(8,128)S(1)} reduce(f32[2,512,1664]{2,1,0:T(8,128)} %all_to_all.20, f32[]{:T(128)} %constant.1.clone.1), dimensions={0}, to_apply=%region_2.3 | reduce | flops 851968 | bytes 10223620 | tf_op jit(solution)/shard_map/reduce_sum | solution.py:16
  109.0 44.0 %all_to_all.21 = f32[4,128,1664]{2,1,0:T(8,128)} all-to-all(f32[4,128,1664]{2,1,0:T(8,128)S(1)} %bitcast.65), channel_id=1, replica_groups=mesh['y'=4,'xl'=2,'z'=8,'xh'=2,'c'=2] {'y'}, dimensions={0} | all-to-all | bytes 6815744 | tf_op jit(solution)/shard_map/all_to_all | solution.py:16
  153.1 3.3 %reduce_sum.57 = f32[128,1664]{1,0:T(8,128)} reduce(f32[4,128,1664]{2,1,0:T(8,128)} %all_to_all.21, f32[]{:T(128)} %constant.1.clone.1), dimensions={0}, to_apply=%region_3.4 | reduce | flops 638976 | bytes 4259844 | tf_op jit(solution)/shard_map/reduce_sum | solution.py:16
  156.3 6.6 %all-to-all-start.2 = ((f32[4,32,1664]{2,1,0:T(8,128)}), f32[4,32,1664]{2,1,0:T(8,128)}, u32[]{:S(2)}, u32[]{:S(2)}) async-start(f32[4,32,1664]{2,1,0:T(8,128)} %bitcast.24), calls=%async_computation.2 | async-start | bytes 1703936 | tf_op jit(solution)/shard_map/all_to_all | solution.py:16
  162.9 3.4 %fusion = f32[512,512]{0,1:T(8,128)S(1)} fusion(f32[2,512,1024]{2,1,0:T(8,128)} %param.9, f32[512,512]{0,1:T(8,128)S(1)} %copy-done.4, f32[512,512]{0,1:T(8,128)S(1)} %copy-done.2), kind=kOutput, calls=%fused_computation.5 | convolution fusion | flops 1611137024 | bytes 5242880 | tf_op jit(solution)/shard_map/dot_general | solution.py:42
  166.4 2.9 %collective-permute-start.3 = (f32[256,256]{0,1:T(8,128)S(1)}, f32[256,256]{0,1:T(8,128)S(1)}, u32[]{:S(2)}, u32[]{:S(2)}) collective-permute-start(f32[256,256]{0,1:T(8,128)S(1)} %get-tuple-element.35), channel_id=1, source_target_pairs={{4,0},{8,4},{12,8},{16,12},{20,16},{24,20},{28,24},{32,28},{36,32}... | collective-permute-start | bytes 786440 | tf_op jit(solution)/shard_map/ppermute | solution.py:34
  169.3 4.3 %all-to-all-done.2 = f32[4,32,1664]{2,1,0:T(8,128)} async-done(((f32[4,32,1664]{2,1,0:T(8,128)}), f32[4,32,1664]{2,1,0:T(8,128)}, u32[]{:S(2)}, u32[]{:S(2)}) %all-to-all-start.2) | async-done | bytes 852000 | tf_op jit(solution)/shard_map/all_to_all | solution.py:16
  173.7 1.2 reduce_sum.58
  174.9 0.7 reshape.53
  175.6 8.6 %all-to-all-start.3 = ((f32[8,4,1664]{2,1,0:T(4,128)}), f32[8,4,1664]{2,1,0:T(4,128)S(1)}, u32[]{:S(2)}, u32[]{:S(2)}) async-start(f32[8,4,1664]{2,1,0:T(4,128)} %reshape.53), calls=%async_computation.3 | async-start | bytes 425984 | tf_op jit(solution)/shard_map/all_to_all | solution.py:16
  184.2 0.1 fusion.41
  184.3 1.0 copy.112
  185.3 8.8 %all-to-all-done.3 = f32[8,4,1664]{2,1,0:T(4,128)S(1)} async-done(((f32[8,4,1664]{2,1,0:T(4,128)}), f32[8,4,1664]{2,1,0:T(4,128)S(1)}, u32[]{:S(2)}, u32[]{:S(2)}) %all-to-all-start.3) | async-done | bytes 213024 | tf_op jit(solution)/shard_map/all_to_all | solution.py:16
  194.2 0.6 slice.162
  194.8 0.6 slice.163
  195.4 0.6 reshape.54
  (66 shorter events, 0.3 us)
Async XLA Ops:
  0.6 5.3 %copy-start.15 = (f32[1,512,256]{2,1,0:T(8,128)S(1)}, f32[1,512,256]{2,1,0:T(8,128)}, u32[]{:S(2)}) copy-start(f32[1,512,256]{2,1,0:T(8,128)} %param.6) | copy-start | bytes 1572868
  2.0 6.3 %copy-start.16 = (f32[2,512,512]{2,1,0:T(8,128)S(1)}, f32[2,512,512]{2,1,0:T(8,128)}, u32[]{:S(2)}) copy-start(f32[2,512,512]{2,1,0:T(8,128)} %param.11) | copy-start | bytes 6291460
  2.0 14.2 %collective-permute-start = (f32[256,256]{0,1:T(8,128)S(1)}, f32[256,256]{0,1:T(8,128)S(1)}, u32[]{:S(2)}, u32[]{:S(2)}) collective-permute-start(f32[256,256]{0,1:T(8,128)S(1)} %get-tuple-element.36), channel_id=1, source_target_pairs={{0,4},{4,8},{8,12},{12,16},{16,20},{20,24},{24,28},{28,32},{32,36}... | collective-permute-start | bytes 786440 | tf_op jit(solution)/shard_map/ppermute | solution.py:34
  6.0 2.5 %copy-start.32 = (f32[2,1024]{1,0:T(2,128)S(1)}, f32[2,1024]{1,0:T(2,128)}, u32[]{:S(2)}) copy-start(f32[2,1024]{1,0:T(2,128)} %param.10) | copy-start | bytes 24580
  8.3 7.9 %copy-start = (f32[2,512,1024]{2,1,0:T(8,128)S(1)}, f32[2,512,1024]{2,1,0:T(8,128)}, u32[]{:S(2)}) copy-start(f32[2,512,1024]{2,1,0:T(8,128)} %param.9) | copy-start | bytes 12582916
  8.5 36.1 %copy-start.10 = (f32[512,512]{1,0:T(8,128)}, f32[512,512]{1,0:T(8,128)S(1)}, u32[]{:S(2)}) copy-start(f32[512,512]{1,0:T(8,128)S(1)} %get-tuple-element.32) | copy-start | bytes 3145732
  16.2 1.4 copy-start.25
  17.6 1.3 copy-start.17
  17.6 3.2 %copy-start.7 = (f32[1,512,256]{2,1,0:T(8,128)S(1)}, f32[1,512,256]{2,1,0:T(8,128)}, u32[]{:S(2)}) copy-start(f32[1,512,256]{2,1,0:T(8,128)} %param.8) | copy-start | bytes 1572868
  18.9 3.6 %copy-start.12 = (f32[512,256]{0,1:T(8,128)}, f32[512,256]{0,1:T(8,128)S(1)}, u32[]{:S(2)}) copy-start(f32[512,256]{0,1:T(8,128)S(1)} %convolution_add_fusion.2) | copy-start | bytes 1572868
  18.9 17.1 %collective-permute-start.1 = (f32[512,256]{0,1:T(8,128)S(1)}, f32[512,256]{0,1:T(8,128)S(1)}, u32[]{:S(2)}, u32[]{:S(2)}) collective-permute-start(f32[512,256]{0,1:T(8,128)S(1)} %convolution_add_fusion.2), channel_id=1, source_target_pairs={{0,4},{4,8},{8,12},{12,16},{16,20},{20,24},{24,28},{28,32},{32,36}... | collective-permute-start | bytes 1572872 | tf_op jit(solution)/shard_map/ppermute | solution.py:34
  36.0 1.4 copy-start.14
  36.0 1.4 copy-start.30
  37.4 1.4 copy-start.19
  40.6 1.1 copy-start.8
  42.5 14.7 %collective-permute-start.2 = (f32[512,256]{0,1:T(8,128)}, f32[512,256]{0,1:T(8,128)}, u32[]{:S(2)}, u32[]{:S(2)}) collective-permute-start(f32[512,256]{0,1:T(8,128)} %slice.157), channel_id=1, source_target_pairs={{4,0},{8,4},{12,8},{16,12},{20,16},{24,20},{28,24},{32,28},{36,32}... | collective-permute-start | bytes 1572872 | tf_op jit(solution)/shard_map/ppermute | solution.py:34
  49.4 1.1 copy-start.13
  50.5 4.4 %copy-start.20 = (f32[512,1024]{0,1:T(8,128)S(1)}, f32[512,1024]{0,1:T(8,128)}, u32[]{:S(2)}) copy-start(f32[512,1024]{0,1:T(8,128)} %copy-done.19) | copy-start | bytes 6291460
  50.5 4.4 %copy-start.21 = (f32[1,512,256]{1,2,0:T(8,128)S(1)}, f32[1,512,256]{1,2,0:T(8,128)}, u32[]{:S(2)}) copy-start(f32[1,512,256]{1,2,0:T(8,128)} %copy.95) | copy-start | bytes 1572868
  50.5 4.4 %copy-start.31 = (f32[1,512,256]{1,2,0:T(8,128)S(1)}, f32[1,512,256]{1,2,0:T(8,128)}, u32[]{:S(2)}) copy-start(f32[1,512,256]{1,2,0:T(8,128)} %copy.96) | copy-start | bytes 1572868
  54.9 2.3 %copy-start.9 = (f32[512,512]{0,1:T(8,128)S(1)}, f32[512,512]{0,1:T(8,128)}, u32[]{:S(2)}) copy-start(f32[512,512]{0,1:T(8,128)} %copy-done.8) | copy-start | bytes 3145732
  57.2 1.7 copy-start.18
  58.9 2.3 %copy-start.22 = (f32[512,256]{0,1:T(8,128)}, f32[512,256]{0,1:T(8,128)S(1)}, u32[]{:S(2)}) copy-start(f32[512,256]{0,1:T(8,128)S(1)} %fusion.44) | copy-start | bytes 1572868
  58.9 2.3 %copy-start.11 = (f32[512,512]{1,0:T(8,128)S(1)}, f32[512,512]{1,0:T(8,128)}, u32[]{:S(2)}) copy-start(f32[512,512]{1,0:T(8,128)} %copy-done.10) | copy-start | bytes 3145732
  58.9 2.3 %copy-start.27 = (f32[512,512]{0,1:T(8,128)S(1)}, f32[512,512]{0,1:T(8,128)}, u32[]{:S(2)}) copy-start(f32[512,512]{0,1:T(8,128)} %fusion.42) | copy-start | bytes 3145732
  62.3 12.3 %copy-start.1 = (f32[512,512]{0,1:T(8,128)}, f32[512,512]{0,1:T(8,128)S(1)}, u32[]{:S(2)}) copy-start(f32[512,512]{0,1:T(8,128)S(1)} %get-tuple-element.28) | copy-start | bytes 3145732
  62.3 12.3 %copy-start.3 = (f32[512,512]{0,1:T(8,128)}, f32[512,512]{0,1:T(8,128)S(1)}, u32[]{:S(2)}) copy-start(f32[512,512]{0,1:T(8,128)S(1)} %get-tuple-element.29) | copy-start | bytes 3145732
  63.7 2.4 %copy-start.28 = (f32[512,512]{1,0:T(8,128)S(1)}, f32[512,512]{1,0:T(8,128)}, u32[]{:S(2)}) copy-start(f32[512,512]{1,0:T(8,128)} %fusion.11) | copy-start | bytes 3145732
  63.7 2.4 %copy-start.29 = (f32[512,512]{1,0:T(8,128)S(1)}, f32[512,512]{1,0:T(8,128)}, u32[]{:S(2)}) copy-start(f32[512,512]{1,0:T(8,128)} %fusion.10) | copy-start | bytes 3145732
  70.5 4.2 %copy-start.26 = (f32[256,256]{0,1:T(8,128)S(1)}, f32[256,256]{0,1:T(8,128)}, u32[]{:S(2)}) copy-start(f32[256,256]{0,1:T(8,128)} %copy-done.25) | copy-start | bytes 786436
  74.7 1.9 copy-start.5
  84.3 6.4 %copy-start.6 = (f32[4,2,8,2,2,4,512]{6,4,5,2,1,3,0:T(2,128)S(1)}, f32[4,2,8,2,2,4,512]{6,4,5,2,1,3,0:T(2,128)}, u32[]{:S(2)}) copy-start(f32[4,2,8,2,2,4,512]{6,4,5,2,1,3,0:T(2,128)} %copy.108) | copy-start | bytes 6291460
  84.3 6.4 %copy-start.24 = (f32[2,4,2,2,8,4,128]{6,0,5,4,3,2,1:T(2,128)S(1)}, f32[2,4,2,2,8,4,128]{6,0,5,4,3,2,1:T(2,128)}, u32[]{:S(2)}) copy-start(f32[2,4,2,2,8,4,128]{6,0,5,4,3,2,1:T(2,128)} %copy.109) | copy-start | bytes 1572868
  153.0 9.8 %copy-start.2 = (f32[512,512]{0,1:T(8,128)S(1)}, f32[512,512]{0,1:T(8,128)}, u32[]{:S(2)}) copy-start(f32[512,512]{0,1:T(8,128)} %copy-done.1) | copy-start | bytes 3145732
  153.0 9.8 %copy-start.4 = (f32[512,512]{0,1:T(8,128)S(1)}, f32[512,512]{0,1:T(8,128)}, u32[]{:S(2)}) copy-start(f32[512,512]{0,1:T(8,128)} %copy-done.3) | copy-start | bytes 3145732
  156.3 17.3 %all-to-all-start.2 = ((f32[4,32,1664]{2,1,0:T(8,128)}), f32[4,32,1664]{2,1,0:T(8,128)}, u32[]{:S(2)}, u32[]{:S(2)}) async-start(f32[4,32,1664]{2,1,0:T(8,128)} %bitcast.24), calls=%async_computation.2 | async-start | bytes 1703936 | tf_op jit(solution)/shard_map/all_to_all | solution.py:16
  166.3 17.9 %copy-start.23 = (f32[512,256]{0,1:T(8,128)S(1)}, f32[512,256]{0,1:T(8,128)}, u32[]{:S(2)}) copy-start(f32[512,256]{0,1:T(8,128)} %copy-done.22) | copy-start | bytes 1572868
  166.4 17.8 %collective-permute-start.3 = (f32[256,256]{0,1:T(8,128)S(1)}, f32[256,256]{0,1:T(8,128)S(1)}, u32[]{:S(2)}, u32[]{:S(2)}) collective-permute-start(f32[256,256]{0,1:T(8,128)S(1)} %get-tuple-element.35), channel_id=1, source_target_pairs={{4,0},{8,4},{12,8},{16,12},{20,16},{24,20},{28,24},{32,28},{36,32}... | collective-permute-start | bytes 786440 | tf_op jit(solution)/shard_map/ppermute | solution.py:34
  175.6 18.5 %all-to-all-start.3 = ((f32[8,4,1664]{2,1,0:T(4,128)}), f32[8,4,1664]{2,1,0:T(4,128)S(1)}, u32[]{:S(2)}, u32[]{:S(2)}) async-start(f32[8,4,1664]{2,1,0:T(4,128)} %reshape.53), calls=%async_computation.3 | async-start | bytes 425984 | tf_op jit(solution)/shard_map/all_to_all | solution.py:16
